TPU v7x, 768 devices: a whole 4x8x12 slice. The times are simulated.
768 devices in a mesh: dp: 128 (over y, x, z_lo), pipe: 6 (over z_hi, core).
Axes of the slice: x: 4, y: 8, z: 12 (z_hi: 3, z_lo: 4; z = z_hi * 4 + z_lo), core: 2. Of those that a mesh axis runs over, the one named last changes fastest.
Arguments:
- latents: bfloat16 [49152, 320], P('dp'), may hold values from -6 to 6
- clip_of_row: int32 [128, 384], P('dp'), may hold values from 0 to 3, never falling along the last dimension, each value on 1 to 192 neighbouring positions
- timestep: int32 [128, 4], P('dp'), may hold values from 0 to 999
- w_in: bfloat16 [6, 320, 640], P('pipe'), may hold values from -0.3125 to 0.3125
- w_out: bfloat16 [6, 640, 320], P('pipe'), may hold values from -0.25 to 0.25
- w_mix: bfloat16 [6, 640, 320], P('pipe'), may hold values from -0.25 to 0.25
- w_up: bfloat16 [6, 320, 320], P('pipe'), may hold values from -0.3125 to 0.3125
- out_grad: bfloat16 [49152, 320], P('dp'), may hold values from -6 to 6
Outputs:
- w_in_grad: float32 [6, 320, 640], P('pipe')
- w_out_grad: float32 [6, 640, 320], P('pipe')
- w_mix_grad: float32 [6, 640, 320], P('pipe')
- w_up_grad: float32 [6, 320, 320], P('pipe')
Inputs may be any that keep to these rules, and one draw needn't show every extreme that they name: `clip_of_row`: along each replica's rows the clip numbers never fall; every clip has 1 to 192 rows, and one has exactly 192.
All inputs are finite; a program needn't handle non-finite values.
Results may differ from a plain program's by a relative error of at most 0.019.
Values may be sent and summed in bfloat16 or wider, within the bound.
No kernel may reach another device: no remote copies, remote signals or barrier semaphores. Data moves between devices by JAX's collectives and lax.ppermute only.
A program may use at most 32 MiB of HBM per device.

v0:
```python
import math

import jax
import jax.numpy as jnp
from jax import lax
from jax.sharding import PartitionSpec as P

MICRO = 4


def shifted(value, axis, steps):
    count = lax.axis_size(axis)
    leading, last = (max(0, -steps), min(count, count - steps))
    return lax.ppermute(value, axis, [(source, source + steps) for source in range(leading, last)])


def rows_product(left, right):
    return lax.dot_general(
        left, right, (((0,), (0,)), ((), ())), preferred_element_type=jnp.float32
    )


def times_transposed(left, right):
    return lax.dot_general(
        left, right, (((1,), (1,)), ((), ())), preferred_element_type=jnp.float32
    )


def rms_scale(values):
    return lax.rsqrt(jnp.mean(values * values, axis=-1, keepdims=True) + 1e-05)


def silu_slope(values):
    sigma = jax.nn.sigmoid(values)
    return sigma * (1.0 + values * (1.0 - sigma))


def embed(moment, width):
    half = width // 2
    freq = jnp.exp(-math.log(10000.0) * jnp.arange(half, dtype=jnp.float32) / half)
    angle = moment[:, None] * freq[None, :]
    return jnp.concatenate([jnp.sin(angle), jnp.cos(angle)], axis=-1)


def down_forward(hidden, embedding, in_matrix, out_matrix):
    lifted = hidden.astype(jnp.float32) + embedding
    normed = lifted * rms_scale(lifted)
    inner = jnp.dot(normed.astype(jnp.bfloat16), in_matrix, preferred_element_type=jnp.float32)
    gated = jax.nn.silu(inner).astype(jnp.bfloat16)
    return (lifted + jnp.dot(gated, out_matrix, preferred_element_type=jnp.float32)).astype(
        jnp.bfloat16
    )


def down_backward(hidden, embedding, in_matrix, out_matrix, cotan):
    lifted = hidden.astype(jnp.float32) + embedding
    scale = rms_scale(lifted)
    normed = lifted * scale
    normed_b = normed.astype(jnp.bfloat16)
    inner = jnp.dot(normed_b, in_matrix, preferred_element_type=jnp.float32)
    gated = jax.nn.silu(inner).astype(jnp.bfloat16)
    grad_out = rows_product(gated, cotan)
    d_gated = times_transposed(cotan, out_matrix)
    d_inner = (d_gated * silu_slope(inner)).astype(jnp.bfloat16)
    grad_in = rows_product(normed_b, d_inner)
    d_normed = times_transposed(d_inner, in_matrix)
    d_lifted = cotan.astype(jnp.float32) + scale * (
        d_normed - normed * jnp.mean(d_normed * normed, axis=-1, keepdims=True)
    )
    return (d_lifted.astype(jnp.bfloat16), grad_in, grad_out)


def up_forward(below, side, mix_matrix, up_matrix):
    joined = jnp.concatenate([below, side], axis=-1)
    mixed = jnp.dot(joined, mix_matrix, preferred_element_type=jnp.float32)
    normed = mixed * rms_scale(mixed)
    active = jax.nn.silu(normed).astype(jnp.bfloat16)
    return (mixed + jnp.dot(active, up_matrix, preferred_element_type=jnp.float32)).astype(
        jnp.bfloat16
    )


def up_backward(below, side, mix_matrix, up_matrix, cotan):
    width = below.shape[-1]
    joined = jnp.concatenate([below, side], axis=-1)
    mixed = jnp.dot(joined, mix_matrix, preferred_element_type=jnp.float32)
    scale = rms_scale(mixed)
    normed = mixed * scale
    active = jax.nn.silu(normed).astype(jnp.bfloat16)
    grad_up = rows_product(active, cotan)
    d_active = times_transposed(cotan, up_matrix)
    d_normed = d_active * silu_slope(normed)
    d_mixed = (
        cotan.astype(jnp.float32)
        + scale * (d_normed - normed * jnp.mean(d_normed * normed, axis=-1, keepdims=True))
    ).astype(jnp.bfloat16)
    grad_mix = rows_product(joined, d_mixed)
    d_joined = times_transposed(d_mixed, mix_matrix)
    return (d_joined[:, :width].astype(jnp.bfloat16), d_joined[:, width:], grad_mix, grad_up)


def pick(store, slot):
    return lax.dynamic_index_in_dim(store, slot, 0, keepdims=False)


def place(store, slot, value, valid):
    return lax.dynamic_update_index_in_dim(
        store, jnp.where(valid, value, pick(store, slot)), slot, 0
    )


def run_ticks(lower, upper, step, carry):
    return lax.fori_loop(lower, upper, lambda tick, state: step(state, tick), carry)


def local(latents, clip_of_row, timestep, w_in, w_out, w_mix, w_up, out_grad):
    sections = lax.axis_size("pipe")
    section = lax.axis_index("pipe")
    width = latents.shape[1]
    micro = MICRO
    rows = latents.shape[0] // micro
    span = micro + sections - 1
    in_matrix = w_in[0]
    out_matrix = w_out[0]
    mix_matrix = w_mix[0]
    up_matrix = w_up[0]
    match = clip_of_row[0][:, None] == jnp.arange(timestep.shape[1], dtype=jnp.int32)[None, :]
    moment = jnp.sum(jnp.where(match, timestep[0][None, :], 0), axis=1).astype(jnp.float32)
    embedding = embed(moment, width)
    input_blocks = latents.reshape(micro, rows, width)
    embed_blocks = embedding.reshape(micro, rows, width)
    grad_blocks = out_grad.reshape(micro, rows, width)
    plain = jnp.zeros((rows, width), jnp.bfloat16)
    blank = jnp.zeros((micro, rows, width), jnp.bfloat16)

    def position(tick, offset):
        batch = tick - offset
        valid = (batch >= 0) & (batch < micro)
        return (jnp.clip(batch, 0, micro - 1), valid)

    def down_tick(carry, tick):
        recv_down, recv_up, down_in, skip, up_in = carry
        slot, valid = position(tick, section)
        source = jnp.where(section == 0, pick(input_blocks, slot), recv_down)
        result = lax.cond(
            valid,
            lambda: down_forward(source, pick(embed_blocks, slot), in_matrix, out_matrix),
            lambda: plain,
        )
        down_in = place(down_in, slot, source, valid)
        skip = place(skip, slot, result, valid)
        recv_down = shifted(result, "pipe", 1)
        return (recv_down, recv_up, down_in, skip, up_in)

    def up_tick(carry, tick):
        recv_down, recv_up, down_in, skip, up_in = carry
        slot, valid = position(tick, sections - 1 - section)
        side = pick(skip, slot)
        below = jnp.where(section == sections - 1, side, recv_up)
        result = lax.cond(
            valid, lambda: up_forward(below, side, mix_matrix, up_matrix), lambda: plain
        )
        up_in = place(up_in, slot, below, valid)
        recv_up = shifted(result, "pipe", -1)
        return (recv_down, recv_up, down_in, skip, up_in)

    forward = (plain, plain, blank, blank, blank)
    forward = run_ticks(0, span, down_tick, forward)
    forward = run_ticks(0, span, up_tick, forward)
    down_in, skip, up_in = (forward[2], forward[3], forward[4])
    zero_in = jnp.zeros(in_matrix.shape, jnp.float32)
    zero_out = jnp.zeros(out_matrix.shape, jnp.float32)
    zero_mix = jnp.zeros(mix_matrix.shape, jnp.float32)
    zero_up = jnp.zeros(up_matrix.shape, jnp.float32)
    zero_side = jnp.zeros((rows, width), jnp.float32)

    def up_back_tick(carry, tick):
        recv_up, recv_down, d_skip, grad_in, grad_out, grad_mix, grad_up = carry
        slot, valid = position(tick, section)
        cotan = jnp.where(section == 0, pick(grad_blocks, slot), recv_up)
        d_below, d_side, part_mix, part_up = lax.cond(
            valid,
            lambda: up_backward(pick(up_in, slot), pick(skip, slot), mix_matrix, up_matrix, cotan),
            lambda: (plain, zero_side, zero_mix, zero_up),
        )
        side_total = d_side + jnp.where(section == sections - 1, d_below.astype(jnp.float32), 0.0)
        d_skip = place(d_skip, slot, side_total, valid)
        recv_up = shifted(d_below, "pipe", 1)
        return (
            recv_up,
            recv_down,
            d_skip,
            grad_in,
            grad_out,
            grad_mix + part_mix,
            grad_up + part_up,
        )

    def down_back_tick(carry, tick):
        recv_up, recv_down, d_skip, grad_in, grad_out, grad_mix, grad_up = carry
        slot, valid = position(tick, sections - 1 - section)
        cotan = (pick(d_skip, slot) + recv_down.astype(jnp.float32)).astype(jnp.bfloat16)
        d_hidden, part_in, part_out = lax.cond(
            valid,
            lambda: down_backward(
                pick(down_in, slot), pick(embed_blocks, slot), in_matrix, out_matrix, cotan
            ),
            lambda: (plain, zero_in, zero_out),
        )
        recv_down = shifted(d_hidden, "pipe", -1)
        return (
            recv_up,
            recv_down,
            d_skip,
            grad_in + part_in,
            grad_out + part_out,
            grad_mix,
            grad_up,
        )

    backward = (
        plain,
        plain,
        jnp.zeros((micro, rows, width), jnp.float32),
        zero_in,
        zero_out,
        zero_mix,
        zero_up,
    )
    backward = run_ticks(0, span, up_back_tick, backward)
    backward = run_ticks(0, span, down_back_tick, backward)
    grad_in, grad_out, grad_mix, grad_up = lax.psum(
        (backward[3], backward[4], backward[5], backward[6]), "dp"
    )
    factor = 1.0 / lax.axis_size("dp")
    return (
        (grad_in * factor)[None],
        (grad_out * factor)[None],
        (grad_mix * factor)[None],
        (grad_up * factor)[None],
    )


def solution(mesh):
    return jax.shard_map(
        local,
        mesh=mesh,
        in_specs=(
            P("dp", None),
            P("dp", None),
            P("dp", None),
            P("pipe", None, None),
            P("pipe", None, None),
            P("pipe", None, None),
            P("pipe", None, None),
            P("dp", None),
        ),
        out_specs=(
            P("pipe", None, None),
            P("pipe", None, None),
            P("pipe", None, None),
            P("pipe", None, None),
        ),
        check_vma=False,
    )
```

profile of v0, /device:TPU:32, one launch (start us, length us, event | category | flops | bytes accessed | tf_op | source)
XLA Modules:
  0.0 1921.6 jit_solution(15158092478362990073)
XLA Ops:
  16.3 111.1 %while.76 = (s32[]{:T(128)}, bf16[96,320]{1,0:T(8,128)(2,1)}, bf16[4,96,320]{2,1,0:T(8,128)(2,1)S(1)}, bf16[4,96,320]{2,1,0:T(8,128)(2,1)S(1)}, s32[]{:T(128)}, ...) while((s32[]{:T(128)}, bf16[96,320]{1,0:T(8,128)(2,1)}, ...), condition=%wide.region_5.6_spmd, body=%wide.region_1.5_spmd.sunk | while | flops 79411304 | bytes 3070988 | solution.py:113
  26.1 10.5 collective-permute-start
  41.6 7.1 collective-permute-start
  53.7 8.7 collective-permute-start
  65.7 10.3 collective-permute-start
  79.4 8.7 collective-permute-start
  91.5 10.3 collective-permute-start
  105.2 8.7 collective-permute-start
  117.2 8.7 collective-permute-start
  128.4 108.2 %while.77 = (s32[]{:T(128)}, bf16[96,320]{1,0:T(8,128)(2,1)S(1)}, bf16[4,96,320]{2,1,0:T(8,128)(2,1)}, s32[]{:T(128)}, pred[]{:T(512)}, /*index=5*/bf16[4,96,320...) while((s32[]{:T(128)}, bf16[96,320]{1,0:T(8,128)(2,1)S(1)}, ...), condition=%wide.region_10.11_spmd, body=%wide.region_6.10_spmd.sunk | while | flops 59596904 | bytes 2615592 | solution.py:113
  131.3 8.1 collective-permute-done.1
  142.3 8.9 collective-permute-done.1
  154.1 8.3 collective-permute-done.1
  165.3 8.3 collective-permute-done.1
  176.5 11.9 collective-permute-done.1
  192.5 8.3 collective-permute-done.1
  204.8 8.3 collective-permute-done.1
  217.2 8.3 collective-permute-done.1
  229.6 7.1 collective-permute-done.1
  238.1 133.7 %while.78 = (s32[]{:T(128)}, bf16[96,320]{1,0:T(8,128)(2,1)}, f32[4,96,320]{2,1,0:T(8,128)}, f32[640,320]{0,1:T(8,128)}, f32[320,320]{1,0:T(8,128)S(1)}, /*index...) while((s32[]{:T(128)}, bf16[96,320]{1,0:T(8,128)(2,1)}, ...), condition=%wide.region_16.17_spmd.clone, body=%wide.region_11.16_spmd.clone.sunk | while | flops 159344736 | bytes 12305658 | solution.py:113
  238.8 5.2 conditional.12
  244.0 6.3 collective-permute-start.2
  254.8 5.2 conditional.12
  259.9 5.2 collective-permute-start.2
  270.7 5.2 conditional.12
  275.9 5.7 collective-permute-start.2
  287.1 5.2 conditional.12
  292.3 5.1 collective-permute-start.2
  305.0 8.2 collective-permute-start.2
  320.8 5.0 collective-permute-start.2
  333.5 8.2 collective-permute-start.2
  349.3 5.0 collective-permute-start.2
  362.0 5.0 collective-permute-start.2
  372.7 107.7 %while.79 = (s32[]{:T(128)}, bf16[96,320]{1,0:T(8,128)(2,1)S(1)}, f32[320,640]{1,0:T(8,128)S(1)}, f32[640,320]{0,1:T(8,128)}, s32[]{:T(128)}, /*index=5*/f32[4,9...) while((s32[]{:T(128)}, bf16[96,320]{1,0:T(8,128)(2,1)S(1)}, ...), condition=%wide.region_22.23_spmd.clone, body=%wide.region_17.22_spmd.clone.sunk | while | flops 198932576 | bytes 12313092 | solution.py:113
  376.3 2.7 collective-permute-done.3
  383.7 5.9 collective-permute-done.3
  394.4 5.9 collective-permute-done.3
  405.0 5.9 collective-permute-done.3
  415.7 9.5 collective-permute-done.3
  426.2 3.7 conditional.13
  433.5 6.6 collective-permute-done.3
  441.0 3.7 conditional.13
  448.4 6.0 collective-permute-done.3
  455.3 3.6 conditional.13
  462.6 5.9 collective-permute-done.3
  469.5 3.7 conditional.13
  476.8 3.6 collective-permute-done.3
  481.3 1428.7 %all-reduce.3.cloned.1.call-done = (f32[320,640]{1,0:T(8,128)}, f32[640,320]{0,1:T(8,128)}, f32[640,320]{0,1:T(8,128)}, f32[320,320]{1,0:T(8,128)}) async-done(((f32[320,640]{1,0:T(8,128)}, f32[640,320]{0,1:T(8,128)}, f32[640,320]{0,1:T(8,128)}, f32[320,320]{1,0:T(8,128)}), (f32[320,640]{1,0:T(8,128)}, f32[640,320]{0,1:T(8,128)}, f32[640,320]{0,1:T(8,128)}, ...) | async-done | bytes 2867216 | tf_op jit(solution)/shard_map/psum | solution.py:232
  (490 shorter events, 243.2 us)
Async XLA Ops:
  7.2 1902.8 %all-reduce.3.cloned.1.call-start = ((), (), s32[]{:S(2)}) async-start(), calls=%async_computation | async-start | bytes 5898240 | tf_op jit(solution)/shard_map/psum | solution.py:232
  8.8 2.0 copy-start.14
  19.8 2.2 collective-permute-start
  26.1 11.4 collective-permute-start
  41.6 8.0 collective-permute-start
  53.7 9.6 collective-permute-start
  65.7 11.2 collective-permute-start
  79.4 9.6 collective-permute-start
  91.5 11.2 collective-permute-start
  105.2 9.6 collective-permute-start
  117.2 9.6 collective-permute-start
  130.0 9.4 collective-permute-start.1
  141.0 10.2 collective-permute-start.1
  152.8 9.6 collective-permute-start.1
  164.0 9.6 collective-permute-start.1
  175.2 13.2 collective-permute-start.1
  191.2 9.6 collective-permute-start.1
  203.5 9.6 collective-permute-start.1
  215.9 9.6 collective-permute-start.1
  228.3 8.4 collective-permute-start.1
  244.0 10.0 collective-permute-start.2
  252.4 1.7 copy-start.5
  259.9 10.0 collective-permute-start.2
  268.3 1.7 copy-start.5
  275.9 10.6 collective-permute-start.2
  284.8 1.7 copy-start.5
  292.3 9.9 collective-permute-start.2
  300.6 1.7 copy-start.5
  305.0 13.0 collective-permute-start.2
  316.4 1.7 copy-start.5
  320.8 9.9 collective-permute-start.2
  329.1 1.7 copy-start.5
  333.5 13.0 collective-permute-start.2
  344.9 1.7 copy-start.5
  349.3 9.9 collective-permute-start.2
  357.5 1.7 copy-start.5
  362.0 9.9 collective-permute-start.2
  373.8 5.2 collective-permute-start.3
  380.0 9.6 collective-permute-start.3
  390.7 9.6 collective-permute-start.3
  401.4 9.6 collective-permute-start.3
  412.1 13.2 collective-permute-start.3
  429.9 10.3 collective-permute-start.3
  444.7 9.6 collective-permute-start.3
  458.9 9.6 collective-permute-start.3
  473.1 7.3 collective-permute-start.3
  1910.0 2.2 copy-start.12
  1910.0 3.0 copy-start.10
  (50 other events, 44.2 us)
Sparse Core Ops, SparseCore 0:
  481.4 1428.5 all-reduce.2
where the time goes:
time: 1930 us; the launch traced here: 1920 us
  waiting for transfers between devices  1570 us (81%)
  starting transfers between devices  151 us (8%)
  other arithmetic  95.4 us (5%)
  local copies, waits for them, and re-layouts  71 us (4%)
  matrix products  21.9 us (1%)
    psum x1, waiting for transfers between devices, local(): lax.psum((backward[3], backward[4], backward[5], backward[6]), 'dp')  1430 us
    ppermute x36, starting transfers between devices, shifted(): lax.ppermute(value, axis, [(source, source + steps) for source in range(l...  151 us
    ppermute x36, waiting for transfers between devices, shifted(): lax.ppermute(value, axis, [(source, source + steps) for source in range(l...  137 us
  transfers between devices with their start and end apart: 37, of which 28 were waited for; matrix products, arithmetic and copies ran while one was open for 3% of the time, Pallas kernels for 0%

commit v1 on v0

--- a/solution.py
+++ b/solution.py
@@ -3,9 +3,10 @@
 import jax
 import jax.numpy as jnp
 from jax import lax
-from jax.sharding import PartitionSpec as P
+from jax.sharding import Mesh, PartitionSpec as P
 
 MICRO = 4
+DP = ("y", "x", "zl")
 
 
 def shifted(value, axis, steps):
@@ -111,6 +112,33 @@
 
 def run_ticks(lower, upper, step, carry):
     return lax.fori_loop(lower, upper, lambda tick, state: step(state, tick), carry)
+
+
+def reduce_replicas(parts):
+    total = sum(part.size for part in parts)
+    groups = math.prod(lax.axis_size(name) for name in DP)
+    lanes = 128
+    length = -(-total // (lanes * groups * 8)) * groups * 8
+    flat = jnp.concatenate([part.reshape(-1) for part in parts])
+    flat = jnp.pad(flat, (0, length * lanes - total)).reshape(length, lanes)
+    for name in reversed(DP):
+        flat = lax.psum_scatter(flat, name, scatter_dimension=0, tiled=True)
+    for name in DP:
+        flat = lax.all_gather(flat, name, axis=0, tiled=True)
+    flat = flat.reshape(-1)
+    out, start = [], 0
+    for part in parts:
+        out.append(flat[start : start + part.size].reshape(part.shape))
+        start += part.size
+    return tuple(out)
+
+
+def dp_split(mesh):
+    column = mesh.devices[:, 0]
+    sizes = [len({int(device.coords[axis]) for device in column}) for axis in (1, 0, 2)]
+    if math.prod(sizes) != column.size:
+        raise ValueError("dp split")
+    return tuple(sizes)
 
 
 def local(latents, clip_of_row, timestep, w_in, w_out, w_mix, w_up, out_grad):
@@ -229,10 +257,10 @@
     )
     backward = run_ticks(0, span, up_back_tick, backward)
     backward = run_ticks(0, span, down_back_tick, backward)
-    grad_in, grad_out, grad_mix, grad_up = lax.psum(
-        (backward[3], backward[4], backward[5], backward[6]), "dp"
-    )
-    factor = 1.0 / lax.axis_size("dp")
+    grad_in, grad_out, grad_mix, grad_up = reduce_replicas(
+        (backward[3], backward[4], backward[5], backward[6])
+    )
+    factor = 1.0 / math.prod(lax.axis_size(name) for name in DP)
     return (
         (grad_in * factor)[None],
         (grad_out * factor)[None],
@@ -242,18 +270,21 @@
 
 
 def solution(mesh):
+    sizes = dp_split(mesh)
+    pipe = mesh.devices.shape[1]
+    split = Mesh(mesh.devices.reshape(*sizes, pipe), DP + ("pipe",))
     return jax.shard_map(
         local,
-        mesh=mesh,
+        mesh=split,
         in_specs=(
-            P("dp", None),
-            P("dp", None),
-            P("dp", None),
-            P("pipe", None, None),
-            P("pipe", None, None),
-            P("pipe", None, None),
-            P("pipe", None, None),
-            P("dp", None),
+            P(DP, None),
+            P(DP, None),
+            P(DP, None),
+            P("pipe", None, None),
+            P("pipe", None, None),
+            P("pipe", None, None),
+            P("pipe", None, None),
+            P(DP, None),
         ),
         out_specs=(
             P("pipe", None, None),

time: 1930 us -> 774 us (0.40)
  the two profiles are of different devices: /device:TPU:32 before, /device:TPU:1 now
where the time goes in v1:
time: 774 us; the launch traced here: 769 us
  waiting for transfers between devices  353 us (46%)
  starting transfers between devices  159 us (21%)
  other arithmetic  111 us (14%)
  local copies, waits for them, and re-layouts  64.8 us (8%)
  matrix products  33.7 us (4%)
  blocking collectives  30.6 us (4%)
  between operations  13.9 us (2%)
    ppermute x36, starting transfers between devices, shifted(): lax.ppermute(value, axis, [(source, source + steps) for source in range(l...  159 us
    reduce_scatter x3, waiting for transfers between devices, reduce_replicas(): flat = lax.psum_scatter(flat, name, scatter_dimension=0, tiled=True)  144 us
    ppermute x36, waiting for transfers between devices, shifted(): lax.ppermute(value, axis, [(source, source + steps) for source in range(l...  124 us
    all_gather x1, waiting for transfers between devices, reduce_replicas(): flat = lax.all_gather(flat, name, axis=0, tiled=True)  85 us
    dynamic_update_slice x36, other arithmetic, place(): lax.dynamic_update_index_in_dim(store, jnp.where(valid, value, pick(store...  42.7 us
    all_gather x2, blocking collectives, reduce_replicas(): flat = lax.all_gather(flat, name, axis=0, tiled=True)  30.6 us
    dynamic_slice x36, local copies, waits for them, and re-layouts, pick(): return lax.dynamic_index_in_dim(store, slot, 0, keepdims=False)  24.5 us
    add x9, other arithmetic, up_back_tick(): grad_mix + part_mix  18 us
  transfers between devices with their start and end apart: 40, of which 23 were waited for; matrix products, arithmetic and copies ran while one was open for 10% of the time, Pallas kernels for 0%

profile of v1, /device:TPU:1, one launch (start us, length us, event | category | flops | bytes accessed | tf_op | source)
XLA Modules:
  0.0 768.6 jit_solution(7979291518868404138)
XLA Ops:
  18.2 105.6 %while.76 = (s32[]{:T(128)}, bf16[96,320]{1,0:T(8,128)(2,1)S(1)}, bf16[4,96,320]{2,1,0:T(8,128)(2,1)S(1)}, bf16[4,96,320]{2,1,0:T(8,128)(2,1)}, s32[]{:T(128)}, ...) while((s32[]{:T(128)}, bf16[96,320]{1,0:T(8,128)(2,1)S(1)}, ...), condition=%wide.region_5.6_spmd, body=%wide.region_1.5_spmd.sunk | while | flops 79411304 | bytes 2555344 | solution.py:114
  19.1 12.0 %collective-permute-start = (bf16[96,320]{1,0:T(8,128)(2,1)S(1)}, bf16[96,320]{1,0:T(8,128)(2,1)S(1)}, u32[]{:S(2)}, u32[]{:S(2)}) collective-permute-start(bf16[96,320]{1,0:T(8,128)(2,1)S(1)} %get-tuple-element.1651), channel_id=1, source_target_pairs={{0,1},{1,2},{2,3},{3,4},{4,5},{6,7},{7,8},{8,9},{9,10},{10,11},{12... | collective-permute-start | bytes 184328 | tf_op jit(solution)/shard_map/while/body/eval_jaxpr/ppermute | solution.py:15
  35.9 5.8 collective-permute-start
  45.9 8.0 %collective-permute-start = (bf16[96,320]{1,0:T(8,128)(2,1)S(1)}, bf16[96,320]{1,0:T(8,128)(2,1)S(1)}, u32[]{:S(2)}, u32[]{:S(2)}) collective-permute-start(bf16[96,320]{1,0:T(8,128)(2,1)S(1)} %get-tuple-element.1651), channel_id=1, source_target_pairs={{0,1},{1,2},{2,3},{3,4},{4,5},{6,7},{7,8},{8,9},{9,10},{10,11},{12... | collective-permute-start | bytes 184328 | tf_op jit(solution)/shard_map/while/body/eval_jaxpr/ppermute | solution.py:15
  58.1 8.0 %collective-permute-start = (bf16[96,320]{1,0:T(8,128)(2,1)S(1)}, bf16[96,320]{1,0:T(8,128)(2,1)S(1)}, u32[]{:S(2)}, u32[]{:S(2)}) collective-permute-start(bf16[96,320]{1,0:T(8,128)(2,1)S(1)} %get-tuple-element.1651), channel_id=1, source_target_pairs={{0,1},{1,2},{2,3},{3,4},{4,5},{6,7},{7,8},{8,9},{9,10},{10,11},{12... | collective-permute-start | bytes 184328 | tf_op jit(solution)/shard_map/while/body/eval_jaxpr/ppermute | solution.py:15
  70.3 8.0 %collective-permute-start = (bf16[96,320]{1,0:T(8,128)(2,1)S(1)}, bf16[96,320]{1,0:T(8,128)(2,1)S(1)}, u32[]{:S(2)}, u32[]{:S(2)}) collective-permute-start(bf16[96,320]{1,0:T(8,128)(2,1)S(1)} %get-tuple-element.1651), channel_id=1, source_target_pairs={{0,1},{1,2},{2,3},{3,4},{4,5},{6,7},{7,8},{8,9},{9,10},{10,11},{12... | collective-permute-start | bytes 184328 | tf_op jit(solution)/shard_map/while/body/eval_jaxpr/ppermute | solution.py:15
  80.9 9.6 %collective-permute-start = (bf16[96,320]{1,0:T(8,128)(2,1)S(1)}, bf16[96,320]{1,0:T(8,128)(2,1)S(1)}, u32[]{:S(2)}, u32[]{:S(2)}) collective-permute-start(bf16[96,320]{1,0:T(8,128)(2,1)S(1)} %get-tuple-element.1651), channel_id=1, source_target_pairs={{0,1},{1,2},{2,3},{3,4},{4,5},{6,7},{7,8},{8,9},{9,10},{10,11},{12... | collective-permute-start | bytes 184328 | tf_op jit(solution)/shard_map/while/body/eval_jaxpr/ppermute | solution.py:15
  93.1 8.0 %collective-permute-start = (bf16[96,320]{1,0:T(8,128)(2,1)S(1)}, bf16[96,320]{1,0:T(8,128)(2,1)S(1)}, u32[]{:S(2)}, u32[]{:S(2)}) collective-permute-start(bf16[96,320]{1,0:T(8,128)(2,1)S(1)} %get-tuple-element.1651), channel_id=1, source_target_pairs={{0,1},{1,2},{2,3},{3,4},{4,5},{6,7},{7,8},{8,9},{9,10},{10,11},{12... | collective-permute-start | bytes 184328 | tf_op jit(solution)/shard_map/while/body/eval_jaxpr/ppermute | solution.py:15
  103.6 8.0 %collective-permute-start = (bf16[96,320]{1,0:T(8,128)(2,1)S(1)}, bf16[96,320]{1,0:T(8,128)(2,1)S(1)}, u32[]{:S(2)}, u32[]{:S(2)}) collective-permute-start(bf16[96,320]{1,0:T(8,128)(2,1)S(1)} %get-tuple-element.1651), channel_id=1, source_target_pairs={{0,1},{1,2},{2,3},{3,4},{4,5},{6,7},{7,8},{8,9},{9,10},{10,11},{12... | collective-permute-start | bytes 184328 | tf_op jit(solution)/shard_map/while/body/eval_jaxpr/ppermute | solution.py:15
  114.2 8.0 %collective-permute-start = (bf16[96,320]{1,0:T(8,128)(2,1)S(1)}, bf16[96,320]{1,0:T(8,128)(2,1)S(1)}, u32[]{:S(2)}, u32[]{:S(2)}) collective-permute-start(bf16[96,320]{1,0:T(8,128)(2,1)S(1)} %get-tuple-element.1651), channel_id=1, source_target_pairs={{0,1},{1,2},{2,3},{3,4},{4,5},{6,7},{7,8},{8,9},{9,10},{10,11},{12... | collective-permute-start | bytes 184328 | tf_op jit(solution)/shard_map/while/body/eval_jaxpr/ppermute | solution.py:15
  124.8 118.6 %while.77 = (s32[]{:T(128)}, bf16[96,320]{1,0:T(8,128)(2,1)S(1)}, bf16[4,96,320]{2,1,0:T(8,128)(2,1)}, s32[]{:T(128)}, pred[]{:T(512)}, /*index=5*/bf16[4,96,320...) while((s32[]{:T(128)}, bf16[96,320]{1,0:T(8,128)(2,1)S(1)}, ...), condition=%wide.region_10.11_spmd, body=%wide.region_6.10_spmd.sunk | while | flops 59596904 | bytes 1808652 | solution.py:114
  129.2 8.5 %collective-permute-done.1 = bf16[96,320]{1,0:T(8,128)(2,1)S(1)} collective-permute-done((bf16[96,320]{1,0:T(8,128)(2,1)S(1)}, bf16[96,320]{1,0:T(8,128)(2,1)S(1)}, u32[]{:S(2)}, u32[]{:S(2)}) %collective-permute-start.1) | collective-permute-done | bytes 61472 | tf_op jit(solution)/shard_map/while/body/eval_jaxpr/ppermute | solution.py:15
  142.1 7.6 collective-permute-done.1
  154.1 7.6 collective-permute-done.1
  166.2 10.5 %collective-permute-done.1 = bf16[96,320]{1,0:T(8,128)(2,1)S(1)} collective-permute-done((bf16[96,320]{1,0:T(8,128)(2,1)S(1)}, bf16[96,320]{1,0:T(8,128)(2,1)S(1)}, u32[]{:S(2)}, u32[]{:S(2)}) %collective-permute-start.1) | collective-permute-done | bytes 61472 | tf_op jit(solution)/shard_map/while/body/eval_jaxpr/ppermute | solution.py:15
  182.7 7.7 collective-permute-done.1
  196.4 7.7 collective-permute-done.1
  210.0 7.7 collective-permute-done.1
  223.7 7.7 collective-permute-done.1
  235.8 7.7 collective-permute-done.1
  244.9 125.9 %while.78 = (s32[]{:T(128)}, bf16[96,320]{1,0:T(8,128)(2,1)}, f32[4,96,320]{2,1,0:T(8,128)}, f32[640,320]{0,1:T(8,128)}, f32[320,320]{1,0:T(8,128)S(1)}, /*index...) while((s32[]{:T(128)}, bf16[96,320]{1,0:T(8,128)(2,1)}, ...), condition=%wide.region_16.17_spmd.clone, body=%wide.region_11.16_spmd.clone.sunk | while | flops 159344736 | bytes 9520294 | solution.py:114
  254.9 6.2 conditional.12
  270.6 6.2 conditional.12
  276.8 5.1 collective-permute-start.2
  286.7 6.2 conditional.12
  292.9 5.1 collective-permute-start.2
  302.7 6.2 conditional.12
  308.9 5.1 collective-permute-start.2
  320.9 9.2 %collective-permute-start.2 = (bf16[96,320]{1,0:T(8,128)(2,1)}, bf16[96,320]{1,0:T(8,128)(2,1)}, u32[]{:S(2)}, u32[]{:S(2)}) collective-permute-start(bf16[96,320]{1,0:T(8,128)(2,1)} %get-tuple-element.1446), channel_id=1, source_target_pairs={{0,1},{1,2},{2,3},{3,4},{4,5},{6,7},{7,8},{8,9},{9,10},{10,11},{12... | collective-permute-start | bytes 184328 | tf_op jit(solution)/shard_map/while/body/eval_jaxpr/ppermute | solution.py:15
  337.0 5.1 collective-permute-start.2
  349.0 5.1 collective-permute-start.2
  360.9 5.1 collective-permute-start.2
  374.7 113.5 %while.79 = (s32[]{:T(128)}, bf16[96,320]{1,0:T(8,128)(2,1)S(1)}, f32[320,640]{1,0:T(8,128)S(1)}, f32[640,320]{0,1:T(8,128)}, s32[]{:T(128)}, /*index=5*/f32[4,9...) while((s32[]{:T(128)}, bf16[96,320]{1,0:T(8,128)(2,1)S(1)}, ...), condition=%wide.region_22.23_spmd.clone, body=%wide.region_17.22_spmd.clone.sunk | while | flops 198932576 | bytes 10674664 | solution.py:114
  379.0 6.4 collective-permute-done.3
  390.8 5.3 collective-permute-done.3
  401.5 5.3 collective-permute-done.3
  412.1 7.5 collective-permute-done.3
  428.8 5.3 collective-permute-done.3
  443.3 5.3 collective-permute-done.3
  457.7 5.3 collective-permute-done.3
  472.2 5.3 collective-permute-done.3
  482.9 5.3 collective-permute-done.3
  494.3 70.2 %reduce-scatter.4.cloned.1.call-done = f32[1536,128]{1,0:T(8,128)} async-done(((f32[6144,128]{1,0:T(8,128)}), f32[1536,128]{1,0:T(8,128)}) %reduce-scatter.4.cloned.1.call-update) | async-done | bytes 786448 | tf_op jit(solution)/shard_map/reduce_scatter | solution.py:125
  564.6 33.4 %reduce-scatter.6.cloned.1.call-done = f32[384,128]{1,0:T(8,128)} async-done(((f32[1536,128]{1,0:T(8,128)}), f32[384,128]{1,0:T(8,128)}) %reduce-scatter.6.cloned.1.call-update) | async-done | bytes 196624 | tf_op jit(solution)/shard_map/reduce_scatter | solution.py:125
  598.1 40.4 %reduce-scatter.8.cloned.1.call-done = f32[48,128]{1,0:T(8,128)} async-done(((f32[384,128]{1,0:T(8,128)}), f32[48,128]{1,0:T(8,128)}) %reduce-scatter.8.cloned.1.call-update) | async-done | bytes 24592 | tf_op jit(solution)/shard_map/reduce_scatter | solution.py:125
  638.5 18.9 %all_gather.9 = f32[384,128]{1,0:T(8,128)S(1)} all-gather(f32[48,128]{1,0:T(8,128)} %reduce-scatter.8.cloned.1.call-done), channel_id=1, replica_groups=mesh['y'=8,'x'=4,'zl'=4,'pipe'=6] {'y'}, dimensions={0}, use_global_device_ids=true | all-gather | bytes 221184 | tf_op jit(solution)/shard_map/all_gather | solution.py:127
  657.4 11.7 %all_gather.10 = f32[1536,128]{1,0:T(8,128)} all-gather(f32[384,128]{1,0:T(8,128)S(1)} %all_gather.9), channel_id=1, replica_groups=mesh['y'=8,'x'=4,'zl'=4,'pipe'=6] {'x'}, dimensions={0}, use_global_device_ids=true | all-gather | bytes 983040 | tf_op jit(solution)/shard_map/all_gather | solution.py:127
  669.1 85.0 %all-gather.2.cloned.1.call-done = f32[6144,128]{1,0:T(8,128)} async-done(((f32[1536,128]{1,0:T(8,128)}), f32[6144,128]{1,0:T(8,128)}) %all-gather.2.cloned.1.call-update) | async-done | bytes 3145744 | tf_op jit(solution)/shard_map/all_gather | solution.py:127
  (401 shorter events, 294.8 us)
Async XLA Ops:
  7.2 11.0 %copy-start = (bf16[1,320,640]{2,1,0:T(8,128)(2,1)S(1)}, bf16[1,320,640]{2,1,0:T(8,128)(2,1)}, u32[]{:S(2)}) copy-start(bf16[1,320,640]{2,1,0:T(8,128)(2,1)} %param.27) | copy-start | bytes 1228804
  7.2 557.3 %reduce-scatter.4.cloned.1.call-start = ((), (), s32[]{:S(2)}) async-start(), calls=%async_computation.3 | async-start | bytes 3932160 | tf_op jit(solution)/shard_map/reduce_scatter | solution.py:125
  19.1 14.2 %collective-permute-start = (bf16[96,320]{1,0:T(8,128)(2,1)S(1)}, bf16[96,320]{1,0:T(8,128)(2,1)S(1)}, u32[]{:S(2)}, u32[]{:S(2)}) collective-permute-start(bf16[96,320]{1,0:T(8,128)(2,1)S(1)} %get-tuple-element.1651), channel_id=1, source_target_pairs={{0,1},{1,2},{2,3},{3,4},{4,5},{6,7},{7,8},{8,9},{9,10},{10,11},{12... | collective-permute-start | bytes 184328 | tf_op jit(solution)/shard_map/while/body/eval_jaxpr/ppermute | solution.py:15
  35.9 7.4 collective-permute-start
  45.9 9.6 %collective-permute-start = (bf16[96,320]{1,0:T(8,128)(2,1)S(1)}, bf16[96,320]{1,0:T(8,128)(2,1)S(1)}, u32[]{:S(2)}, u32[]{:S(2)}) collective-permute-start(bf16[96,320]{1,0:T(8,128)(2,1)S(1)} %get-tuple-element.1651), channel_id=1, source_target_pairs={{0,1},{1,2},{2,3},{3,4},{4,5},{6,7},{7,8},{8,9},{9,10},{10,11},{12... | collective-permute-start | bytes 184328 | tf_op jit(solution)/shard_map/while/body/eval_jaxpr/ppermute | solution.py:15
  58.1 9.6 %collective-permute-start = (bf16[96,320]{1,0:T(8,128)(2,1)S(1)}, bf16[96,320]{1,0:T(8,128)(2,1)S(1)}, u32[]{:S(2)}, u32[]{:S(2)}) collective-permute-start(bf16[96,320]{1,0:T(8,128)(2,1)S(1)} %get-tuple-element.1651), channel_id=1, source_target_pairs={{0,1},{1,2},{2,3},{3,4},{4,5},{6,7},{7,8},{8,9},{9,10},{10,11},{12... | collective-permute-start | bytes 184328 | tf_op jit(solution)/shard_map/while/body/eval_jaxpr/ppermute | solution.py:15
  70.3 9.6 %collective-permute-start = (bf16[96,320]{1,0:T(8,128)(2,1)S(1)}, bf16[96,320]{1,0:T(8,128)(2,1)S(1)}, u32[]{:S(2)}, u32[]{:S(2)}) collective-permute-start(bf16[96,320]{1,0:T(8,128)(2,1)S(1)} %get-tuple-element.1651), channel_id=1, source_target_pairs={{0,1},{1,2},{2,3},{3,4},{4,5},{6,7},{7,8},{8,9},{9,10},{10,11},{12... | collective-permute-start | bytes 184328 | tf_op jit(solution)/shard_map/while/body/eval_jaxpr/ppermute | solution.py:15
  80.9 11.2 %collective-permute-start = (bf16[96,320]{1,0:T(8,128)(2,1)S(1)}, bf16[96,320]{1,0:T(8,128)(2,1)S(1)}, u32[]{:S(2)}, u32[]{:S(2)}) collective-permute-start(bf16[96,320]{1,0:T(8,128)(2,1)S(1)} %get-tuple-element.1651), channel_id=1, source_target_pairs={{0,1},{1,2},{2,3},{3,4},{4,5},{6,7},{7,8},{8,9},{9,10},{10,11},{12... | collective-permute-start | bytes 184328 | tf_op jit(solution)/shard_map/while/body/eval_jaxpr/ppermute | solution.py:15
  93.1 9.6 %collective-permute-start = (bf16[96,320]{1,0:T(8,128)(2,1)S(1)}, bf16[96,320]{1,0:T(8,128)(2,1)S(1)}, u32[]{:S(2)}, u32[]{:S(2)}) collective-permute-start(bf16[96,320]{1,0:T(8,128)(2,1)S(1)} %get-tuple-element.1651), channel_id=1, source_target_pairs={{0,1},{1,2},{2,3},{3,4},{4,5},{6,7},{7,8},{8,9},{9,10},{10,11},{12... | collective-permute-start | bytes 184328 | tf_op jit(solution)/shard_map/while/body/eval_jaxpr/ppermute | solution.py:15
  103.6 9.6 %collective-permute-start = (bf16[96,320]{1,0:T(8,128)(2,1)S(1)}, bf16[96,320]{1,0:T(8,128)(2,1)S(1)}, u32[]{:S(2)}, u32[]{:S(2)}) collective-permute-start(bf16[96,320]{1,0:T(8,128)(2,1)S(1)} %get-tuple-element.1651), channel_id=1, source_target_pairs={{0,1},{1,2},{2,3},{3,4},{4,5},{6,7},{7,8},{8,9},{9,10},{10,11},{12... | collective-permute-start | bytes 184328 | tf_op jit(solution)/shard_map/while/body/eval_jaxpr/ppermute | solution.py:15
  114.2 9.6 %collective-permute-start = (bf16[96,320]{1,0:T(8,128)(2,1)S(1)}, bf16[96,320]{1,0:T(8,128)(2,1)S(1)}, u32[]{:S(2)}, u32[]{:S(2)}) collective-permute-start(bf16[96,320]{1,0:T(8,128)(2,1)S(1)} %get-tuple-element.1651), channel_id=1, source_target_pairs={{0,1},{1,2},{2,3},{3,4},{4,5},{6,7},{7,8},{8,9},{9,10},{10,11},{12... | collective-permute-start | bytes 184328 | tf_op jit(solution)/shard_map/while/body/eval_jaxpr/ppermute | solution.py:15
  123.8 0.9 copy-start.1
  123.8 1.0 copy-start.2
  127.3 10.4 %collective-permute-start.1 = (bf16[96,320]{1,0:T(8,128)(2,1)S(1)}, bf16[96,320]{1,0:T(8,128)(2,1)S(1)}, u32[]{:S(2)}, u32[]{:S(2)}) collective-permute-start(bf16[96,320]{1,0:T(8,128)(2,1)S(1)} %get-tuple-element.1652), channel_id=1, source_target_pairs={{1,0},{2,1},{3,2},{4,3},{5,4},{7,6},{8,7},{9,8},{10,9},{11,10},{13... | collective-permute-start | bytes 184328 | tf_op jit(solution)/shard_map/while/body/eval_jaxpr/ppermute | solution.py:15
  140.1 9.6 %collective-permute-start.1 = (bf16[96,320]{1,0:T(8,128)(2,1)S(1)}, bf16[96,320]{1,0:T(8,128)(2,1)S(1)}, u32[]{:S(2)}, u32[]{:S(2)}) collective-permute-start(bf16[96,320]{1,0:T(8,128)(2,1)S(1)} %get-tuple-element.1652), channel_id=1, source_target_pairs={{1,0},{2,1},{3,2},{4,3},{5,4},{7,6},{8,7},{9,8},{10,9},{11,10},{13... | collective-permute-start | bytes 184328 | tf_op jit(solution)/shard_map/while/body/eval_jaxpr/ppermute | solution.py:15
  152.2 9.6 %collective-permute-start.1 = (bf16[96,320]{1,0:T(8,128)(2,1)S(1)}, bf16[96,320]{1,0:T(8,128)(2,1)S(1)}, u32[]{:S(2)}, u32[]{:S(2)}) collective-permute-start(bf16[96,320]{1,0:T(8,128)(2,1)S(1)} %get-tuple-element.1652), channel_id=1, source_target_pairs={{1,0},{2,1},{3,2},{4,3},{5,4},{7,6},{8,7},{9,8},{10,9},{11,10},{13... | collective-permute-start | bytes 184328 | tf_op jit(solution)/shard_map/while/body/eval_jaxpr/ppermute | solution.py:15
  164.2 12.5 %collective-permute-start.1 = (bf16[96,320]{1,0:T(8,128)(2,1)S(1)}, bf16[96,320]{1,0:T(8,128)(2,1)S(1)}, u32[]{:S(2)}, u32[]{:S(2)}) collective-permute-start(bf16[96,320]{1,0:T(8,128)(2,1)S(1)} %get-tuple-element.1652), channel_id=1, source_target_pairs={{1,0},{2,1},{3,2},{4,3},{5,4},{7,6},{8,7},{9,8},{10,9},{11,10},{13... | collective-permute-start | bytes 184328 | tf_op jit(solution)/shard_map/while/body/eval_jaxpr/ppermute | solution.py:15
  180.8 9.6 %collective-permute-start.1 = (bf16[96,320]{1,0:T(8,128)(2,1)S(1)}, bf16[96,320]{1,0:T(8,128)(2,1)S(1)}, u32[]{:S(2)}, u32[]{:S(2)}) collective-permute-start(bf16[96,320]{1,0:T(8,128)(2,1)S(1)} %get-tuple-element.1652), channel_id=1, source_target_pairs={{1,0},{2,1},{3,2},{4,3},{5,4},{7,6},{8,7},{9,8},{10,9},{11,10},{13... | collective-permute-start | bytes 184328 | tf_op jit(solution)/shard_map/while/body/eval_jaxpr/ppermute | solution.py:15
  194.4 9.6 %collective-permute-start.1 = (bf16[96,320]{1,0:T(8,128)(2,1)S(1)}, bf16[96,320]{1,0:T(8,128)(2,1)S(1)}, u32[]{:S(2)}, u32[]{:S(2)}) collective-permute-start(bf16[96,320]{1,0:T(8,128)(2,1)S(1)} %get-tuple-element.1652), channel_id=1, source_target_pairs={{1,0},{2,1},{3,2},{4,3},{5,4},{7,6},{8,7},{9,8},{10,9},{11,10},{13... | collective-permute-start | bytes 184328 | tf_op jit(solution)/shard_map/while/body/eval_jaxpr/ppermute | solution.py:15
  208.1 9.6 %collective-permute-start.1 = (bf16[96,320]{1,0:T(8,128)(2,1)S(1)}, bf16[96,320]{1,0:T(8,128)(2,1)S(1)}, u32[]{:S(2)}, u32[]{:S(2)}) collective-permute-start(bf16[96,320]{1,0:T(8,128)(2,1)S(1)} %get-tuple-element.1652), channel_id=1, source_target_pairs={{1,0},{2,1},{3,2},{4,3},{5,4},{7,6},{8,7},{9,8},{10,9},{11,10},{13... | collective-permute-start | bytes 184328 | tf_op jit(solution)/shard_map/while/body/eval_jaxpr/ppermute | solution.py:15
  221.8 9.6 %collective-permute-start.1 = (bf16[96,320]{1,0:T(8,128)(2,1)S(1)}, bf16[96,320]{1,0:T(8,128)(2,1)S(1)}, u32[]{:S(2)}, u32[]{:S(2)}) collective-permute-start(bf16[96,320]{1,0:T(8,128)(2,1)S(1)} %get-tuple-element.1652), channel_id=1, source_target_pairs={{1,0},{2,1},{3,2},{4,3},{5,4},{7,6},{8,7},{9,8},{10,9},{11,10},{13... | collective-permute-start | bytes 184328 | tf_op jit(solution)/shard_map/while/body/eval_jaxpr/ppermute | solution.py:15
  233.8 9.6 %collective-permute-start.1 = (bf16[96,320]{1,0:T(8,128)(2,1)S(1)}, bf16[96,320]{1,0:T(8,128)(2,1)S(1)}, u32[]{:S(2)}, u32[]{:S(2)}) collective-permute-start(bf16[96,320]{1,0:T(8,128)(2,1)S(1)} %get-tuple-element.1652), channel_id=1, source_target_pairs={{1,0},{2,1},{3,2},{4,3},{5,4},{7,6},{8,7},{9,8},{10,9},{11,10},{13... | collective-permute-start | bytes 184328 | tf_op jit(solution)/shard_map/while/body/eval_jaxpr/ppermute | solution.py:15
  247.0 7.9 %collective-permute-start.2 = (bf16[96,320]{1,0:T(8,128)(2,1)}, bf16[96,320]{1,0:T(8,128)(2,1)}, u32[]{:S(2)}, u32[]{:S(2)}) collective-permute-start(bf16[96,320]{1,0:T(8,128)(2,1)} %get-tuple-element.1446), channel_id=1, source_target_pairs={{0,1},{1,2},{2,3},{3,4},{4,5},{6,7},{7,8},{8,9},{9,10},{10,11},{12... | collective-permute-start | bytes 184328 | tf_op jit(solution)/shard_map/while/body/eval_jaxpr/ppermute | solution.py:15
  261.1 9.6 %collective-permute-start.2 = (bf16[96,320]{1,0:T(8,128)(2,1)}, bf16[96,320]{1,0:T(8,128)(2,1)}, u32[]{:S(2)}, u32[]{:S(2)}) collective-permute-start(bf16[96,320]{1,0:T(8,128)(2,1)} %get-tuple-element.1446), channel_id=1, source_target_pairs={{0,1},{1,2},{2,3},{3,4},{4,5},{6,7},{7,8},{8,9},{9,10},{10,11},{12... | collective-permute-start | bytes 184328 | tf_op jit(solution)/shard_map/while/body/eval_jaxpr/ppermute | solution.py:15
  276.8 9.9 %collective-permute-start.2 = (bf16[96,320]{1,0:T(8,128)(2,1)}, bf16[96,320]{1,0:T(8,128)(2,1)}, u32[]{:S(2)}, u32[]{:S(2)}) collective-permute-start(bf16[96,320]{1,0:T(8,128)(2,1)} %get-tuple-element.1446), channel_id=1, source_target_pairs={{0,1},{1,2},{2,3},{3,4},{4,5},{6,7},{7,8},{8,9},{9,10},{10,11},{12... | collective-permute-start | bytes 184328 | tf_op jit(solution)/shard_map/while/body/eval_jaxpr/ppermute | solution.py:15
  292.9 9.9 %collective-permute-start.2 = (bf16[96,320]{1,0:T(8,128)(2,1)}, bf16[96,320]{1,0:T(8,128)(2,1)}, u32[]{:S(2)}, u32[]{:S(2)}) collective-permute-start(bf16[96,320]{1,0:T(8,128)(2,1)} %get-tuple-element.1446), channel_id=1, source_target_pairs={{0,1},{1,2},{2,3},{3,4},{4,5},{6,7},{7,8},{8,9},{9,10},{10,11},{12... | collective-permute-start | bytes 184328 | tf_op jit(solution)/shard_map/while/body/eval_jaxpr/ppermute | solution.py:15
  308.9 9.9 %collective-permute-start.2 = (bf16[96,320]{1,0:T(8,128)(2,1)}, bf16[96,320]{1,0:T(8,128)(2,1)}, u32[]{:S(2)}, u32[]{:S(2)}) collective-permute-start(bf16[96,320]{1,0:T(8,128)(2,1)} %get-tuple-element.1446), channel_id=1, source_target_pairs={{0,1},{1,2},{2,3},{3,4},{4,5},{6,7},{7,8},{8,9},{9,10},{10,11},{12... | collective-permute-start | bytes 184328 | tf_op jit(solution)/shard_map/while/body/eval_jaxpr/ppermute | solution.py:15
  320.9 14.0 %collective-permute-start.2 = (bf16[96,320]{1,0:T(8,128)(2,1)}, bf16[96,320]{1,0:T(8,128)(2,1)}, u32[]{:S(2)}, u32[]{:S(2)}) collective-permute-start(bf16[96,320]{1,0:T(8,128)(2,1)} %get-tuple-element.1446), channel_id=1, source_target_pairs={{0,1},{1,2},{2,3},{3,4},{4,5},{6,7},{7,8},{8,9},{9,10},{10,11},{12... | collective-permute-start | bytes 184328 | tf_op jit(solution)/shard_map/while/body/eval_jaxpr/ppermute | solution.py:15
  337.0 9.9 %collective-permute-start.2 = (bf16[96,320]{1,0:T(8,128)(2,1)}, bf16[96,320]{1,0:T(8,128)(2,1)}, u32[]{:S(2)}, u32[]{:S(2)}) collective-permute-start(bf16[96,320]{1,0:T(8,128)(2,1)} %get-tuple-element.1446), channel_id=1, source_target_pairs={{0,1},{1,2},{2,3},{3,4},{4,5},{6,7},{7,8},{8,9},{9,10},{10,11},{12... | collective-permute-start | bytes 184328 | tf_op jit(solution)/shard_map/while/body/eval_jaxpr/ppermute | solution.py:15
  349.0 9.9 %collective-permute-start.2 = (bf16[96,320]{1,0:T(8,128)(2,1)}, bf16[96,320]{1,0:T(8,128)(2,1)}, u32[]{:S(2)}, u32[]{:S(2)}) collective-permute-start(bf16[96,320]{1,0:T(8,128)(2,1)} %get-tuple-element.1446), channel_id=1, source_target_pairs={{0,1},{1,2},{2,3},{3,4},{4,5},{6,7},{7,8},{8,9},{9,10},{10,11},{12... | collective-permute-start | bytes 184328 | tf_op jit(solution)/shard_map/while/body/eval_jaxpr/ppermute | solution.py:15
  360.9 9.9 %collective-permute-start.2 = (bf16[96,320]{1,0:T(8,128)(2,1)}, bf16[96,320]{1,0:T(8,128)(2,1)}, u32[]{:S(2)}, u32[]{:S(2)}) collective-permute-start(bf16[96,320]{1,0:T(8,128)(2,1)} %get-tuple-element.1446), channel_id=1, source_target_pairs={{0,1},{1,2},{2,3},{3,4},{4,5},{6,7},{7,8},{8,9},{9,10},{10,11},{12... | collective-permute-start | bytes 184328 | tf_op jit(solution)/shard_map/while/body/eval_jaxpr/ppermute | solution.py:15
  375.8 9.6 %collective-permute-start.3 = (bf16[96,320]{1,0:T(8,128)(2,1)S(1)}, bf16[96,320]{1,0:T(8,128)(2,1)S(1)}, u32[]{:S(2)}, u32[]{:S(2)}) collective-permute-start(bf16[96,320]{1,0:T(8,128)(2,1)S(1)} %get-tuple-element.1461), channel_id=1, source_target_pairs={{1,0},{2,1},{3,2},{4,3},{5,4},{7,6},{8,7},{9,8},{10,9},{11,10},{13... | collective-permute-start | bytes 184328 | tf_op jit(solution)/shard_map/while/body/eval_jaxpr/ppermute | solution.py:15
  386.5 9.6 %collective-permute-start.3 = (bf16[96,320]{1,0:T(8,128)(2,1)S(1)}, bf16[96,320]{1,0:T(8,128)(2,1)S(1)}, u32[]{:S(2)}, u32[]{:S(2)}) collective-permute-start(bf16[96,320]{1,0:T(8,128)(2,1)S(1)} %get-tuple-element.1461), channel_id=1, source_target_pairs={{1,0},{2,1},{3,2},{4,3},{5,4},{7,6},{8,7},{9,8},{10,9},{11,10},{13... | collective-permute-start | bytes 184328 | tf_op jit(solution)/shard_map/while/body/eval_jaxpr/ppermute | solution.py:15
  397.2 9.6 %collective-permute-start.3 = (bf16[96,320]{1,0:T(8,128)(2,1)S(1)}, bf16[96,320]{1,0:T(8,128)(2,1)S(1)}, u32[]{:S(2)}, u32[]{:S(2)}) collective-permute-start(bf16[96,320]{1,0:T(8,128)(2,1)S(1)} %get-tuple-element.1461), channel_id=1, source_target_pairs={{1,0},{2,1},{3,2},{4,3},{5,4},{7,6},{8,7},{9,8},{10,9},{11,10},{13... | collective-permute-start | bytes 184328 | tf_op jit(solution)/shard_map/while/body/eval_jaxpr/ppermute | solution.py:15
  407.9 11.8 %collective-permute-start.3 = (bf16[96,320]{1,0:T(8,128)(2,1)S(1)}, bf16[96,320]{1,0:T(8,128)(2,1)S(1)}, u32[]{:S(2)}, u32[]{:S(2)}) collective-permute-start(bf16[96,320]{1,0:T(8,128)(2,1)S(1)} %get-tuple-element.1461), channel_id=1, source_target_pairs={{1,0},{2,1},{3,2},{4,3},{5,4},{7,6},{8,7},{9,8},{10,9},{11,10},{13... | collective-permute-start | bytes 184328 | tf_op jit(solution)/shard_map/while/body/eval_jaxpr/ppermute | solution.py:15
  424.5 9.6 %collective-permute-start.3 = (bf16[96,320]{1,0:T(8,128)(2,1)S(1)}, bf16[96,320]{1,0:T(8,128)(2,1)S(1)}, u32[]{:S(2)}, u32[]{:S(2)}) collective-permute-start(bf16[96,320]{1,0:T(8,128)(2,1)S(1)} %get-tuple-element.1461), channel_id=1, source_target_pairs={{1,0},{2,1},{3,2},{4,3},{5,4},{7,6},{8,7},{9,8},{10,9},{11,10},{13... | collective-permute-start | bytes 184328 | tf_op jit(solution)/shard_map/while/body/eval_jaxpr/ppermute | solution.py:15
  439.0 9.6 %collective-permute-start.3 = (bf16[96,320]{1,0:T(8,128)(2,1)S(1)}, bf16[96,320]{1,0:T(8,128)(2,1)S(1)}, u32[]{:S(2)}, u32[]{:S(2)}) collective-permute-start(bf16[96,320]{1,0:T(8,128)(2,1)S(1)} %get-tuple-element.1461), channel_id=1, source_target_pairs={{1,0},{2,1},{3,2},{4,3},{5,4},{7,6},{8,7},{9,8},{10,9},{11,10},{13... | collective-permute-start | bytes 184328 | tf_op jit(solution)/shard_map/while/body/eval_jaxpr/ppermute | solution.py:15
  453.4 9.6 %collective-permute-start.3 = (bf16[96,320]{1,0:T(8,128)(2,1)S(1)}, bf16[96,320]{1,0:T(8,128)(2,1)S(1)}, u32[]{:S(2)}, u32[]{:S(2)}) collective-permute-start(bf16[96,320]{1,0:T(8,128)(2,1)S(1)} %get-tuple-element.1461), channel_id=1, source_target_pairs={{1,0},{2,1},{3,2},{4,3},{5,4},{7,6},{8,7},{9,8},{10,9},{11,10},{13... | collective-permute-start | bytes 184328 | tf_op jit(solution)/shard_map/while/body/eval_jaxpr/ppermute | solution.py:15
  467.9 9.6 %collective-permute-start.3 = (bf16[96,320]{1,0:T(8,128)(2,1)S(1)}, bf16[96,320]{1,0:T(8,128)(2,1)S(1)}, u32[]{:S(2)}, u32[]{:S(2)}) collective-permute-start(bf16[96,320]{1,0:T(8,128)(2,1)S(1)} %get-tuple-element.1461), channel_id=1, source_target_pairs={{1,0},{2,1},{3,2},{4,3},{5,4},{7,6},{8,7},{9,8},{10,9},{11,10},{13... | collective-permute-start | bytes 184328 | tf_op jit(solution)/shard_map/while/body/eval_jaxpr/ppermute | solution.py:15
  478.6 9.6 %collective-permute-start.3 = (bf16[96,320]{1,0:T(8,128)(2,1)S(1)}, bf16[96,320]{1,0:T(8,128)(2,1)S(1)}, u32[]{:S(2)}, u32[]{:S(2)}) collective-permute-start(bf16[96,320]{1,0:T(8,128)(2,1)S(1)} %get-tuple-element.1461), channel_id=1, source_target_pairs={{1,0},{2,1},{3,2},{4,3},{5,4},{7,6},{8,7},{9,8},{10,9},{11,10},{13... | collective-permute-start | bytes 184328 | tf_op jit(solution)/shard_map/while/body/eval_jaxpr/ppermute | solution.py:15
  488.2 3.0 copy-start.3
  488.2 3.0 copy-start.4
  494.2 103.8 %reduce-scatter.6.cloned.1.call-start = ((), (), s32[]{:S(2)}) async-start(), calls=%async_computation.4 | async-start | bytes 983040 | tf_op jit(solution)/shard_map/reduce_scatter | solution.py:125
  564.5 73.9 %reduce-scatter.8.cloned.1.call-start = ((), (), s32[]{:S(2)}) async-start(), calls=%async_computation.5 | async-start | bytes 221184 | tf_op jit(solution)/shard_map/reduce_scatter | solution.py:125
  598.0 156.1 %all-gather.2.cloned.1.call-start = ((), (), s32[]{:S(2)}) async-start(), calls=%async_computation.6 | async-start | bytes 3932160 | tf_op jit(solution)/shard_map/all_gather | solution.py:127
Sparse Core Ops, SparseCore 0:
  494.3 70.1 reduce-scatter.3
  567.7 30.3 reduce-scatter.5
  601.1 37.3 reduce-scatter.7
  669.2 84.8 all-gather.1

commit v2 on v1

v2 whole, which is shorter than its diff:
```python
import math

import jax
import jax.numpy as jnp
from jax import lax
from jax.sharding import Mesh, PartitionSpec as P

DP = ("y", "x", "zl")
SCATTER = ("y", "x", "zl")


def rows_product(left, right):
    return lax.dot_general(
        left, right, (((0,), (0,)), ((), ())), preferred_element_type=jnp.float32
    )


def times_transposed(left, right):
    return lax.dot_general(
        left, right, (((1,), (1,)), ((), ())), preferred_element_type=jnp.float32
    )


def rms_scale(values):
    return lax.rsqrt(jnp.mean(values * values, axis=-1, keepdims=True) + 1e-05)


def silu_slope(values):
    sigma = jax.nn.sigmoid(values)
    return sigma * (1.0 + values * (1.0 - sigma))


def embed(moment, width):
    half = width // 2
    freq = jnp.exp(-math.log(10000.0) * jnp.arange(half, dtype=jnp.float32) / half)
    angle = moment[:, None] * freq[None, :]
    return jnp.concatenate([jnp.sin(angle), jnp.cos(angle)], axis=-1)


def down_forward(hidden, embedding, in_matrix, out_matrix):
    lifted = hidden.astype(jnp.float32) + embedding
    normed = lifted * rms_scale(lifted)
    inner = jnp.dot(normed.astype(jnp.bfloat16), in_matrix, preferred_element_type=jnp.float32)
    gated = jax.nn.silu(inner).astype(jnp.bfloat16)
    return (lifted + jnp.dot(gated, out_matrix, preferred_element_type=jnp.float32)).astype(
        jnp.bfloat16
    )


def down_backward(hidden, embedding, in_matrix, out_matrix, cotan):
    lifted = hidden.astype(jnp.float32) + embedding
    scale = rms_scale(lifted)
    normed = lifted * scale
    normed_b = normed.astype(jnp.bfloat16)
    inner = jnp.dot(normed_b, in_matrix, preferred_element_type=jnp.float32)
    gated = jax.nn.silu(inner).astype(jnp.bfloat16)
    grad_out = rows_product(gated, cotan)
    d_gated = times_transposed(cotan, out_matrix)
    d_inner = (d_gated * silu_slope(inner)).astype(jnp.bfloat16)
    grad_in = rows_product(normed_b, d_inner)
    d_normed = times_transposed(d_inner, in_matrix)
    d_lifted = cotan.astype(jnp.float32) + scale * (
        d_normed - normed * jnp.mean(d_normed * normed, axis=-1, keepdims=True)
    )
    return (d_lifted.astype(jnp.bfloat16), grad_in, grad_out)


def up_forward(below, side, mix_matrix, up_matrix):
    joined = jnp.concatenate([below, side], axis=-1)
    mixed = jnp.dot(joined, mix_matrix, preferred_element_type=jnp.float32)
    normed = mixed * rms_scale(mixed)
    active = jax.nn.silu(normed).astype(jnp.bfloat16)
    return (mixed + jnp.dot(active, up_matrix, preferred_element_type=jnp.float32)).astype(
        jnp.bfloat16
    )


def up_backward(below, side, mix_matrix, up_matrix, cotan):
    width = below.shape[-1]
    joined = jnp.concatenate([below, side], axis=-1)
    mixed = jnp.dot(joined, mix_matrix, preferred_element_type=jnp.float32)
    scale = rms_scale(mixed)
    normed = mixed * scale
    active = jax.nn.silu(normed).astype(jnp.bfloat16)
    grad_up = rows_product(active, cotan)
    d_active = times_transposed(cotan, up_matrix)
    d_normed = d_active * silu_slope(normed)
    d_mixed = (
        cotan.astype(jnp.float32)
        + scale * (d_normed - normed * jnp.mean(d_normed * normed, axis=-1, keepdims=True))
    ).astype(jnp.bfloat16)
    grad_mix = rows_product(joined, d_mixed)
    d_joined = times_transposed(d_mixed, mix_matrix)
    return (d_joined[:, :width].astype(jnp.bfloat16), d_joined[:, width:], grad_mix, grad_up)


def reduce_replicas(parts):
    total = sum(part.size for part in parts)
    groups = math.prod(lax.axis_size(name) for name in DP)
    lanes = 128
    length = -(-total // (lanes * groups * 8)) * groups * 8
    flat = jnp.concatenate([part.reshape(-1) for part in parts])
    flat = jnp.pad(flat, (0, length * lanes - total)).reshape(length, lanes)
    for name in SCATTER:
        flat = lax.psum_scatter(flat, name, scatter_dimension=0, tiled=True)
    for name in reversed(SCATTER):
        flat = lax.all_gather(flat, name, axis=0, tiled=True)
    flat = flat.reshape(-1)
    out, start = [], 0
    for part in parts:
        out.append(flat[start : start + part.size].reshape(part.shape))
        start += part.size
    return tuple(out)


def dp_split(mesh):
    column = mesh.devices[:, 0]
    sizes = [len({int(device.coords[axis]) for device in column}) for axis in (1, 0, 2)]
    if math.prod(sizes) != column.size:
        raise ValueError("dp split")
    return tuple(sizes)


def swap_core(value):
    return lax.ppermute(value, "core", [(0, 1), (1, 0)])


def hop(value, source, target):
    return lax.ppermute(value, "zh", [(source, target)])


def keep(valid, new, old):
    return new if old is None else jnp.where(valid, new, old)


def local(latents, clip_of_row, timestep, w_in, w_out, w_mix, w_up, out_grad):
    stages = lax.axis_size("zh")
    stage = lax.axis_index("zh")
    core = lax.axis_index("core")
    first = core == 0
    width = latents.shape[1]
    rows = latents.shape[0] // lax.axis_size("core")

    def pair(weights):
        own = weights[0]
        other = swap_core(own)
        return (jnp.where(first, own, other), jnp.where(first, other, own))

    in_pair, out_pair = pair(w_in), pair(w_out)
    mix_pair, up_pair = pair(w_mix), pair(w_up)

    offset = core * rows
    match = clip_of_row[0][:, None] == jnp.arange(timestep.shape[1], dtype=jnp.int32)[None, :]
    moment = jnp.sum(jnp.where(match, timestep[0][None, :], 0), axis=1).astype(jnp.float32)
    moment = lax.dynamic_slice_in_dim(moment, offset, rows)
    embedding = embed(moment, width)
    source = lax.dynamic_slice_in_dim(latents, offset, rows)
    seed = lax.dynamic_slice_in_dim(out_grad, offset, rows)

    down_in = [None, None]
    skip = [None, None]
    hidden = source
    for tick in range(stages):
        if tick > 0:
            hidden = hop(hidden, tick - 1, tick)
        valid = stage == tick
        lower = hidden
        upper = down_forward(lower, embedding, in_pair[0], out_pair[0])
        hidden = down_forward(upper, embedding, in_pair[1], out_pair[1])
        down_in = [keep(valid, lower, down_in[0]), keep(valid, upper, down_in[1])]
        skip = [keep(valid, upper, skip[0]), keep(valid, hidden, skip[1])]

    up_in = [None, None]
    below = skip[1]
    for tick in range(stages):
        owner = stages - 1 - tick
        if tick > 0:
            below = hop(below, owner + 1, owner)
        valid = stage == owner
        middle = up_forward(below, skip[1], mix_pair[1], up_pair[1])
        up_in = [keep(valid, middle, up_in[0]), keep(valid, below, up_in[1])]
        below = up_forward(middle, skip[0], mix_pair[0], up_pair[0])

    d_skip = [None, None]
    grad_mix = [None, None]
    grad_up = [None, None]
    cotan = seed
    for tick in range(stages):
        if tick > 0:
            cotan = hop(cotan, tick - 1, tick)
        valid = stage == tick
        middle, side0, mix0, up0 = up_backward(up_in[0], skip[0], mix_pair[0], up_pair[0], cotan)
        cotan, side1, mix1, up1 = up_backward(up_in[1], skip[1], mix_pair[1], up_pair[1], middle)
        d_skip = [keep(valid, side0, d_skip[0]), keep(valid, side1, d_skip[1])]
        grad_mix = [keep(valid, mix0, grad_mix[0]), keep(valid, mix1, grad_mix[1])]
        grad_up = [keep(valid, up0, grad_up[0]), keep(valid, up1, grad_up[1])]

    def combine(grads):
        mine = jnp.where(first, grads[0], grads[1])
        theirs = jnp.where(first, grads[1], grads[0])
        return mine + swap_core(theirs)

    factor = 1.0 / math.prod(lax.axis_size(name) for name in DP)
    total_mix, total_up = reduce_replicas((combine(grad_mix), combine(grad_up)))

    grad_in = [None, None]
    grad_out = [None, None]
    carry = cotan
    for tick in range(stages):
        owner = stages - 1 - tick
        if tick > 0:
            carry = hop(carry, owner + 1, owner)
        valid = stage == owner
        upper_c = (d_skip[1] + carry.astype(jnp.float32)).astype(jnp.bfloat16)
        upper_d, in1, out1 = down_backward(down_in[1], embedding, in_pair[1], out_pair[1], upper_c)
        lower_c = (d_skip[0] + upper_d.astype(jnp.float32)).astype(jnp.bfloat16)
        carry, in0, out0 = down_backward(down_in[0], embedding, in_pair[0], out_pair[0], lower_c)
        grad_in = [keep(valid, in0, grad_in[0]), keep(valid, in1, grad_in[1])]
        grad_out = [keep(valid, out0, grad_out[0]), keep(valid, out1, grad_out[1])]

    total_in, total_out = reduce_replicas((combine(grad_in), combine(grad_out)))
    return (
        (total_in * factor)[None],
        (total_out * factor)[None],
        (total_mix * factor)[None],
        (total_up * factor)[None],
    )


def solution(mesh):
    sizes = dp_split(mesh)
    pipe = mesh.devices.shape[1]
    split = Mesh(mesh.devices.reshape(*sizes, pipe // 2, 2), DP + ("zh", "core"))
    sections = ("zh", "core")
    return jax.shard_map(
        local,
        mesh=split,
        in_specs=(
            P(DP, None),
            P(DP, None),
            P(DP, None),
            P(sections, None, None),
            P(sections, None, None),
            P(sections, None, None),
            P(sections, None, None),
            P(DP, None),
        ),
        out_specs=(
            P(sections, None, None),
            P(sections, None, None),
            P(sections, None, None),
            P(sections, None, None),
        ),
        check_vma=False,
    )
```

time: 774 us -> 476 us (0.61)
  the two profiles are of different devices: /device:TPU:1 before, /device:TPU:2 now
where the time goes in v2:
time: 476 us; the launch traced here: 475 us
  waiting for transfers between devices  304 us (64%)
  blocking collectives  52.4 us (11%)
  matrix products  37.4 us (8%)
  starting transfers between devices  35.9 us (8%)
  other arithmetic  18.5 us (4%)
  between operations  15.3 us (3%)
  local copies, waits for them, and re-layouts  11 us (2%)
    reduce_scatter x5, waiting for transfers between devices, reduce_replicas(): flat = lax.psum_scatter(flat, name, scatter_dimension=0, tiled=True)  153 us
    all_gather x2, waiting for transfers between devices, reduce_replicas(): flat = lax.all_gather(flat, name, axis=0, tiled=True)  63.1 us
    ppermute x8, waiting for transfers between devices, hop(): return lax.ppermute(value, 'zh', [(source, target)])  52.8 us
    all_gather x4, blocking collectives, reduce_replicas(): flat = lax.all_gather(flat, name, axis=0, tiled=True)  52.4 us
    unnamed x9, waiting for transfers between devices  33.3 us
    ppermute x8, starting transfers between devices, hop(): return lax.ppermute(value, 'zh', [(source, target)])  18 us
    ppermute x8, starting transfers between devices, swap_core(): return lax.ppermute(value, 'core', [(0, 1), (1, 0)])  17.6 us
    dot_general x24, matrix products, rows_product(): lax.dot_general(left, right, (((0,), (0,)), ((), ())), preferred_element_...  16.1 us
  transfers between devices with their start and end apart: 24, of which 13 were waited for; matrix products, arithmetic and copies ran while one was open for 8% of the time, Pallas kernels for 0%

profile of v2, /device:TPU:2, one launch (start us, length us, event | category | flops | bytes accessed | tf_op | source)
XLA Modules:
  0.0 474.8 jit_solution(14703041180477426190)
XLA Ops:
  7.2 2.1 collective-permute-start
  9.3 2.4 collective-permute-start.1
  11.7 1.9 collective-permute-start.4
  13.6 2.4 collective-permute-start.5
  16.1 1.2 constant_dynamic-slice_fusion
  22.7 10.9 %collective-permute-start.2 = (bf16[192,320]{1,0:T(8,128)(2,1)S(1)}, bf16[192,320]{1,0:T(8,128)(2,1)S(1)}, u32[]{:S(2)}, u32[]{:S(2)}) collective-permute-start(bf16[192,320]{1,0:T(8,128)(2,1)S(1)} %fusion.10), channel_id=1, source_target_pairs={{0,2},{1,3},{6,8},{7,9},{12,14},{13,15},{18,20},{19,21},{24,26},{2... | collective-permute-start | bytes 368648 | tf_op jit(solution)/shard_map/ppermute | solution.py:129
  33.6 1.7 broadcast_select_fusion.10
  35.3 1.5 collective-permute-done.2
  38.3 1.6 fusion.12
  42.0 2.4 multiply_reduce_fusion.5
  44.4 1.6 fusion.21
  50.7 1.3 collective-permute-start.7
  52.3 26.5 %collective-permute-done.7 = bf16[192,320]{1,0:T(8,128)(2,1)S(1)} collective-permute-done((bf16[192,320]{1,0:T(8,128)(2,1)S(1)}, bf16[192,320]{1,0:T(8,128)(2,1)S(1)}, u32[]{:S(2)}, u32[]{:S(2)}) %collective-permute-start.7) | collective-permute-done | bytes 122912 | tf_op jit(solution)/shard_map/ppermute | solution.py:129
  83.3 1.6 collective-permute-start.8
  85.3 2.1 collective-permute-done.8
  94.9 1.6 broadcast_select_fusion
  96.5 1.9 collective-permute-start.14
  101.6 2.4 collective-permute-start.15
  106.8 1.2 convolution_select_fusion.8
  108.2 1.5 collective-permute-start.11
  109.7 1.3 convolution_select_fusion.4
  111.0 1.3 convolution_select_fusion.6
  112.3 1.2 convolution_select_fusion.10
  113.5 22.6 %collective-permute-done.11 = bf16[192,320]{1,0:T(8,128)(2,1)S(1)} collective-permute-done((bf16[192,320]{1,0:T(8,128)(2,1)S(1)}, bf16[192,320]{1,0:T(8,128)(2,1)S(1)}, u32[]{:S(2)}, u32[]{:S(2)}) %collective-permute-start.11) | collective-permute-done | bytes 122912 | tf_op jit(solution)/shard_map/ppermute | solution.py:129
  137.9 1.3 select_add_fusion
  140.1 1.2 fusion.1
  142.4 1.6 convolution_select_fusion.11
  144.4 2.1 collective-permute-start.12
  147.0 1.6 broadcast_select_fusion.1
  148.5 2.4 collective-permute-start.13
  151.1 2.1 collective-permute-done.13
  153.2 1.3 select_add_fusion.1
  155.3 1.5 fusion
  156.9 35.4 %reduce-scatter.16.cloned.1.call-done = f32[384,128]{1,0:T(8,128)} async-done(((f32[3072,128]{1,0:T(8,128)}), f32[384,128]{1,0:T(8,128)}) %reduce-scatter.16.cloned.1.call-update) | async-done | bytes 196624 | tf_op jit(solution)/shard_map/reduce_scatter | solution.py:105
  192.3 49.6 %reduce-scatter.10.cloned.1.call-done = f32[512,128]{1,0:T(8,128)} async-done(((f32[4096,128]{1,0:T(8,128)}), f32[512,128]{1,0:T(8,128)}) %reduce-scatter.10.cloned.1.call-update) | async-done | bytes 262160 | tf_op jit(solution)/shard_map/reduce_scatter | solution.py:105
  242.0 30.5 %reduce-scatter.18.cloned.1.call-done = f32[96,128]{1,0:T(8,128)} async-done(((f32[384,128]{1,0:T(8,128)}), f32[96,128]{1,0:T(8,128)}) %reduce-scatter.18.cloned.1.call-update) | async-done | bytes 49168 | tf_op jit(solution)/shard_map/reduce_scatter | solution.py:105
  272.5 31.7 %reduce-scatter.12.cloned.1.call-done = f32[128,128]{1,0:T(8,128)} async-done(((f32[512,128]{1,0:T(8,128)}), f32[128,128]{1,0:T(8,128)}) %reduce-scatter.12.cloned.1.call-update) | async-done | bytes 65552 | tf_op jit(solution)/shard_map/reduce_scatter | solution.py:105
  304.3 33.2 %reduce-scatter.20.cloned.1.call-done = f32[24,128]{1,0:T(8,128)} async-done(((f32[96,128]{1,0:T(8,128)}), f32[24,128]{1,0:T(8,128)}) %reduce-scatter.20.cloned.1.call-update) | async-done | bytes 12304
  337.4 13.3 %all_gather.21 = f32[96,128]{1,0:T(8,128)S(1)} all-gather(f32[24,128]{1,0:T(8,128)} %reduce-scatter.20.cloned.1.call-done), channel_id=1, replica_groups=mesh['y'=8,'x'=4,'zl'=4,'zh'=3,'core'=2] {'zl'}, dimensions={0}, use_global_device_ids=true | all-gather | bytes 61440 | tf_op jit(solution)/shard_map/all_gather | solution.py:107
  350.7 12.8 %all_gather.22 = f32[384,128]{1,0:T(8,128)} all-gather(f32[96,128]{1,0:T(8,128)S(1)} %all_gather.21), channel_id=1, replica_groups=mesh['y'=8,'x'=4,'zl'=4,'zh'=3,'core'=2] {'x'}, dimensions={0}, use_global_device_ids=true | all-gather | bytes 245760 | tf_op jit(solution)/shard_map/all_gather | solution.py:107
  363.6 6.1 %reduce-scatter.14.cloned.1.call-done = f32[32,128]{1,0:T(8,128)} async-done(((f32[128,128]{1,0:T(8,128)}), f32[32,128]{1,0:T(8,128)}) %reduce-scatter.14.cloned.1.call-update) | async-done | bytes 16400 | tf_op jit(solution)/shard_map/reduce_scatter | solution.py:105
  369.7 13.3 %all_gather.18 = f32[128,128]{1,0:T(8,128)S(1)} all-gather(f32[32,128]{1,0:T(8,128)} %reduce-scatter.14.cloned.1.call-done), channel_id=1, replica_groups=mesh['y'=8,'x'=4,'zl'=4,'zh'=3,'core'=2] {'zl'}, dimensions={0}, use_global_device_ids=true | all-gather | bytes 81920 | tf_op jit(solution)/shard_map/all_gather | solution.py:107
  383.0 13.0 %all_gather.19 = f32[512,128]{1,0:T(8,128)} all-gather(f32[128,128]{1,0:T(8,128)S(1)} %all_gather.18), channel_id=1, replica_groups=mesh['y'=8,'x'=4,'zl'=4,'zh'=3,'core'=2] {'x'}, dimensions={0}, use_global_device_ids=true | all-gather | bytes 327680 | tf_op jit(solution)/shard_map/all_gather | solution.py:107
  396.0 20.2 %all-gather.5.cloned.1.call-done = f32[3072,128]{1,0:T(8,128)} async-done(((f32[384,128]{1,0:T(8,128)}), f32[3072,128]{1,0:T(8,128)}) %all-gather.5.cloned.1.call-update) | async-done | bytes 1572880 | tf_op jit(solution)/shard_map/all_gather | solution.py:107
  417.8 1.2 copy.31
  421.0 42.9 %all-gather.3.cloned.1.call-done = f32[4096,128]{1,0:T(8,128)} async-done(((f32[512,128]{1,0:T(8,128)}), f32[4096,128]{1,0:T(8,128)}) %all-gather.3.cloned.1.call-update) | async-done | bytes 2097168 | tf_op jit(solution)/shard_map/all_gather | solution.py:107
  463.9 1.5 slice_multiply_fusion.1
  465.7 1.2 copy.30
  (212 shorter events, 42.4 us)
Async XLA Ops:
  7.2 13.0 %copy-start.11 = (bf16[1,320,640]{2,1,0:T(8,128)(2,1)S(1)}, bf16[1,320,640]{2,1,0:T(8,128)(2,1)}, u32[]{:S(2)}) copy-start(bf16[1,320,640]{2,1,0:T(8,128)(2,1)} %param.11) | copy-start | bytes 1228804
  7.2 185.1 %reduce-scatter.16.cloned.1.call-start = ((), (), s32[]{:S(2)}) async-start(), calls=%async_computation.10 | async-start | bytes 1769472 | tf_op jit(solution)/shard_map/reduce_scatter | solution.py:105
  7.2 12.9 %collective-permute-start = (bf16[320,640]{1,0:T(8,128)(2,1)}, bf16[320,640]{1,0:T(8,128)(2,1)S(1)}, u32[]{:S(2)}, u32[]{:S(2)}) collective-permute-start(bf16[320,640]{1,0:T(8,128)(2,1)} %bitcast.118), channel_id=1, source_target_pairs={{0,1},{1,0},{2,3},{3,2},{4,5},{5,4},{6,7},{7,6},{8,9},{9,8},{10,11... | collective-permute-start | bytes 1228808 | tf_op jit(solution)/shard_map/ppermute | solution.py:125
  9.3 11.0 %collective-permute-start.1 = (bf16[640,320]{0,1:T(8,128)(2,1)}, bf16[640,320]{0,1:T(8,128)(2,1)}, u32[]{:S(2)}, u32[]{:S(2)}) collective-permute-start(bf16[640,320]{0,1:T(8,128)(2,1)} %bitcast.119), channel_id=1, source_target_pairs={{0,1},{1,0},{2,3},{3,2},{4,5},{5,4},{6,7},{7,6},{8,9},{9,8},{10,11... | collective-permute-start | bytes 1228808 | tf_op jit(solution)/shard_map/ppermute | solution.py:125
  11.7 29.0 %collective-permute-start.4 = (bf16[640,320]{0,1:T(8,128)(2,1)}, bf16[640,320]{0,1:T(8,128)(2,1)}, u32[]{:S(2)}, u32[]{:S(2)}) collective-permute-start(bf16[640,320]{0,1:T(8,128)(2,1)} %bitcast.120), channel_id=1, source_target_pairs={{0,1},{1,0},{2,3},{3,2},{4,5},{5,4},{6,7},{7,6},{8,9},{9,8},{10,11... | collective-permute-start | bytes 1228808 | tf_op jit(solution)/shard_map/ppermute | solution.py:125
  13.6 20.0 %collective-permute-start.5 = (bf16[320,320]{1,0:T(8,128)(2,1)}, bf16[320,320]{1,0:T(8,128)(2,1)}, u32[]{:S(2)}, u32[]{:S(2)}) collective-permute-start(bf16[320,320]{1,0:T(8,128)(2,1)} %bitcast.121), channel_id=1, source_target_pairs={{0,1},{1,0},{2,3},{3,2},{4,5},{5,4},{6,7},{7,6},{8,9},{9,8},{10,11... | collective-permute-start | bytes 614408 | tf_op jit(solution)/shard_map/ppermute | solution.py:125
  19.0 1.3 copy-start.12
  21.3 0.8 copy-start.16
  21.4 15.6 %copy-start.14 = (bf16[640,320]{0,1:T(8,128)(2,1)}, bf16[640,320]{0,1:T(8,128)(2,1)S(1)}, u32[]{:S(2)}) copy-start(bf16[640,320]{0,1:T(8,128)(2,1)S(1)} %get-tuple-element.36) | copy-start | bytes 1228804
  22.1 11.5 %copy-start.19 = (bf16[1,320,320]{2,1,0:T(8,128)(2,1)S(1)}, bf16[1,320,320]{2,1,0:T(8,128)(2,1)}, u32[]{:S(2)}) copy-start(bf16[1,320,320]{2,1,0:T(8,128)(2,1)} %param.14) | copy-start | bytes 614404
  22.7 12.6 %copy-start.21 = (bf16[192,320]{1,0:T(8,128)(2,1)}, bf16[192,320]{1,0:T(8,128)(2,1)S(1)}, u32[]{:S(2)}) copy-start(bf16[192,320]{1,0:T(8,128)(2,1)S(1)} %fusion.10) | copy-start | bytes 368644
  22.7 14.1 %collective-permute-start.2 = (bf16[192,320]{1,0:T(8,128)(2,1)S(1)}, bf16[192,320]{1,0:T(8,128)(2,1)S(1)}, u32[]{:S(2)}, u32[]{:S(2)}) collective-permute-start(bf16[192,320]{1,0:T(8,128)(2,1)S(1)} %fusion.10), channel_id=1, source_target_pairs={{0,2},{1,3},{6,8},{7,9},{12,14},{13,15},{18,20},{19,21},{24,26},{2... | collective-permute-start | bytes 368648 | tf_op jit(solution)/shard_map/ppermute | solution.py:129
  38.3 2.3 copy-start.13
  40.0 2.0 copy-start.22
  40.0 1.8 collective-permute-start.3
  42.0 2.4 copy-start.17
  46.5 1.0 copy-start.20
  47.8 1.2 collective-permute-start.6
  48.9 87.3 %copy-start.5 = (f32[192,640]{1,0:T(8,128)}, f32[192,640]{1,0:T(8,128)S(1)}, u32[]{:S(2)}) copy-start(f32[192,640]{1,0:T(8,128)S(1)} %fusion.104) | copy-start | bytes 1474564
  49.0 63.3 %copy-start.3 = (bf16[192,320]{1,0:T(8,128)(2,1)}, bf16[192,320]{1,0:T(8,128)(2,1)S(1)}, u32[]{:S(2)}) copy-start(bf16[192,320]{1,0:T(8,128)(2,1)S(1)} %multiply_convert_fusion.32) | copy-start | bytes 368644
  50.7 28.1 %collective-permute-start.7 = (bf16[192,320]{1,0:T(8,128)(2,1)S(1)}, bf16[192,320]{1,0:T(8,128)(2,1)S(1)}, u32[]{:S(2)}, u32[]{:S(2)}) collective-permute-start(bf16[192,320]{1,0:T(8,128)(2,1)S(1)} %fusion.18), channel_id=1, source_target_pairs={{2,0},{3,1},{8,6},{9,7},{14,12},{15,13},{20,18},{21,19},{26,24},{2... | collective-permute-start | bytes 368648 | tf_op jit(solution)/shard_map/ppermute | solution.py:129
  52.3 58.7 %copy-start.9 = (f32[192,640]{1,0:T(8,128)}, f32[192,640]{1,0:T(8,128)S(1)}, u32[]{:S(2)}) copy-start(f32[192,640]{1,0:T(8,128)S(1)} %fusion.105) | copy-start | bytes 1474564
  83.3 4.1 collective-permute-start.8
  89.9 1.4 collective-permute-start.9
  92.8 1.0 copy-start.18
  96.5 41.5 %collective-permute-start.14 = (f32[640,320]{0,1:T(8,128)}, f32[640,320]{0,1:T(8,128)}, u32[]{:S(2)}, u32[]{:S(2)}) collective-permute-start(f32[640,320]{0,1:T(8,128)} %get-tuple-element.90), channel_id=1, source_target_pairs={{0,1},{1,0},{2,3},{3,2},{4,5},{5,4},{6,7},{7,6},{8,9},{9,8},{10,11... | collective-permute-start | bytes 2457608 | tf_op jit(solution)/shard_map/ppermute | solution.py:125
  98.4 1.0 copy-start.15
  100.3 3.8 collective-permute-start.10
  101.6 35.9 %collective-permute-start.15 = (f32[320,320]{1,0:T(8,128)S(1)}, f32[320,320]{1,0:T(8,128)S(1)}, u32[]{:S(2)}, u32[]{:S(2)}) collective-permute-start(f32[320,320]{1,0:T(8,128)S(1)} %get-tuple-element.88), channel_id=1, source_target_pairs={{0,1},{1,0},{2,3},{3,2},{4,5},{5,4},{6,7},{7,6},{8,9},{9,8},{10,11... | collective-permute-start | bytes 1228808 | tf_op jit(solution)/shard_map/ppermute | solution.py:125
  108.2 28.0 %collective-permute-start.11 = (bf16[192,320]{1,0:T(8,128)(2,1)S(1)}, bf16[192,320]{1,0:T(8,128)(2,1)S(1)}, u32[]{:S(2)}, u32[]{:S(2)}) collective-permute-start(bf16[192,320]{1,0:T(8,128)(2,1)S(1)} %add_convert_fusion.3), channel_id=1, source_target_pairs={{2,0},{3,1},{8,6},{9,7},{14,12},{15,13},{20,18},{21,19},{26,24},{2... | collective-permute-start | bytes 368648 | tf_op jit(solution)/shard_map/ppermute | solution.py:129
  140.1 1.3 copy-start.7
  141.3 0.9 copy-start.4
  141.3 1.1 copy-start.10
  141.3 100.5 %reduce-scatter.10.cloned.1.call-start = ((), (), s32[]{:S(2)}) async-start(), calls=%async_computation.6 | async-start | bytes 2359296 | tf_op jit(solution)/shard_map/reduce_scatter | solution.py:105
  142.4 1.6 copy-start
  144.1 2.4 copy-start.23
  144.4 2.5 copy-start.6
  144.4 2.5 copy-start.8
  144.4 6.5 %collective-permute-start.12 = (f32[320,640]{1,0:T(8,128)S(1)}, f32[320,640]{1,0:T(8,128)S(1)}, u32[]{:S(2)}, u32[]{:S(2)}) collective-permute-start(f32[320,640]{1,0:T(8,128)S(1)} %get-tuple-element.86), channel_id=1, source_target_pairs={{0,1},{1,0},{2,3},{3,2},{4,5},{5,4},{6,7},{7,6},{8,9},{9,8},{10,11... | collective-permute-start | bytes 2457608 | tf_op jit(solution)/shard_map/ppermute | solution.py:125
  146.9 1.6 copy-start.1
  148.5 4.7 collective-permute-start.13
  151.1 2.1 copy-start.2
  156.8 115.6 %reduce-scatter.18.cloned.1.call-start = ((), (), s32[]{:S(2)}) async-start(), calls=%async_computation.11 | async-start | bytes 245760 | tf_op jit(solution)/shard_map/reduce_scatter | solution.py:105
  192.3 112.0 %reduce-scatter.12.cloned.1.call-start = ((), (), s32[]{:S(2)}) async-start(), calls=%async_computation.7 | async-start | bytes 327680 | tf_op jit(solution)/shard_map/reduce_scatter | solution.py:105
  241.9 95.5 %reduce-scatter.20.cloned.1.call-start = ((), (), s32[]{:S(2)}) async-start(), calls=%async_computation.13 | async-start | bytes 61440
  272.5 97.2 %reduce-scatter.14.cloned.1.call-start = ((), (), s32[]{:S(2)}) async-start(), calls=%async_computation.8 | async-start | bytes 81920 | tf_op jit(solution)/shard_map/reduce_scatter | solution.py:105
  304.2 112.0 %all-gather.5.cloned.1.call-start = ((), (), s32[]{:S(2)}) async-start(), calls=%async_computation.12 | async-start | bytes 1769472 | tf_op jit(solution)/shard_map/all_gather | solution.py:107
  363.6 100.3 %all-gather.3.cloned.1.call-start = ((), (), s32[]{:S(2)}) async-start(), calls=%async_computation.9 | async-start | bytes 2359296 | tf_op jit(solution)/shard_map/all_gather | solution.py:107
  (2 other events, 1.3 us)
Sparse Core Ops, SparseCore 0:
  141.5 50.7 reduce-scatter.15
  195.4 46.4 reduce-scatter.9
  245.0 27.3 reduce-scatter.17
  275.7 28.4 reduce-scatter.11
  307.1 30.2 reduce-scatter.19
  340.7 28.9 reduce-scatter.13
  372.1 44.1 all-gather.4
  418.6 45.2 all-gather.2

commit v3 on v2

--- a/solution.py
+++ b/solution.py
@@ -101,10 +101,8 @@
     length = -(-total // (lanes * groups * 8)) * groups * 8
     flat = jnp.concatenate([part.reshape(-1) for part in parts])
     flat = jnp.pad(flat, (0, length * lanes - total)).reshape(length, lanes)
-    for name in SCATTER:
-        flat = lax.psum_scatter(flat, name, scatter_dimension=0, tiled=True)
-    for name in reversed(SCATTER):
-        flat = lax.all_gather(flat, name, axis=0, tiled=True)
+    flat = lax.psum(flat, ("y", "x"))
+    flat = lax.psum(flat, "zl")
     flat = flat.reshape(-1)
     out, start = [], 0
     for part in parts:

time: 476 us -> 530 us (1.11)
  the two profiles are of different devices: /device:TPU:2 before, /device:TPU:1 now
where the time goes in v3:
time: 530 us; the launch traced here: 528 us
  waiting for transfers between devices  402 us (76%)
  starting transfers between devices  39.1 us (7%)
  matrix products  38.6 us (7%)
  other arithmetic  21.2 us (4%)
  between operations  15.2 us (3%)
  local copies, waits for them, and re-layouts  12.5 us (2%)
    psum x1, waiting for transfers between devices, reduce_replicas(): flat = lax.psum(flat, ('y', 'x'))  186 us
    psum x1, waiting for transfers between devices, reduce_replicas(): flat = lax.psum(flat, 'zl')  164 us
    ppermute x8, waiting for transfers between devices, hop(): return lax.ppermute(value, 'zh', [(source, target)])  51.2 us
    ppermute x8, starting transfers between devices, swap_core(): return lax.ppermute(value, 'core', [(0, 1), (1, 0)])  30.3 us
    dot_general x24, matrix products, rows_product(): lax.dot_general(left, right, (((0,), (0,)), ((), ())), preferred_element_...  18 us
  transfers between devices with their start and end apart: 18, of which 6 were waited for; matrix products, arithmetic and copies ran while one was open for 7% of the time, Pallas kernels for 0%

profile of v3, /device:TPU:1, one launch (start us, length us, event | category | flops | bytes accessed | tf_op | source)
XLA Modules:
  0.0 528.4 jit_solution(7471543347545260073)
XLA Ops:
  7.2 12.6 %collective-permute-start = (bf16[320,640]{1,0:T(8,128)(2,1)}, bf16[320,640]{1,0:T(8,128)(2,1)}, u32[]{:S(2)}, u32[]{:S(2)}) collective-permute-start(bf16[320,640]{1,0:T(8,128)(2,1)} %bitcast.117), channel_id=1, source_target_pairs={{0,1},{1,0},{2,3},{3,2},{4,5},{5,4},{6,7},{7,6},{8,9},{9,8},{10,11... | collective-permute-start | bytes 1228808 | tf_op jit(solution)/shard_map/ppermute | solution.py:123
  19.8 1.9 collective-permute-start.1
  21.7 2.4 collective-permute-start.4
  24.1 1.9 collective-permute-start.5
  26.1 1.2 constant_dynamic-slice_fusion
  30.1 1.1 broadcast_select_fusion.7
  31.2 1.8 broadcast_select_fusion.4
  35.0 1.6 collective-permute-start.2
  36.6 0.8 broadcast_select_fusion.10
  37.4 1.8 collective-permute-done.2
  42.1 1.2 broadcast_select_fusion.3
  43.6 2.3 multiply_reduce_fusion.5
  45.9 1.7 fusion.21
  48.0 1.3 fusion.15
  53.1 1.3 collective-permute-start.7
  54.7 26.9 %collective-permute-done.7 = bf16[192,320]{1,0:T(8,128)(2,1)S(1)} collective-permute-done((bf16[192,320]{1,0:T(8,128)(2,1)S(1)}, bf16[192,320]{1,0:T(8,128)(2,1)S(1)}, u32[]{:S(2)}, u32[]{:S(2)}) %collective-permute-start.7) | collective-permute-done | bytes 122912 | tf_op jit(solution)/shard_map/ppermute | solution.py:127
  86.0 1.5 collective-permute-start.8
  87.9 1.5 collective-permute-done.8
  96.9 1.3 broadcast_select_fusion
  98.2 4.5 collective-permute-start.14
  105.7 1.2 broadcast_select_fusion.9
  107.0 1.9 collective-permute-start.15
  111.7 1.2 convolution_select_fusion.8
  113.1 1.5 collective-permute-start.11
  114.6 1.3 convolution_select_fusion.4
  115.9 1.3 convolution_select_fusion.6
  117.2 1.2 convolution_select_fusion.10
  118.4 21.0 %collective-permute-done.11 = bf16[192,320]{1,0:T(8,128)(2,1)S(1)} collective-permute-done((bf16[192,320]{1,0:T(8,128)(2,1)S(1)}, bf16[192,320]{1,0:T(8,128)(2,1)S(1)}, u32[]{:S(2)}, u32[]{:S(2)}) %collective-permute-start.11) | collective-permute-done | bytes 122912 | tf_op jit(solution)/shard_map/ppermute | solution.py:127
  140.4 1.7 convolution_select_fusion.11
  142.1 1.5 broadcast_select_fusion.6
  143.6 3.2 collective-permute-start.12
  147.3 1.6 broadcast_select_fusion.1
  148.9 1.9 collective-permute-start.13
  150.8 1.1 select_add_fusion.3
  152.2 1.3 select_add_fusion
  154.3 1.3 fusion.1
  156.3 1.3 select_add_fusion.2
  157.6 1.1 copy-done.3
  158.9 1.3 select_add_fusion.1
  161.1 1.5 fusion
  162.6 186.2 %all-reduce.7.cloned.1.call-done = (f32[4096,128]{1,0:T(8,128)}, f32[3072,128]{1,0:T(8,128)}) async-done(((f32[4096,128]{1,0:T(8,128)}, f32[3072,128]{1,0:T(8,128)}), (f32[4096,128]{1,0:T(8,128)}, f32[3072,128]{1,0:T(8,128)})) %all-reduce.7.cloned.1.call-update) | async-done | bytes 3670032 | tf_op jit(solution)/shard_map/psum | solution.py:104
  348.8 164.4 %all-reduce.9.cloned.1.call-done = (f32[4096,128]{1,0:T(8,128)}, f32[3072,128]{1,0:T(8,128)}) async-done(((f32[4096,128]{1,0:T(8,128)}, f32[3072,128]{1,0:T(8,128)}), (f32[4096,128]{1,0:T(8,128)}, f32[3072,128]{1,0:T(8,128)})) %all-reduce.9.cloned.1.call-update) | async-done | bytes 3670032 | tf_op jit(solution)/shard_map/psum | solution.py:105
  513.2 1.3 slice_multiply_fusion
  514.5 1.8 slice_multiply_fusion.3
  516.8 1.2 copy.24
  518.4 1.2 copy.25
  519.6 1.1 mul.728
  520.6 1.0 mul.737
  (196 shorter events, 35.2 us)
Async XLA Ops:
  7.2 22.9 %copy-start.16 = (bf16[1,320,640]{2,1,0:T(8,128)(2,1)S(1)}, bf16[1,320,640]{2,1,0:T(8,128)(2,1)}, u32[]{:S(2)}) copy-start(bf16[1,320,640]{2,1,0:T(8,128)(2,1)} %param.11) | copy-start | bytes 1228804
  7.2 341.6 %all-reduce.7.cloned.1.call-start = ((), (), s32[]{:S(2)}) async-start(), calls=%async_computation | async-start | bytes 7340032 | tf_op jit(solution)/shard_map/psum | solution.py:104
  7.2 22.9 %collective-permute-start = (bf16[320,640]{1,0:T(8,128)(2,1)}, bf16[320,640]{1,0:T(8,128)(2,1)}, u32[]{:S(2)}, u32[]{:S(2)}) collective-permute-start(bf16[320,640]{1,0:T(8,128)(2,1)} %bitcast.117), channel_id=1, source_target_pairs={{0,1},{1,0},{2,3},{3,2},{4,5},{5,4},{6,7},{7,6},{8,9},{9,8},{10,11... | collective-permute-start | bytes 1228808 | tf_op jit(solution)/shard_map/ppermute | solution.py:123
  19.8 11.4 %collective-permute-start.1 = (bf16[640,320]{0,1:T(8,128)(2,1)}, bf16[640,320]{0,1:T(8,128)(2,1)}, u32[]{:S(2)}, u32[]{:S(2)}) collective-permute-start(bf16[640,320]{0,1:T(8,128)(2,1)} %bitcast.118), channel_id=1, source_target_pairs={{0,1},{1,0},{2,3},{3,2},{4,5},{5,4},{6,7},{7,6},{8,9},{9,8},{10,11... | collective-permute-start | bytes 1228808 | tf_op jit(solution)/shard_map/ppermute | solution.py:123
  21.7 20.4 %collective-permute-start.4 = (bf16[640,320]{0,1:T(8,128)(2,1)}, bf16[640,320]{0,1:T(8,128)(2,1)}, u32[]{:S(2)}, u32[]{:S(2)}) collective-permute-start(bf16[640,320]{0,1:T(8,128)(2,1)} %bitcast.119), channel_id=1, source_target_pairs={{0,1},{1,0},{2,3},{3,2},{4,5},{5,4},{6,7},{7,6},{8,9},{9,8},{10,11... | collective-permute-start | bytes 1228808 | tf_op jit(solution)/shard_map/ppermute | solution.py:123
  24.1 12.5 %collective-permute-start.5 = (bf16[320,320]{1,0:T(8,128)(2,1)}, bf16[320,320]{1,0:T(8,128)(2,1)S(1)}, u32[]{:S(2)}, u32[]{:S(2)}) collective-permute-start(bf16[320,320]{1,0:T(8,128)(2,1)} %bitcast.120), channel_id=1, source_target_pairs={{0,1},{1,0},{2,3},{3,2},{4,5},{5,4},{6,7},{7,6},{8,9},{9,8},{10,11... | collective-permute-start | bytes 614408 | tf_op jit(solution)/shard_map/ppermute | solution.py:123
  28.9 2.3 copy-start.17
  33.0 6.3 %copy-start.18 = (bf16[640,320]{0,1:T(8,128)(2,1)}, bf16[640,320]{0,1:T(8,128)(2,1)S(1)}, u32[]{:S(2)}) copy-start(bf16[640,320]{0,1:T(8,128)(2,1)S(1)} %get-tuple-element.36) | copy-start | bytes 1228804
  33.0 1.3 copy-start.20
  33.7 0.7 copy-start.26
  34.4 2.2 copy-start.22
  35.0 4.3 collective-permute-start.2
  40.0 0.7 copy-start.28
  41.3 2.3 copy-start.27
  41.3 2.0 collective-permute-start.3
  48.0 1.8 copy-start.24
  50.2 1.2 collective-permute-start.6
  50.9 1.0 copy-start.23
  51.3 88.2 %copy-start.6 = (f32[192,640]{1,0:T(8,128)}, f32[192,640]{1,0:T(8,128)S(1)}, u32[]{:S(2)}) copy-start(f32[192,640]{1,0:T(8,128)S(1)} %fusion.104) | copy-start | bytes 1474564
  53.1 28.5 %collective-permute-start.7 = (bf16[192,320]{1,0:T(8,128)(2,1)S(1)}, bf16[192,320]{1,0:T(8,128)(2,1)S(1)}, u32[]{:S(2)}, u32[]{:S(2)}) collective-permute-start(bf16[192,320]{1,0:T(8,128)(2,1)S(1)} %fusion.18), channel_id=1, source_target_pairs={{2,0},{3,1},{8,6},{9,7},{14,12},{15,13},{20,18},{21,19},{26,24},{2... | collective-permute-start | bytes 368648 | tf_op jit(solution)/shard_map/ppermute | solution.py:127
  54.7 61.2 %copy-start.14 = (f32[192,640]{1,0:T(8,128)}, f32[192,640]{1,0:T(8,128)S(1)}, u32[]{:S(2)}) copy-start(f32[192,640]{1,0:T(8,128)S(1)} %fusion.105) | copy-start | bytes 1474564
  86.0 3.4 collective-permute-start.8
  91.9 1.4 collective-permute-start.9
  94.8 1.0 copy-start.21
  98.2 54.0 %collective-permute-start.14 = (f32[640,320]{0,1:T(8,128)}, f32[640,320]{0,1:T(8,128)}, u32[]{:S(2)}, u32[]{:S(2)}) collective-permute-start(f32[640,320]{0,1:T(8,128)} %get-tuple-element.90), channel_id=1, source_target_pairs={{0,1},{1,0},{2,3},{3,2},{4,5},{5,4},{6,7},{7,6},{8,9},{9,8},{10,11... | collective-permute-start | bytes 2457608 | tf_op jit(solution)/shard_map/ppermute | solution.py:123
  102.7 1.0 copy-start.19
  104.6 4.3 collective-permute-start.10
  105.7 3.2 copy-start.8
  107.0 43.8 %collective-permute-start.15 = (f32[320,320]{1,0:T(8,128)}, f32[320,320]{1,0:T(8,128)}, u32[]{:S(2)}, u32[]{:S(2)}) collective-permute-start(f32[320,320]{1,0:T(8,128)} %get-tuple-element.88), channel_id=1, source_target_pairs={{0,1},{1,0},{2,3},{3,2},{4,5},{5,4},{6,7},{7,6},{8,9},{9,8},{10,11... | collective-permute-start | bytes 1228808 | tf_op jit(solution)/shard_map/ppermute | solution.py:123
  113.1 26.4 %collective-permute-start.11 = (bf16[192,320]{1,0:T(8,128)(2,1)S(1)}, bf16[192,320]{1,0:T(8,128)(2,1)S(1)}, u32[]{:S(2)}, u32[]{:S(2)}) collective-permute-start(bf16[192,320]{1,0:T(8,128)(2,1)S(1)} %add_convert_fusion.3), channel_id=1, source_target_pairs={{2,0},{3,1},{8,6},{9,7},{14,12},{15,13},{20,18},{21,19},{26,24},{2... | collective-permute-start | bytes 368648 | tf_op jit(solution)/shard_map/ppermute | solution.py:127
  142.1 1.5 copy-start
  142.1 4.7 copy-start.15
  142.1 4.7 copy-start.25
  143.6 3.6 copy-start.7
  143.6 3.6 copy-start.13
  143.6 12.0 %collective-permute-start.12 = (f32[320,640]{1,0:T(8,128)}, f32[320,640]{1,0:T(8,128)}, u32[]{:S(2)}, u32[]{:S(2)}) collective-permute-start(f32[320,640]{1,0:T(8,128)} %get-tuple-element.86), channel_id=1, source_target_pairs={{0,1},{1,0},{2,3},{3,2},{4,5},{5,4},{6,7},{7,6},{8,9},{9,8},{10,11... | collective-permute-start | bytes 2457608 | tf_op jit(solution)/shard_map/ppermute | solution.py:123
  147.3 1.6 copy-start.2
  147.3 3.5 copy-start.9
  147.3 3.5 copy-start.10
  148.9 8.8 %collective-permute-start.13 = (f32[640,320]{0,1:T(8,128)}, f32[640,320]{0,1:T(8,128)}, u32[]{:S(2)}, u32[]{:S(2)}) collective-permute-start(f32[640,320]{0,1:T(8,128)} %get-tuple-element.84), channel_id=1, source_target_pairs={{0,1},{1,0},{2,3},{3,2},{4,5},{5,4},{6,7},{7,6},{8,9},{9,8},{10,11... | collective-permute-start | bytes 2457608 | tf_op jit(solution)/shard_map/ppermute | solution.py:123
  154.3 1.4 copy-start.1
  154.3 2.0 copy-start.4
  157.5 1.1 copy-start.3
  157.6 1.4 copy-start.5
  162.6 350.6 %all-reduce.9.cloned.1.call-start = ((), (), s32[]{:S(2)}) async-start(), calls=%async_computation.1 | async-start | bytes 7340032 | tf_op jit(solution)/shard_map/psum | solution.py:105
  513.2 3.1 copy-start.12
  518.4 2.3 copy-start.11
Sparse Core Ops, SparseCore 0:
  162.7 186.0 all-reduce.6
  352.1 161.0 all-reduce.8

commit v4 on v2

--- a/solution.py
+++ b/solution.py
@@ -102,15 +102,30 @@
     flat = jnp.concatenate([part.reshape(-1) for part in parts])
     flat = jnp.pad(flat, (0, length * lanes - total)).reshape(length, lanes)
     for name in SCATTER:
-        flat = lax.psum_scatter(flat, name, scatter_dimension=0, tiled=True)
+        flat = scatter_sum(flat, name)
+    flat = flat.astype(jnp.bfloat16)
     for name in reversed(SCATTER):
-        flat = lax.all_gather(flat, name, axis=0, tiled=True)
+        flat = gather_all(flat, name)
+    flat = flat.astype(jnp.float32)
     flat = flat.reshape(-1)
     out, start = [], 0
     for part in parts:
         out.append(flat[start : start + part.size].reshape(part.shape))
         start += part.size
     return tuple(out)
+
+
+def scatter_sum(flat, name):
+    count = lax.axis_size(name)
+    blocks = flat.astype(jnp.bfloat16).reshape(count, flat.shape[0] // count, flat.shape[1])
+    got = lax.all_to_all(blocks, name, 0, 0, tiled=False)
+    return jnp.sum(got.astype(jnp.float32), axis=0)
+
+
+def gather_all(flat, name):
+    count = lax.axis_size(name)
+    blocks = jnp.broadcast_to(flat[None], (count,) + flat.shape)
+    return lax.all_to_all(blocks, name, 0, 0, tiled=False).reshape(-1, flat.shape[1])
 
 
 def dp_split(mesh):
@@ -201,7 +216,6 @@
         return mine + swap_core(theirs)
 
     factor = 1.0 / math.prod(lax.axis_size(name) for name in DP)
-    total_mix, total_up = reduce_replicas((combine(grad_mix), combine(grad_up)))
 
     grad_in = [None, None]
     grad_out = [None, None]
@@ -218,7 +232,9 @@
         grad_in = [keep(valid, in0, grad_in[0]), keep(valid, in1, grad_in[1])]
         grad_out = [keep(valid, out0, grad_out[0]), keep(valid, out1, grad_out[1])]
 
-    total_in, total_out = reduce_replicas((combine(grad_in), combine(grad_out)))
+    total_in, total_out, total_mix, total_up = reduce_replicas(
+        (combine(grad_in), combine(grad_out), combine(grad_mix), combine(grad_up))
+    )
     return (
         (total_in * factor)[None],
         (total_out * factor)[None],

time: 476 us -> 287 us (0.60)
  waiting for transfers between devices: 304 us -> 55.4 us
  blocking collectives: 52.4 us -> 128 us
  between operations: 15.3 us -> 1.85 us
    reduce_scatter x5 -> x0, waiting for transfers between devices: 153 us -> none  [reduce_replicas(): flat = lax.psum_scatter(flat, name, scatter_dimension=0, tiled=True)]
    all_to_all x0 -> x6, blocking collectives: none -> 128 us  [the longest x3 75.6 us: scatter_sum(): got = lax.all_to_all(blocks, name, 0, 0, tiled=False)]
    all_gather x2 -> x0, waiting for transfers between devices: 63.1 us -> none  [reduce_replicas(): flat = lax.all_gather(flat, name, axis=0, tiled=True)]
    all_gather x4 -> x0, blocking collectives: 52.4 us -> none  [reduce_replicas(): flat = lax.all_gather(flat, name, axis=0, tiled=True)]
    unnamed x9 -> x0, waiting for transfers between devices: 33.3 us -> none
    another operation x0 -> x4, other arithmetic: none -> 5.68 us
  transfers between devices with their start and end apart: 24 -> 16, of which waited for: 13 -> 4; matrix products, arithmetic and copies ran while one was open for 8% -> 13% of each run, Pallas kernels for 0% -> 0%
where the time goes in v4:
time: 287 us; the launch traced here: 286 us
  blocking collectives  128 us (45%)
  waiting for transfers between devices  55.4 us (19%)
  matrix products  35.9 us (13%)
  starting transfers between devices  35.7 us (12%)
  other arithmetic  15.1 us (5%)
  local copies, waits for them, and re-layouts  13.3 us (5%)
    all_to_all x3, blocking collectives, scatter_sum(): got = lax.all_to_all(blocks, name, 0, 0, tiled=False)  75.6 us
    ppermute x8, waiting for transfers between devices, hop(): return lax.ppermute(value, 'zh', [(source, target)])  55.4 us
    all_to_all x3, blocking collectives, gather_all(): lax.all_to_all(blocks, name, 0, 0, tiled=False).reshape(-1, flat.shape[1])  52.8 us
    ppermute x8, starting transfers between devices, hop(): return lax.ppermute(value, 'zh', [(source, target)])  18.2 us
    ppermute x8, starting transfers between devices, swap_core(): return lax.ppermute(value, 'core', [(0, 1), (1, 0)])  17.5 us
    dot_general x24, matrix products, rows_product(): lax.dot_general(left, right, (((0,), (0,)), ((), ())), preferred_element_...  16.2 us
    dot_general x22, matrix products, times_transposed(): lax.dot_general(left, right, (((1,), (1,)), ((), ())), preferred_element_...  7.57 us
    dot_general x6, matrix products, down_forward(): jnp.dot(gated, out_matrix, preferred_element_type=jnp.float32)  6.5 us
  transfers between devices with their start and end apart: 16, of which 4 were waited for; matrix products, arithmetic and copies ran while one was open for 13% of the time, Pallas kernels for 0%

profile of v4, /device:TPU:2, one launch (start us, length us, event | category | flops | bytes accessed | tf_op | source)
XLA Modules:
  0.0 285.7 jit_solution(13788281991586711839)
XLA Ops:
  0.6 2.1 collective-permute-start.4
  2.7 2.4 collective-permute-start.1
  5.1 1.9 collective-permute-start
  7.0 2.4 collective-permute-start.5
  9.5 1.2 constant_dynamic-slice_fusion
  11.6 0.7 select_reduce_fusion
  12.5 0.8 multiply_sine_fusion
  13.6 1.1 broadcast_select_fusion.5
  16.7 10.9 %collective-permute-start.2 = (bf16[192,320]{1,0:T(8,128)(2,1)S(1)}, bf16[192,320]{1,0:T(8,128)(2,1)S(1)}, u32[]{:S(2)}, u32[]{:S(2)}) collective-permute-start(bf16[192,320]{1,0:T(8,128)(2,1)S(1)} %fusion.15), channel_id=1, source_target_pairs={{0,2},{1,3},{6,8},{7,9},{12,14},{13,15},{18,20},{19,21},{24,26},{2... | collective-permute-start | bytes 368648 | tf_op jit(solution)/shard_map/ppermute | solution.py:144
  27.6 0.8 broadcast_select_fusion.10
  28.5 2.4 collective-permute-done.2
  33.6 1.1 broadcast_select_fusion.2
  35.0 2.4 multiply_reduce_fusion.5
  37.4 1.7 fusion.26
  43.7 1.3 collective-permute-start.7
  45.3 27.6 %collective-permute-done.7 = bf16[192,320]{1,0:T(8,128)(2,1)S(1)} collective-permute-done((bf16[192,320]{1,0:T(8,128)(2,1)S(1)}, bf16[192,320]{1,0:T(8,128)(2,1)S(1)}, u32[]{:S(2)}, u32[]{:S(2)}) %collective-permute-start.7) | collective-permute-done | bytes 122912 | tf_op jit(solution)/shard_map/ppermute | solution.py:144
  77.3 1.6 collective-permute-start.8
  79.4 2.1 collective-permute-done.8
  88.7 1.2 broadcast_select_fusion.9
  89.9 1.9 collective-permute-start.15
  94.2 0.8 collective-permute-start.10
  95.0 1.3 broadcast_select_fusion
  96.3 2.4 collective-permute-start.14
  102.0 1.5 collective-permute-start.11
  103.9 1.2 convolution_select_fusion.10
  105.2 1.2 convolution_select_fusion.8
  106.4 23.4 %collective-permute-done.11 = bf16[192,320]{1,0:T(8,128)(2,1)S(1)} collective-permute-done((bf16[192,320]{1,0:T(8,128)(2,1)S(1)}, bf16[192,320]{1,0:T(8,128)(2,1)S(1)}, u32[]{:S(2)}, u32[]{:S(2)}) %collective-permute-start.11) | collective-permute-done | bytes 122912 | tf_op jit(solution)/shard_map/ppermute | solution.py:144
  131.4 1.6 broadcast_select_fusion.1
  132.9 2.0 collective-permute-start.13
  135.0 1.7 convolution_select_fusion.11
  136.7 1.5 broadcast_select_fusion.6
  138.3 2.4 collective-permute-start.12
  140.7 1.1 add_convert_fusion.3
  142.1 2.0 add_convert_fusion
  144.1 1.4 copy.23
  145.5 1.3 reshape.274
  146.9 1.3 add_convert_fusion.1
  149.3 1.3 add_convert_fusion.2
  151.0 47.0 %all_to_all.30 = bf16[8,768,128]{2,1,0:T(8,128)(2,1)S(1)} all-to-all(bf16[8,768,128]{2,1,0:T(8,128)(2,1)S(1)} %bitcast.121), channel_id=1, replica_groups=mesh['y'=8,'x'=4,'zl'=4,'zh'=3,'core'=2] {'y'}, dimensions={0} | all-to-all | bytes 3145728 | tf_op jit(solution)/shard_map/all_to_all | solution.py:121
  198.3 9.5 %all_to_all.31 = bf16[4,192,128]{2,1,0:T(8,128)(2,1)S(1)} all-to-all(bf16[4,192,128]{2,1,0:T(8,128)(2,1)S(1)} %bitcast.123), channel_id=1, replica_groups=mesh['y'=8,'x'=4,'zl'=4,'zh'=3,'core'=2] {'x'}, dimensions={0} | all-to-all | bytes 393216 | tf_op jit(solution)/shard_map/all_to_all | solution.py:121
  207.9 19.1 %all_to_all.32 = bf16[4,48,128]{2,1,0:T(8,128)(2,1)S(1)} all-to-all(bf16[4,48,128]{2,1,0:T(8,128)(2,1)S(1)} %bitcast.128), channel_id=1, replica_groups=mesh['y'=8,'x'=4,'zl'=4,'zh'=3,'core'=2] {'zl'}, dimensions={0} | all-to-all | bytes 98304 | tf_op jit(solution)/shard_map/all_to_all | solution.py:121
  227.0 8.1 %all_to_all.33 = bf16[4,48,128]{2,1,0:T(8,128)(2,1)S(1)} all-to-all(bf16[4,48,128]{2,1,0:T(8,128)(2,1)S(1)} %broadcast_in_dim.27), channel_id=1, replica_groups=mesh['y'=8,'x'=4,'zl'=4,'zh'=3,'core'=2] {'zl'}, dimensions={0} | all-to-all | bytes 98304 | tf_op jit(solution)/shard_map/all_to_all | solution.py:128
  235.1 8.7 %all_to_all.34 = bf16[4,192,128]{2,1,0:T(8,128)(2,1)S(1)} all-to-all(bf16[4,192,128]{2,1,0:T(8,128)(2,1)S(1)} %broadcast_in_dim.29), channel_id=1, replica_groups=mesh['y'=8,'x'=4,'zl'=4,'zh'=3,'core'=2] {'x'}, dimensions={0} | all-to-all | bytes 393216 | tf_op jit(solution)/shard_map/all_to_all | solution.py:128
  244.0 36.1 %all_to_all.35 = bf16[8,768,128]{2,1,0:T(8,128)(2,1)S(1)} all-to-all(bf16[8,768,128]{2,1,0:T(8,128)(2,1)S(1)} %broadcast_in_dim.31), channel_id=1, replica_groups=mesh['y'=8,'x'=4,'zl'=4,'zh'=3,'core'=2] {'y'}, dimensions={0} | all-to-all | bytes 3145728 | tf_op jit(solution)/shard_map/all_to_all | solution.py:128
  280.6 1.1 mul.730
  282.0 1.2 copy.24
  283.5 1.2 copy.25
  284.7 1.0 mul.737
  (197 shorter events, 33.9 us)
Async XLA Ops:
  0.6 12.9 %copy-start.11 = (bf16[1,640,320]{1,2,0:T(8,128)(2,1)S(1)}, bf16[1,640,320]{1,2,0:T(8,128)(2,1)}, u32[]{:S(2)}) copy-start(bf16[1,640,320]{1,2,0:T(8,128)(2,1)} %param.12) | copy-start | bytes 1228804
  0.6 33.0 %collective-permute-start.4 = (bf16[640,320]{0,1:T(8,128)(2,1)}, bf16[640,320]{0,1:T(8,128)(2,1)}, u32[]{:S(2)}, u32[]{:S(2)}) collective-permute-start(bf16[640,320]{0,1:T(8,128)(2,1)} %bitcast.126), channel_id=1, source_target_pairs={{0,1},{1,0},{2,3},{3,2},{4,5},{5,4},{6,7},{7,6},{8,9},{9,8},{10,11... | collective-permute-start | bytes 1228808 | tf_op jit(solution)/shard_map/ppermute | solution.py:140
  2.7 10.8 %collective-permute-start.1 = (bf16[640,320]{0,1:T(8,128)(2,1)}, bf16[640,320]{0,1:T(8,128)(2,1)}, u32[]{:S(2)}, u32[]{:S(2)}) collective-permute-start(bf16[640,320]{0,1:T(8,128)(2,1)} %bitcast.124), channel_id=1, source_target_pairs={{0,1},{1,0},{2,3},{3,2},{4,5},{5,4},{6,7},{7,6},{8,9},{9,8},{10,11... | collective-permute-start | bytes 1228808 | tf_op jit(solution)/shard_map/ppermute | solution.py:140
  5.1 9.6 %collective-permute-start = (bf16[320,640]{1,0:T(8,128)(2,1)}, bf16[320,640]{1,0:T(8,128)(2,1)S(1)}, u32[]{:S(2)}, u32[]{:S(2)}) collective-permute-start(bf16[320,640]{1,0:T(8,128)(2,1)} %bitcast.125), channel_id=1, source_target_pairs={{0,1},{1,0},{2,3},{3,2},{4,5},{5,4},{6,7},{7,6},{8,9},{9,8},{10,11... | collective-permute-start | bytes 1228808 | tf_op jit(solution)/shard_map/ppermute | solution.py:140
  7.0 20.6 %collective-permute-start.5 = (bf16[320,320]{1,0:T(8,128)(2,1)}, bf16[320,320]{1,0:T(8,128)(2,1)S(1)}, u32[]{:S(2)}, u32[]{:S(2)}) collective-permute-start(bf16[320,320]{1,0:T(8,128)(2,1)} %bitcast.127), channel_id=1, source_target_pairs={{0,1},{1,0},{2,3},{3,2},{4,5},{5,4},{6,7},{7,6},{8,9},{9,8},{10,11... | collective-permute-start | bytes 614408 | tf_op jit(solution)/shard_map/ppermute | solution.py:140
  12.4 2.3 copy-start.12
  14.7 16.3 %copy-start.14 = (bf16[640,320]{0,1:T(8,128)(2,1)}, bf16[640,320]{0,1:T(8,128)(2,1)S(1)}, u32[]{:S(2)}) copy-start(bf16[640,320]{0,1:T(8,128)(2,1)S(1)} %get-tuple-element.32) | copy-start | bytes 1228804
  14.7 17.0 %copy-start.16 = (bf16[640,320]{0,1:T(8,128)(2,1)}, bf16[640,320]{0,1:T(8,128)(2,1)S(1)}, u32[]{:S(2)}) copy-start(bf16[640,320]{0,1:T(8,128)(2,1)S(1)} %get-tuple-element.33) | copy-start | bytes 1228804
  15.5 0.7 copy-start.25
  16.1 11.5 %copy-start.19 = (bf16[1,320,320]{2,1,0:T(8,128)(2,1)S(1)}, bf16[1,320,320]{2,1,0:T(8,128)(2,1)}, u32[]{:S(2)}) copy-start(bf16[1,320,320]{2,1,0:T(8,128)(2,1)} %param.14) | copy-start | bytes 614404
  16.7 15.0 %copy-start.23 = (bf16[192,320]{1,0:T(8,128)(2,1)}, bf16[192,320]{1,0:T(8,128)(2,1)S(1)}, u32[]{:S(2)}) copy-start(bf16[192,320]{1,0:T(8,128)(2,1)S(1)} %fusion.15) | copy-start | bytes 368644
  16.7 14.2 %collective-permute-start.2 = (bf16[192,320]{1,0:T(8,128)(2,1)S(1)}, bf16[192,320]{1,0:T(8,128)(2,1)S(1)}, u32[]{:S(2)}, u32[]{:S(2)}) collective-permute-start(bf16[192,320]{1,0:T(8,128)(2,1)S(1)} %fusion.15), channel_id=1, source_target_pairs={{0,2},{1,3},{6,8},{7,9},{12,14},{13,15},{18,20},{19,21},{24,26},{2... | collective-permute-start | bytes 368648 | tf_op jit(solution)/shard_map/ppermute | solution.py:144
  31.7 0.7 copy-start.26
  32.3 1.3 copy-start.13
  32.9 1.8 copy-start.24
  32.9 1.8 collective-permute-start.3
  34.9 2.4 copy-start.17
  37.3 2.2 copy-start.20
  39.5 1.0 copy-start.22
  40.8 1.2 collective-permute-start.6
  41.5 1.0 copy-start.21
  43.7 29.2 %collective-permute-start.7 = (bf16[192,320]{1,0:T(8,128)(2,1)S(1)}, bf16[192,320]{1,0:T(8,128)(2,1)S(1)}, u32[]{:S(2)}, u32[]{:S(2)}) collective-permute-start(bf16[192,320]{1,0:T(8,128)(2,1)S(1)} %fusion.23), channel_id=1, source_target_pairs={{2,0},{3,1},{8,6},{9,7},{14,12},{15,13},{20,18},{21,19},{26,24},{2... | collective-permute-start | bytes 368648 | tf_op jit(solution)/shard_map/ppermute | solution.py:144
  45.3 85.6 %copy-start.10 = (f32[192,640]{1,0:T(8,128)}, f32[192,640]{1,0:T(8,128)S(1)}, u32[]{:S(2)}) copy-start(f32[192,640]{1,0:T(8,128)S(1)} %fusion.110) | copy-start | bytes 1474564
  77.3 4.1 %collective-permute-start.8 = (bf16[192,320]{1,0:T(8,128)(2,1)S(1)}, bf16[192,320]{1,0:T(8,128)(2,1)S(1)}, u32[]{:S(2)}, u32[]{:S(2)}) collective-permute-start(bf16[192,320]{1,0:T(8,128)(2,1)S(1)} %slice.125), channel_id=1, source_target_pairs={{0,2},{1,3},{6,8},{7,9},{12,14},{13,15},{18,20},{19,21},{24,26},{2... | collective-permute-start | bytes 368648 | tf_op jit(solution)/shard_map/ppermute | solution.py:144
  83.1 1.9 collective-permute-start.9
  88.7 3.6 %copy-start.4 = (f32[320,320]{1,0:T(8,128)}, f32[320,320]{1,0:T(8,128)S(1)}, u32[]{:S(2)}) copy-start(f32[320,320]{1,0:T(8,128)S(1)} %convolution_select_fusion.14) | copy-start | bytes 1228804
  89.9 50.7 %collective-permute-start.15 = (f32[320,320]{1,0:T(8,128)}, f32[320,320]{1,0:T(8,128)}, u32[]{:S(2)}, u32[]{:S(2)}) collective-permute-start(f32[320,320]{1,0:T(8,128)} %get-tuple-element.72), channel_id=1, source_target_pairs={{0,1},{1,0},{2,3},{3,2},{4,5},{5,4},{6,7},{7,6},{8,9},{9,8},{10,11... | collective-permute-start | bytes 1228808 | tf_op jit(solution)/shard_map/ppermute | solution.py:140
  92.3 1.0 copy-start.15
  94.2 4.6 %copy-start.18 = (bf16[640,320]{0,1:T(8,128)(2,1)S(1)}, bf16[640,320]{0,1:T(8,128)(2,1)}, u32[]{:S(2)}) copy-start(bf16[640,320]{0,1:T(8,128)(2,1)} %copy-done.16) | copy-start | bytes 1228804
  94.2 4.5 %collective-permute-start.10 = (bf16[192,320]{1,0:T(8,128)(2,1)S(1)}, bf16[192,320]{1,0:T(8,128)(2,1)S(1)}, u32[]{:S(2)}, u32[]{:S(2)}) collective-permute-start(bf16[192,320]{1,0:T(8,128)(2,1)S(1)} %add_convert_fusion.11), channel_id=1, source_target_pairs={{4,2},{5,3},{10,8},{11,9},{16,14},{17,15},{22,20},{23,21},{28,26},... | collective-permute-start | bytes 368648 | tf_op jit(solution)/shard_map/ppermute | solution.py:144
  96.3 45.8 %collective-permute-start.14 = (f32[640,320]{0,1:T(8,128)}, f32[640,320]{0,1:T(8,128)}, u32[]{:S(2)}, u32[]{:S(2)}) collective-permute-start(f32[640,320]{0,1:T(8,128)} %get-tuple-element.74), channel_id=1, source_target_pairs={{0,1},{1,0},{2,3},{3,2},{4,5},{5,4},{6,7},{7,6},{8,9},{9,8},{10,11... | collective-permute-start | bytes 2457608 | tf_op jit(solution)/shard_map/ppermute | solution.py:140
  102.0 27.8 %collective-permute-start.11 = (bf16[192,320]{1,0:T(8,128)(2,1)S(1)}, bf16[192,320]{1,0:T(8,128)(2,1)S(1)}, u32[]{:S(2)}, u32[]{:S(2)}) collective-permute-start(bf16[192,320]{1,0:T(8,128)(2,1)S(1)} %add_convert_fusion.7), channel_id=1, source_target_pairs={{2,0},{3,1},{8,6},{9,7},{14,12},{15,13},{20,18},{21,19},{26,24},{2... | collective-permute-start | bytes 368648 | tf_op jit(solution)/shard_map/ppermute | solution.py:144
  130.1 0.7 copy-start.8
  131.3 1.6 copy-start
  132.9 3.8 %copy-start.9 = (bf16[192,640]{1,0:T(8,128)(2,1)S(1)}, bf16[192,640]{1,0:T(8,128)(2,1)}, u32[]{:S(2)}) copy-start(bf16[192,640]{1,0:T(8,128)(2,1)} %copy-done.8) | copy-start | bytes 737284
  132.9 13.9 %collective-permute-start.13 = (f32[640,320]{0,1:T(8,128)}, f32[640,320]{0,1:T(8,128)}, u32[]{:S(2)}, u32[]{:S(2)}) collective-permute-start(f32[640,320]{0,1:T(8,128)} %get-tuple-element.86), channel_id=1, source_target_pairs={{0,1},{1,0},{2,3},{3,2},{4,5},{5,4},{6,7},{7,6},{8,9},{9,8},{10,11... | collective-permute-start | bytes 2457608 | tf_op jit(solution)/shard_map/ppermute | solution.py:140
  136.7 4.0 %copy-start.5 = (f32[320,320]{1,0:T(8,128)S(1)}, f32[320,320]{1,0:T(8,128)}, u32[]{:S(2)}) copy-start(f32[320,320]{1,0:T(8,128)} %copy-done.4) | copy-start | bytes 1228804
  136.7 4.0 %copy-start.6 = (f32[320,320]{1,0:T(8,128)S(1)}, f32[320,320]{1,0:T(8,128)}, u32[]{:S(2)}) copy-start(f32[320,320]{1,0:T(8,128)} %get-tuple-element.73) | copy-start | bytes 1228804
  138.3 10.7 %collective-permute-start.12 = (f32[320,640]{1,0:T(8,128)}, f32[320,640]{1,0:T(8,128)}, u32[]{:S(2)}, u32[]{:S(2)}) collective-permute-start(f32[320,640]{1,0:T(8,128)} %get-tuple-element.88), channel_id=1, source_target_pairs={{0,1},{1,0},{2,3},{3,2},{4,5},{5,4},{6,7},{7,6},{8,9},{9,8},{10,11... | collective-permute-start | bytes 2457608 | tf_op jit(solution)/shard_map/ppermute | solution.py:140
  144.1 2.7 copy-start.1
  144.1 2.7 copy-start.2
  148.1 1.1 copy-start.3
  149.3 1.6 copy-start.7

commit v5 on v4

--- a/solution.py
+++ b/solution.py
@@ -6,7 +6,7 @@
 from jax.sharding import Mesh, PartitionSpec as P
 
 DP = ("y", "x", "zl")
-SCATTER = ("y", "x", "zl")
+SCATTER = ("x", "y", "zl")
 
 
 def rows_product(left, right):
@@ -106,7 +106,7 @@
     flat = flat.astype(jnp.bfloat16)
     for name in reversed(SCATTER):
         flat = gather_all(flat, name)
-    flat = flat.astype(jnp.float32)
+    flat = flat.astype(jnp.float32) * (1.0 / groups)
     flat = flat.reshape(-1)
     out, start = [], 0
     for part in parts:
@@ -213,9 +213,8 @@
     def combine(grads):
         mine = jnp.where(first, grads[0], grads[1])
         theirs = jnp.where(first, grads[1], grads[0])
-        return mine + swap_core(theirs)
-
-    factor = 1.0 / math.prod(lax.axis_size(name) for name in DP)
+        return mine + swap_core(theirs.astype(jnp.bfloat16)).astype(jnp.float32)
+
 
     grad_in = [None, None]
     grad_out = [None, None]
@@ -235,12 +234,7 @@
     total_in, total_out, total_mix, total_up = reduce_replicas(
         (combine(grad_in), combine(grad_out), combine(grad_mix), combine(grad_up))
     )
-    return (
-        (total_in * factor)[None],
-        (total_out * factor)[None],
-        (total_mix * factor)[None],
-        (total_up * factor)[None],
-    )
+    return (total_in[None], total_out[None], total_mix[None], total_up[None])
 
 
 def solution(mesh):

time: 287 us -> 265 us (0.923)
  blocking collectives: 128 us -> 103 us
    all_to_all x3, blocking collectives: 52.8 us -> 39.4 us  [gather_all(): lax.all_to_all(blocks, name, 0, 0, tiled=False).reshape(-1, flat.shape[1])]
    all_to_all x3, blocking collectives: 75.6 us -> 63.4 us  [scatter_sum(): got = lax.all_to_all(blocks, name, 0, 0, tiled=False)]
    another operation x2 -> x6, local copies, waits for them, and re-layouts: 1.64 us -> 5.22 us  [the longest x4 2.71 us: local(): return (total_in[None], total_out[None], total_mix[None], total_up[None])]
    unnamed x59 -> x79, local copies, waits for them, and re-layouts: 6.09 us -> 6.97 us
  transfers between devices with their start and end apart: 16 -> 16, of which waited for: 4 -> 4; matrix products, arithmetic and copies ran while one was open for 13% -> 16% of each run, Pallas kernels for 0% -> 0%
where the time goes in v5:
time: 265 us; the launch traced here: 264 us
  blocking collectives  103 us (39%)
  waiting for transfers between devices  53.8 us (20%)
  matrix products  37 us (14%)
  starting transfers between devices  35.6 us (13%)
  other arithmetic  16.5 us (6%)
  local copies, waits for them, and re-layouts  16 us (6%)
    all_to_all x3, blocking collectives, scatter_sum(): got = lax.all_to_all(blocks, name, 0, 0, tiled=False)  63.4 us
    ppermute x8, waiting for transfers between devices, hop(): return lax.ppermute(value, 'zh', [(source, target)])  53.7 us
    all_to_all x3, blocking collectives, gather_all(): lax.all_to_all(blocks, name, 0, 0, tiled=False).reshape(-1, flat.shape[1])  39.4 us
    ppermute x8, starting transfers between devices, hop(): return lax.ppermute(value, 'zh', [(source, target)])  18 us
    ppermute x8, starting transfers between devices, swap_core(): return lax.ppermute(value, 'core', [(0, 1), (1, 0)])  17.5 us
    dot_general x24, matrix products, rows_product(): lax.dot_general(left, right, (((0,), (0,)), ((), ())), preferred_element_...  16.1 us
    dot_general x22, matrix products, times_transposed(): lax.dot_general(left, right, (((1,), (1,)), ((), ())), preferred_element_...  8.71 us
    unnamed x79, local copies, waits for them, and re-layouts  6.97 us
  transfers between devices with their start and end apart: 16, of which 4 were waited for; matrix products, arithmetic and copies ran while one was open for 16% of the time, Pallas kernels for 0%

profile of v5, /device:TPU:2, one launch (start us, length us, event | category | flops | bytes accessed | tf_op | source)
XLA Modules:
  0.0 263.6 jit_solution(3949898311518334981)
XLA Ops:
  0.6 2.1 collective-permute-start.4
  2.7 2.4 collective-permute-start.1
  5.1 1.9 collective-permute-start
  7.0 2.4 collective-permute-start.5
  9.5 1.2 constant_dynamic-slice_fusion
  13.7 1.4 broadcast_select_fusion.5
  16.4 10.9 %collective-permute-start.2 = (bf16[192,320]{1,0:T(8,128)(2,1)S(1)}, bf16[192,320]{1,0:T(8,128)(2,1)S(1)}, u32[]{:S(2)}, u32[]{:S(2)}) collective-permute-start(bf16[192,320]{1,0:T(8,128)(2,1)S(1)} %fusion.15), channel_id=1, source_target_pairs={{0,2},{1,3},{6,8},{7,9},{12,14},{13,15},{18,20},{19,21},{24,26},{2... | collective-permute-start | bytes 368648 | tf_op jit(solution)/shard_map/ppermute | solution.py:144
  27.3 1.7 broadcast_select_fusion.6
  29.0 1.5 collective-permute-done.2
  33.0 1.1 broadcast_select_fusion
  34.8 2.5 multiply_reduce_fusion.5
  37.3 1.7 fusion.26
  43.6 1.3 collective-permute-start.7
  45.2 27.9 %collective-permute-done.7 = bf16[192,320]{1,0:T(8,128)(2,1)S(1)} collective-permute-done((bf16[192,320]{1,0:T(8,128)(2,1)S(1)}, bf16[192,320]{1,0:T(8,128)(2,1)S(1)}, u32[]{:S(2)}, u32[]{:S(2)}) %collective-permute-start.7) | collective-permute-done | bytes 122912 | tf_op jit(solution)/shard_map/ppermute | solution.py:144
  77.5 1.6 collective-permute-start.8
  79.6 2.1 collective-permute-done.8
  89.3 1.9 collective-permute-start.15
  94.2 1.4 select_convert_fusion
  95.7 2.4 collective-permute-start.14
  100.8 1.3 convolution_select_fusion.6
  102.3 1.5 collective-permute-start.11
  103.8 1.3 convolution_select_fusion.4
  105.1 1.2 convolution_select_fusion.10
  106.8 1.0 reshape.224
  107.7 22.3 %collective-permute-done.11 = bf16[192,320]{1,0:T(8,128)(2,1)} collective-permute-done((bf16[192,320]{1,0:T(8,128)(2,1)S(1)}, bf16[192,320]{1,0:T(8,128)(2,1)}, u32[]{:S(2)}, u32[]{:S(2)}) %collective-permute-start.11) | collective-permute-done | bytes 122912 | tf_op jit(solution)/shard_map/ppermute | solution.py:144
  130.0 0.9 add_convert_fusion.6
  131.0 1.4 fusion.12
  135.2 1.5 select_convert_fusion.1
  136.6 2.0 collective-permute-start.13
  138.7 1.8 convolution_select_fusion.11
  140.5 1.4 select_convert_fusion.2
  141.9 2.4 collective-permute-start.12
  144.3 2.0 add_convert_fusion
  146.3 1.3 copy.23
  147.6 1.3 reshape.223
  148.9 1.9 add_convert_fusion.1
  150.9 1.3 copy.22
  152.8 1.2 add_convert_fusion.2
  154.4 24.0 %all_to_all.30 = bf16[4,1536,128]{2,1,0:T(8,128)(2,1)S(1)} all-to-all(bf16[4,1536,128]{2,1,0:T(8,128)(2,1)S(1)} %bitcast.121), channel_id=1, replica_groups=mesh['y'=8,'x'=4,'zl'=4,'zh'=3,'core'=2] {'x'}, dimensions={0} | all-to-all | bytes 3145728 | tf_op jit(solution)/shard_map/all_to_all | solution.py:121
  178.9 20.3 %all_to_all.31 = bf16[8,192,128]{2,1,0:T(8,128)(2,1)S(1)} all-to-all(bf16[8,192,128]{2,1,0:T(8,128)(2,1)S(1)} %bitcast.122), channel_id=1, replica_groups=mesh['y'=8,'x'=4,'zl'=4,'zh'=3,'core'=2] {'y'}, dimensions={0} | all-to-all | bytes 786432 | tf_op jit(solution)/shard_map/all_to_all | solution.py:121
  199.3 19.1 %all_to_all.32 = bf16[4,48,128]{2,1,0:T(8,128)(2,1)S(1)} all-to-all(bf16[4,48,128]{2,1,0:T(8,128)(2,1)S(1)} %bitcast.129), channel_id=1, replica_groups=mesh['y'=8,'x'=4,'zl'=4,'zh'=3,'core'=2] {'zl'}, dimensions={0} | all-to-all | bytes 98304 | tf_op jit(solution)/shard_map/all_to_all | solution.py:121
  218.4 8.1 %all_to_all.33 = bf16[4,48,128]{2,1,0:T(8,128)(2,1)S(1)} all-to-all(bf16[4,48,128]{2,1,0:T(8,128)(2,1)S(1)} %broadcast_in_dim.27), channel_id=1, replica_groups=mesh['y'=8,'x'=4,'zl'=4,'zh'=3,'core'=2] {'zl'}, dimensions={0} | all-to-all | bytes 98304 | tf_op jit(solution)/shard_map/all_to_all | solution.py:128
  226.5 14.3 %all_to_all.34 = bf16[8,192,128]{2,1,0:T(8,128)(2,1)S(1)} all-to-all(bf16[8,192,128]{2,1,0:T(8,128)(2,1)S(1)} %broadcast_in_dim.29), channel_id=1, replica_groups=mesh['y'=8,'x'=4,'zl'=4,'zh'=3,'core'=2] {'y'}, dimensions={0} | all-to-all | bytes 786432 | tf_op jit(solution)/shard_map/all_to_all | solution.py:128
  241.0 17.1 %all_to_all.35 = bf16[4,1536,128]{2,1,0:T(8,128)(2,1)S(1)} all-to-all(bf16[4,1536,128]{2,1,0:T(8,128)(2,1)S(1)} %broadcast_in_dim.31), channel_id=1, replica_groups=mesh['y'=8,'x'=4,'zl'=4,'zh'=3,'core'=2] {'x'}, dimensions={0} | all-to-all | bytes 3145728 | tf_op jit(solution)/shard_map/all_to_all | solution.py:128
  258.5 1.1 broadcast_in_dim_reshape.14
  259.9 1.2 copy.24
  261.4 1.2 copy.25
  262.6 1.0 broadcast_in_dim_reshape.17
  (217 shorter events, 36.1 us)
Async XLA Ops:
  0.6 12.9 %copy-start.18 = (bf16[1,640,320]{1,2,0:T(8,128)(2,1)S(1)}, bf16[1,640,320]{1,2,0:T(8,128)(2,1)}, u32[]{:S(2)}) copy-start(bf16[1,640,320]{1,2,0:T(8,128)(2,1)} %param.12) | copy-start | bytes 1228804
  0.6 32.3 %collective-permute-start.4 = (bf16[640,320]{0,1:T(8,128)(2,1)}, bf16[640,320]{0,1:T(8,128)(2,1)}, u32[]{:S(2)}, u32[]{:S(2)}) collective-permute-start(bf16[640,320]{0,1:T(8,128)(2,1)} %bitcast.126), channel_id=1, source_target_pairs={{0,1},{1,0},{2,3},{3,2},{4,5},{5,4},{6,7},{7,6},{8,9},{9,8},{10,11... | collective-permute-start | bytes 1228808 | tf_op jit(solution)/shard_map/ppermute | solution.py:140
  2.7 10.8 %collective-permute-start.1 = (bf16[640,320]{0,1:T(8,128)(2,1)}, bf16[640,320]{0,1:T(8,128)(2,1)S(1)}, u32[]{:S(2)}, u32[]{:S(2)}) collective-permute-start(bf16[640,320]{0,1:T(8,128)(2,1)} %bitcast.124), channel_id=1, source_target_pairs={{0,1},{1,0},{2,3},{3,2},{4,5},{5,4},{6,7},{7,6},{8,9},{9,8},{10,11... | collective-permute-start | bytes 1228808 | tf_op jit(solution)/shard_map/ppermute | solution.py:140
  5.1 8.6 %collective-permute-start = (bf16[320,640]{1,0:T(8,128)(2,1)}, bf16[320,640]{1,0:T(8,128)(2,1)}, u32[]{:S(2)}, u32[]{:S(2)}) collective-permute-start(bf16[320,640]{1,0:T(8,128)(2,1)} %bitcast.125), channel_id=1, source_target_pairs={{0,1},{1,0},{2,3},{3,2},{4,5},{5,4},{6,7},{7,6},{8,9},{9,8},{10,11... | collective-permute-start | bytes 1228808 | tf_op jit(solution)/shard_map/ppermute | solution.py:140
  7.0 20.3 %collective-permute-start.5 = (bf16[320,320]{1,0:T(8,128)(2,1)}, bf16[320,320]{1,0:T(8,128)(2,1)}, u32[]{:S(2)}, u32[]{:S(2)}) collective-permute-start(bf16[320,320]{1,0:T(8,128)(2,1)} %bitcast.127), channel_id=1, source_target_pairs={{0,1},{1,0},{2,3},{3,2},{4,5},{5,4},{6,7},{7,6},{8,9},{9,8},{10,11... | collective-permute-start | bytes 614408 | tf_op jit(solution)/shard_map/ppermute | solution.py:140
  12.4 1.3 copy-start.19
  13.7 2.1 copy-start.23
  13.7 17.0 %copy-start.21 = (bf16[640,320]{0,1:T(8,128)(2,1)}, bf16[640,320]{0,1:T(8,128)(2,1)S(1)}, u32[]{:S(2)}) copy-start(bf16[640,320]{0,1:T(8,128)(2,1)S(1)} %get-tuple-element.32) | copy-start | bytes 1228804
  15.8 11.6 %copy-start.26 = (bf16[1,320,320]{2,1,0:T(8,128)(2,1)S(1)}, bf16[1,320,320]{2,1,0:T(8,128)(2,1)}, u32[]{:S(2)}) copy-start(bf16[1,320,320]{2,1,0:T(8,128)(2,1)} %param.14) | copy-start | bytes 614404
  16.4 14.3 %copy-start.30 = (bf16[192,320]{1,0:T(8,128)(2,1)}, bf16[192,320]{1,0:T(8,128)(2,1)S(1)}, u32[]{:S(2)}) copy-start(bf16[192,320]{1,0:T(8,128)(2,1)S(1)} %fusion.15) | copy-start | bytes 368644
  16.4 14.1 %collective-permute-start.2 = (bf16[192,320]{1,0:T(8,128)(2,1)S(1)}, bf16[192,320]{1,0:T(8,128)(2,1)S(1)}, u32[]{:S(2)}, u32[]{:S(2)}) collective-permute-start(bf16[192,320]{1,0:T(8,128)(2,1)S(1)} %fusion.15), channel_id=1, source_target_pairs={{0,2},{1,3},{6,8},{7,9},{12,14},{13,15},{18,20},{19,21},{24,26},{2... | collective-permute-start | bytes 368648 | tf_op jit(solution)/shard_map/ppermute | solution.py:144
  30.7 1.0 copy-start.24
  31.7 1.3 copy-start.20
  32.3 1.8 copy-start.32
  32.3 1.8 collective-permute-start.3
  34.8 2.5 copy-start.31
  34.8 2.5 copy-start.33
  40.7 1.2 collective-permute-start.6
  41.8 62.0 %copy-start.9 = (f32[192,640]{1,0:T(8,128)}, f32[192,640]{1,0:T(8,128)S(1)}, u32[]{:S(2)}) copy-start(f32[192,640]{1,0:T(8,128)S(1)} %fusion.110) | copy-start | bytes 1474564
  41.9 63.2 %copy-start.7 = (bf16[192,320]{1,0:T(8,128)(2,1)}, bf16[192,320]{1,0:T(8,128)(2,1)S(1)}, u32[]{:S(2)}) copy-start(bf16[192,320]{1,0:T(8,128)(2,1)S(1)} %multiply_convert_fusion.32) | copy-start | bytes 368644
  43.6 29.5 %collective-permute-start.7 = (bf16[192,320]{1,0:T(8,128)(2,1)S(1)}, bf16[192,320]{1,0:T(8,128)(2,1)S(1)}, u32[]{:S(2)}, u32[]{:S(2)}) collective-permute-start(bf16[192,320]{1,0:T(8,128)(2,1)S(1)} %fusion.23), channel_id=1, source_target_pairs={{2,0},{3,1},{8,6},{9,7},{14,12},{15,13},{20,18},{21,19},{26,24},{2... | collective-permute-start | bytes 368648 | tf_op jit(solution)/shard_map/ppermute | solution.py:144
  45.2 55.6 %copy-start.16 = (f32[192,640]{1,0:T(8,128)}, f32[192,640]{1,0:T(8,128)S(1)}, u32[]{:S(2)}) copy-start(f32[192,640]{1,0:T(8,128)S(1)} %fusion.111) | copy-start | bytes 1474564
  77.5 4.1 %collective-permute-start.8 = (bf16[192,320]{1,0:T(8,128)(2,1)S(1)}, bf16[192,320]{1,0:T(8,128)(2,1)S(1)}, u32[]{:S(2)}, u32[]{:S(2)}) collective-permute-start(bf16[192,320]{1,0:T(8,128)(2,1)S(1)} %slice.121), channel_id=1, source_target_pairs={{0,2},{1,3},{6,8},{7,9},{12,14},{13,15},{18,20},{19,21},{24,26},{2... | collective-permute-start | bytes 368648 | tf_op jit(solution)/shard_map/ppermute | solution.py:144
  83.3 1.9 collective-permute-start.9
  86.9 1.0 copy-start.25
  87.8 10.3 %copy-start.5 = (f32[192,320]{1,0:T(8,128)}, f32[192,320]{1,0:T(8,128)S(1)}, u32[]{:S(2)}) copy-start(f32[192,320]{1,0:T(8,128)S(1)} %get-tuple-element.21) | copy-start | bytes 737284
  89.3 17.4 %collective-permute-start.15 = (bf16[320,320]{1,0:T(8,128)(2,1)S(1)}, bf16[320,320]{1,0:T(8,128)(2,1)S(1)}, u32[]{:S(2)}, u32[]{:S(2)}) collective-permute-start(bf16[320,320]{1,0:T(8,128)(2,1)S(1)} %get-tuple-element.72), channel_id=1, source_target_pairs={{0,1},{1,0},{2,3},{3,2},{4,5},{5,4},{6,7},{7,6},{8,9},{9,8},{10,11... | collective-permute-start | bytes 614408 | tf_op jit(solution)/shard_map/ppermute | solution.py:140
  91.7 1.0 copy-start.22
  93.6 4.5 %collective-permute-start.10 = (bf16[192,320]{1,0:T(8,128)(2,1)S(1)}, bf16[192,320]{1,0:T(8,128)(2,1)S(1)}, u32[]{:S(2)}, u32[]{:S(2)}) collective-permute-start(bf16[192,320]{1,0:T(8,128)(2,1)S(1)} %add_convert_fusion.11), channel_id=1, source_target_pairs={{4,2},{5,3},{10,8},{11,9},{16,14},{17,15},{22,20},{23,21},{28,26},... | collective-permute-start | bytes 368648 | tf_op jit(solution)/shard_map/ppermute | solution.py:144
  95.7 48.6 %collective-permute-start.14 = (bf16[640,320]{0,1:T(8,128)(2,1)}, bf16[640,320]{0,1:T(8,128)(2,1)}, u32[]{:S(2)}, u32[]{:S(2)}) collective-permute-start(bf16[640,320]{0,1:T(8,128)(2,1)} %get-tuple-element.74), channel_id=1, source_target_pairs={{0,1},{1,0},{2,3},{3,2},{4,5},{5,4},{6,7},{7,6},{8,9},{9,8},{10,11... | collective-permute-start | bytes 1228808 | tf_op jit(solution)/shard_map/ppermute | solution.py:140
  102.3 27.8 %collective-permute-start.11 = (bf16[192,320]{1,0:T(8,128)(2,1)S(1)}, bf16[192,320]{1,0:T(8,128)(2,1)}, u32[]{:S(2)}, u32[]{:S(2)}) collective-permute-start(bf16[192,320]{1,0:T(8,128)(2,1)S(1)} %add_convert_fusion.7), channel_id=1, source_target_pairs={{2,0},{3,1},{8,6},{9,7},{14,12},{15,13},{20,18},{21,19},{26,24},{2... | collective-permute-start | bytes 368648 | tf_op jit(solution)/shard_map/ppermute | solution.py:144
  106.3 23.7 %copy-start.6 = (f32[192,320]{1,0:T(8,128)S(1)}, f32[192,320]{1,0:T(8,128)}, u32[]{:S(2)}) copy-start(f32[192,320]{1,0:T(8,128)} %copy-done.5) | copy-start | bytes 737284
  132.4 1.1 copy-start.17
  132.5 1.4 copy-start.34
  133.8 2.8 %copy-start.29 = (bf16[192,320]{1,0:T(8,128)(2,1)}, bf16[192,320]{1,0:T(8,128)(2,1)S(1)}, u32[]{:S(2)}) copy-start(bf16[192,320]{1,0:T(8,128)(2,1)S(1)} %add_convert_fusion.4) | copy-start | bytes 368644
  133.8 1.1 copy-start.10
  133.8 1.3 copy-start.15
  135.2 1.5 copy-start.1
  135.2 3.5 %copy-start.8 = (bf16[192,320]{1,0:T(8,128)(2,1)S(1)}, bf16[192,320]{1,0:T(8,128)(2,1)}, u32[]{:S(2)}) copy-start(bf16[192,320]{1,0:T(8,128)(2,1)} %copy-done.7) | copy-start | bytes 368644
  136.6 3.9 %copy-start.13 = (bf16[192,640]{1,0:T(8,128)(2,1)S(1)}, bf16[192,640]{1,0:T(8,128)(2,1)}, u32[]{:S(2)}) copy-start(bf16[192,640]{1,0:T(8,128)(2,1)} %copy-done.12) | copy-start | bytes 737284
  136.6 12.3 %collective-permute-start.13 = (bf16[640,320]{0,1:T(8,128)(2,1)}, bf16[640,320]{0,1:T(8,128)(2,1)}, u32[]{:S(2)}, u32[]{:S(2)}) collective-permute-start(bf16[640,320]{0,1:T(8,128)(2,1)} %get-tuple-element.86), channel_id=1, source_target_pairs={{0,1},{1,0},{2,3},{3,2},{4,5},{5,4},{6,7},{7,6},{8,9},{9,8},{10,11... | collective-permute-start | bytes 1228808 | tf_op jit(solution)/shard_map/ppermute | solution.py:140
  140.5 3.8 %copy-start = (f32[640,320]{0,1:T(8,128)S(1)}, f32[640,320]{0,1:T(8,128)}, u32[]{:S(2)}) copy-start(f32[640,320]{0,1:T(8,128)} %get-tuple-element.75) | copy-start | bytes 2457604
  141.9 10.8 %collective-permute-start.12 = (bf16[320,640]{1,0:T(8,128)(2,1)}, bf16[320,640]{1,0:T(8,128)(2,1)}, u32[]{:S(2)}, u32[]{:S(2)}) collective-permute-start(bf16[320,640]{1,0:T(8,128)(2,1)} %get-tuple-element.88), channel_id=1, source_target_pairs={{0,1},{1,0},{2,3},{3,2},{4,5},{5,4},{6,7},{7,6},{8,9},{9,8},{10,11... | collective-permute-start | bytes 1228808 | tf_op jit(solution)/shard_map/ppermute | solution.py:140
  144.3 4.6 %copy-start.2 = (f32[640,320]{0,1:T(8,128)S(1)}, f32[640,320]{0,1:T(8,128)}, u32[]{:S(2)}) copy-start(f32[640,320]{0,1:T(8,128)} %copy-done.1) | copy-start | bytes 2457604
  144.3 4.6 %copy-start.3 = (f32[640,320]{0,1:T(8,128)S(1)}, f32[640,320]{0,1:T(8,128)}, u32[]{:S(2)}) copy-start(f32[640,320]{0,1:T(8,128)} %get-tuple-element.87) | copy-start | bytes 2457604
  148.9 3.8 %copy-start.4 = (f32[320,640]{1,0:T(8,128)S(1)}, f32[320,640]{1,0:T(8,128)}, u32[]{:S(2)}) copy-start(f32[320,640]{1,0:T(8,128)} %get-tuple-element.89) | copy-start | bytes 2457604
  152.7 1.5 copy-start.11
  152.8 1.5 copy-start.14
  (5 other events, 3.9 us)

commit v6 on v5

--- a/solution.py
+++ b/solution.py
@@ -6,7 +6,7 @@
 from jax.sharding import Mesh, PartitionSpec as P
 
 DP = ("y", "x", "zl")
-SCATTER = ("x", "y", "zl")
+SCATTER = ("x", ("y", "zl"))
 
 
 def rows_product(left, right):
@@ -115,15 +115,19 @@
     return tuple(out)
 
 
+def axis_count(name):
+    return math.prod(lax.axis_size(part) for part in (name if isinstance(name, tuple) else (name,)))
+
+
 def scatter_sum(flat, name):
-    count = lax.axis_size(name)
+    count = axis_count(name)
     blocks = flat.astype(jnp.bfloat16).reshape(count, flat.shape[0] // count, flat.shape[1])
     got = lax.all_to_all(blocks, name, 0, 0, tiled=False)
     return jnp.sum(got.astype(jnp.float32), axis=0)
 
 
 def gather_all(flat, name):
-    count = lax.axis_size(name)
+    count = axis_count(name)
     blocks = jnp.broadcast_to(flat[None], (count,) + flat.shape)
     return lax.all_to_all(blocks, name, 0, 0, tiled=False).reshape(-1, flat.shape[1])
 

time: 265 us -> 258 us (0.974)
  blocking collectives: 103 us -> 96.2 us
    all_to_all x3 -> x2, blocking collectives: 63.4 us -> 56.6 us  [scatter_sum(): got = lax.all_to_all(blocks, name, 0, 0, tiled=False)]
    all_to_all x3 -> x2, blocking collectives: 39.4 us -> 39.5 us  [gather_all(): lax.all_to_all(blocks, name, 0, 0, tiled=False).reshape(-1, flat.shape[1])]
where the time goes in v6:
time: 258 us; the launch traced here: 257 us
  blocking collectives  96.2 us (37%)
  waiting for transfers between devices  53.8 us (21%)
  matrix products  37 us (14%)
  starting transfers between devices  35.6 us (14%)
  other arithmetic  16.5 us (6%)
  local copies, waits for them, and re-layouts  16 us (6%)
    all_to_all x2, blocking collectives, scatter_sum(): got = lax.all_to_all(blocks, name, 0, 0, tiled=False)  56.6 us
    ppermute x8, waiting for transfers between devices, hop(): return lax.ppermute(value, 'zh', [(source, target)])  53.7 us
    all_to_all x2, blocking collectives, gather_all(): lax.all_to_all(blocks, name, 0, 0, tiled=False).reshape(-1, flat.shape[1])  39.5 us
    ppermute x8, starting transfers between devices, hop(): return lax.ppermute(value, 'zh', [(source, target)])  18 us
    ppermute x8, starting transfers between devices, swap_core(): return lax.ppermute(value, 'core', [(0, 1), (1, 0)])  17.5 us
    dot_general x24, matrix products, rows_product(): lax.dot_general(left, right, (((0,), (0,)), ((), ())), preferred_element_...  16.1 us
    dot_general x22, matrix products, times_transposed(): lax.dot_general(left, right, (((1,), (1,)), ((), ())), preferred_element_...  8.7 us
    unnamed x79, local copies, waits for them, and re-layouts  6.97 us
  transfers between devices with their start and end apart: 16, of which 4 were waited for; matrix products, arithmetic and copies ran while one was open for 16% of the time, Pallas kernels for 0%

profile of v6, /device:TPU:2, one launch (start us, length us, event | category | flops | bytes accessed | tf_op | source)
XLA Modules:
  0.0 256.9 jit_solution(5082207822700611545)
XLA Ops:
  0.6 2.1 collective-permute-start.4
  2.7 2.4 collective-permute-start.1
  5.1 1.9 collective-permute-start
  7.0 2.4 collective-permute-start.5
  9.5 1.2 constant_dynamic-slice_fusion
  11.6 0.7 select_reduce_fusion
  12.5 0.8 multiply_sine_fusion
  13.7 1.4 broadcast_select_fusion.5
  16.4 10.9 %collective-permute-start.2 = (bf16[192,320]{1,0:T(8,128)(2,1)S(1)}, bf16[192,320]{1,0:T(8,128)(2,1)S(1)}, u32[]{:S(2)}, u32[]{:S(2)}) collective-permute-start(bf16[192,320]{1,0:T(8,128)(2,1)S(1)} %fusion.15), channel_id=1, source_target_pairs={{0,2},{1,3},{6,8},{7,9},{12,14},{13,15},{18,20},{19,21},{24,26},{2... | collective-permute-start | bytes 368648 | tf_op jit(solution)/shard_map/ppermute | solution.py:148
  27.3 1.7 broadcast_select_fusion.6
  29.0 1.5 collective-permute-done.2
  33.0 1.1 broadcast_select_fusion
  34.8 2.5 multiply_reduce_fusion.5
  37.3 1.7 fusion.26
  43.6 1.3 collective-permute-start.7
  45.2 27.9 %collective-permute-done.7 = bf16[192,320]{1,0:T(8,128)(2,1)S(1)} collective-permute-done((bf16[192,320]{1,0:T(8,128)(2,1)S(1)}, bf16[192,320]{1,0:T(8,128)(2,1)S(1)}, u32[]{:S(2)}, u32[]{:S(2)}) %collective-permute-start.7) | collective-permute-done | bytes 122912 | tf_op jit(solution)/shard_map/ppermute | solution.py:148
  77.5 1.6 collective-permute-start.8
  79.6 2.1 collective-permute-done.8
  89.3 1.9 collective-permute-start.15
  94.2 1.4 select_convert_fusion
  95.7 2.4 collective-permute-start.14
  100.8 1.3 convolution_select_fusion.6
  102.3 1.5 collective-permute-start.11
  103.8 1.3 convolution_select_fusion.4
  105.1 1.2 convolution_select_fusion.10
  106.7 1.0 reshape.220
  107.7 22.3 %collective-permute-done.11 = bf16[192,320]{1,0:T(8,128)(2,1)} collective-permute-done((bf16[192,320]{1,0:T(8,128)(2,1)S(1)}, bf16[192,320]{1,0:T(8,128)(2,1)}, u32[]{:S(2)}, u32[]{:S(2)}) %collective-permute-start.11) | collective-permute-done | bytes 122912 | tf_op jit(solution)/shard_map/ppermute | solution.py:148
  130.0 0.9 add_convert_fusion.6
  131.0 1.4 fusion.12
  135.2 1.5 select_convert_fusion.1
  136.7 2.0 collective-permute-start.13
  138.7 1.8 convolution_select_fusion.11
  140.5 1.4 select_convert_fusion.2
  141.9 2.4 collective-permute-start.12
  144.4 2.0 add_convert_fusion
  146.3 1.3 copy.23
  147.6 1.3 reshape.219
  149.0 1.9 add_convert_fusion.1
  150.9 1.3 copy.22
  152.8 1.2 add_convert_fusion.2
  154.4 24.0 %all_to_all.20 = bf16[4,1536,128]{2,1,0:T(8,128)(2,1)S(1)} all-to-all(bf16[4,1536,128]{2,1,0:T(8,128)(2,1)S(1)} %bitcast.119), channel_id=1, replica_groups=mesh['y'=8,'x'=4,'zl'=4,'zh'=3,'core'=2] {'x'}, dimensions={0} | all-to-all | bytes 3145728 | tf_op jit(solution)/shard_map/all_to_all | solution.py:125
  178.9 32.6 %all_to_all.21 = bf16[32,48,128]{2,1,0:T(8,128)(2,1)S(1)} all-to-all(bf16[32,48,128]{2,1,0:T(8,128)(2,1)S(1)} %bitcast.120), channel_id=1, replica_groups=mesh['y'=8,'x'=4,'zl'=4,'zh'=3,'core'=2] {'y','zl'}, dimensions={0} | all-to-all | bytes 786432 | tf_op jit(solution)/shard_map/all_to_all | solution.py:125
  211.6 18.6 %all_to_all.22 = bf16[32,48,128]{2,1,0:T(8,128)(2,1)S(1)} all-to-all(bf16[32,48,128]{2,1,0:T(8,128)(2,1)S(1)} %broadcast_in_dim.23), channel_id=1, replica_groups=mesh['y'=8,'x'=4,'zl'=4,'zh'=3,'core'=2] {'y','zl'}, dimensions={0} | all-to-all | bytes 786432 | tf_op jit(solution)/shard_map/all_to_all | solution.py:132
  230.4 20.9 %all_to_all.23 = bf16[4,1536,128]{2,1,0:T(8,128)(2,1)S(1)} all-to-all(bf16[4,1536,128]{2,1,0:T(8,128)(2,1)S(1)} %broadcast_in_dim.25), channel_id=1, replica_groups=mesh['y'=8,'x'=4,'zl'=4,'zh'=3,'core'=2] {'x'}, dimensions={0} | all-to-all | bytes 3145728 | tf_op jit(solution)/shard_map/all_to_all | solution.py:132
  251.8 1.1 broadcast_in_dim_reshape.13
  253.2 1.2 copy.24
  254.7 1.2 copy.25
  255.9 1.0 broadcast_in_dim_reshape.16
  (213 shorter events, 34.6 us)
Async XLA Ops:
  0.6 12.9 %copy-start.18 = (bf16[1,640,320]{1,2,0:T(8,128)(2,1)S(1)}, bf16[1,640,320]{1,2,0:T(8,128)(2,1)}, u32[]{:S(2)}) copy-start(bf16[1,640,320]{1,2,0:T(8,128)(2,1)} %param.12) | copy-start | bytes 1228804
  0.6 32.3 %collective-permute-start.4 = (bf16[640,320]{0,1:T(8,128)(2,1)}, bf16[640,320]{0,1:T(8,128)(2,1)}, u32[]{:S(2)}, u32[]{:S(2)}) collective-permute-start(bf16[640,320]{0,1:T(8,128)(2,1)} %bitcast.124), channel_id=1, source_target_pairs={{0,1},{1,0},{2,3},{3,2},{4,5},{5,4},{6,7},{7,6},{8,9},{9,8},{10,11... | collective-permute-start | bytes 1228808 | tf_op jit(solution)/shard_map/ppermute | solution.py:144
  2.7 10.8 %collective-permute-start.1 = (bf16[640,320]{0,1:T(8,128)(2,1)}, bf16[640,320]{0,1:T(8,128)(2,1)S(1)}, u32[]{:S(2)}, u32[]{:S(2)}) collective-permute-start(bf16[640,320]{0,1:T(8,128)(2,1)} %bitcast.122), channel_id=1, source_target_pairs={{0,1},{1,0},{2,3},{3,2},{4,5},{5,4},{6,7},{7,6},{8,9},{9,8},{10,11... | collective-permute-start | bytes 1228808 | tf_op jit(solution)/shard_map/ppermute | solution.py:144
  5.1 8.6 %collective-permute-start = (bf16[320,640]{1,0:T(8,128)(2,1)}, bf16[320,640]{1,0:T(8,128)(2,1)}, u32[]{:S(2)}, u32[]{:S(2)}) collective-permute-start(bf16[320,640]{1,0:T(8,128)(2,1)} %bitcast.123), channel_id=1, source_target_pairs={{0,1},{1,0},{2,3},{3,2},{4,5},{5,4},{6,7},{7,6},{8,9},{9,8},{10,11... | collective-permute-start | bytes 1228808 | tf_op jit(solution)/shard_map/ppermute | solution.py:144
  7.0 20.3 %collective-permute-start.5 = (bf16[320,320]{1,0:T(8,128)(2,1)}, bf16[320,320]{1,0:T(8,128)(2,1)}, u32[]{:S(2)}, u32[]{:S(2)}) collective-permute-start(bf16[320,320]{1,0:T(8,128)(2,1)} %bitcast.125), channel_id=1, source_target_pairs={{0,1},{1,0},{2,3},{3,2},{4,5},{5,4},{6,7},{7,6},{8,9},{9,8},{10,11... | collective-permute-start | bytes 614408 | tf_op jit(solution)/shard_map/ppermute | solution.py:144
  12.4 1.3 copy-start.19
  13.7 2.1 copy-start.23
  13.7 17.0 %copy-start.21 = (bf16[640,320]{0,1:T(8,128)(2,1)}, bf16[640,320]{0,1:T(8,128)(2,1)S(1)}, u32[]{:S(2)}) copy-start(bf16[640,320]{0,1:T(8,128)(2,1)S(1)} %get-tuple-element.32) | copy-start | bytes 1228804
  15.8 11.6 %copy-start.26 = (bf16[1,320,320]{2,1,0:T(8,128)(2,1)S(1)}, bf16[1,320,320]{2,1,0:T(8,128)(2,1)}, u32[]{:S(2)}) copy-start(bf16[1,320,320]{2,1,0:T(8,128)(2,1)} %param.14) | copy-start | bytes 614404
  16.4 14.3 %copy-start.30 = (bf16[192,320]{1,0:T(8,128)(2,1)}, bf16[192,320]{1,0:T(8,128)(2,1)S(1)}, u32[]{:S(2)}) copy-start(bf16[192,320]{1,0:T(8,128)(2,1)S(1)} %fusion.15) | copy-start | bytes 368644
  16.4 14.1 %collective-permute-start.2 = (bf16[192,320]{1,0:T(8,128)(2,1)S(1)}, bf16[192,320]{1,0:T(8,128)(2,1)S(1)}, u32[]{:S(2)}, u32[]{:S(2)}) collective-permute-start(bf16[192,320]{1,0:T(8,128)(2,1)S(1)} %fusion.15), channel_id=1, source_target_pairs={{0,2},{1,3},{6,8},{7,9},{12,14},{13,15},{18,20},{19,21},{24,26},{2... | collective-permute-start | bytes 368648 | tf_op jit(solution)/shard_map/ppermute | solution.py:148
  30.7 1.0 copy-start.24
  31.7 1.3 copy-start.20
  32.3 1.8 copy-start.32
  32.3 1.8 collective-permute-start.3
  34.8 2.5 copy-start.31
  34.8 2.5 copy-start.33
  40.7 1.2 collective-permute-start.6
  41.8 62.0 %copy-start.9 = (f32[192,640]{1,0:T(8,128)}, f32[192,640]{1,0:T(8,128)S(1)}, u32[]{:S(2)}) copy-start(f32[192,640]{1,0:T(8,128)S(1)} %fusion.110) | copy-start | bytes 1474564
  41.9 63.2 %copy-start.7 = (bf16[192,320]{1,0:T(8,128)(2,1)}, bf16[192,320]{1,0:T(8,128)(2,1)S(1)}, u32[]{:S(2)}) copy-start(bf16[192,320]{1,0:T(8,128)(2,1)S(1)} %multiply_convert_fusion.32) | copy-start | bytes 368644
  43.6 29.5 %collective-permute-start.7 = (bf16[192,320]{1,0:T(8,128)(2,1)S(1)}, bf16[192,320]{1,0:T(8,128)(2,1)S(1)}, u32[]{:S(2)}, u32[]{:S(2)}) collective-permute-start(bf16[192,320]{1,0:T(8,128)(2,1)S(1)} %fusion.23), channel_id=1, source_target_pairs={{2,0},{3,1},{8,6},{9,7},{14,12},{15,13},{20,18},{21,19},{26,24},{2... | collective-permute-start | bytes 368648 | tf_op jit(solution)/shard_map/ppermute | solution.py:148
  45.2 55.6 %copy-start.16 = (f32[192,640]{1,0:T(8,128)}, f32[192,640]{1,0:T(8,128)S(1)}, u32[]{:S(2)}) copy-start(f32[192,640]{1,0:T(8,128)S(1)} %fusion.111) | copy-start | bytes 1474564
  77.5 4.1 %collective-permute-start.8 = (bf16[192,320]{1,0:T(8,128)(2,1)S(1)}, bf16[192,320]{1,0:T(8,128)(2,1)S(1)}, u32[]{:S(2)}, u32[]{:S(2)}) collective-permute-start(bf16[192,320]{1,0:T(8,128)(2,1)S(1)} %slice.121), channel_id=1, source_target_pairs={{0,2},{1,3},{6,8},{7,9},{12,14},{13,15},{18,20},{19,21},{24,26},{2... | collective-permute-start | bytes 368648 | tf_op jit(solution)/shard_map/ppermute | solution.py:148
  83.3 1.9 collective-permute-start.9
  86.9 1.0 copy-start.25
  87.8 10.3 %copy-start.5 = (f32[192,320]{1,0:T(8,128)}, f32[192,320]{1,0:T(8,128)S(1)}, u32[]{:S(2)}) copy-start(f32[192,320]{1,0:T(8,128)S(1)} %get-tuple-element.21) | copy-start | bytes 737284
  89.3 17.4 %collective-permute-start.15 = (bf16[320,320]{1,0:T(8,128)(2,1)S(1)}, bf16[320,320]{1,0:T(8,128)(2,1)S(1)}, u32[]{:S(2)}, u32[]{:S(2)}) collective-permute-start(bf16[320,320]{1,0:T(8,128)(2,1)S(1)} %get-tuple-element.72), channel_id=1, source_target_pairs={{0,1},{1,0},{2,3},{3,2},{4,5},{5,4},{6,7},{7,6},{8,9},{9,8},{10,11... | collective-permute-start | bytes 614408 | tf_op jit(solution)/shard_map/ppermute | solution.py:144
  91.7 1.0 copy-start.22
  93.6 4.5 %collective-permute-start.10 = (bf16[192,320]{1,0:T(8,128)(2,1)S(1)}, bf16[192,320]{1,0:T(8,128)(2,1)S(1)}, u32[]{:S(2)}, u32[]{:S(2)}) collective-permute-start(bf16[192,320]{1,0:T(8,128)(2,1)S(1)} %add_convert_fusion.11), channel_id=1, source_target_pairs={{4,2},{5,3},{10,8},{11,9},{16,14},{17,15},{22,20},{23,21},{28,26},... | collective-permute-start | bytes 368648 | tf_op jit(solution)/shard_map/ppermute | solution.py:148
  95.7 48.7 %collective-permute-start.14 = (bf16[640,320]{0,1:T(8,128)(2,1)}, bf16[640,320]{0,1:T(8,128)(2,1)}, u32[]{:S(2)}, u32[]{:S(2)}) collective-permute-start(bf16[640,320]{0,1:T(8,128)(2,1)} %get-tuple-element.74), channel_id=1, source_target_pairs={{0,1},{1,0},{2,3},{3,2},{4,5},{5,4},{6,7},{7,6},{8,9},{9,8},{10,11... | collective-permute-start | bytes 1228808 | tf_op jit(solution)/shard_map/ppermute | solution.py:144
  102.3 27.8 %collective-permute-start.11 = (bf16[192,320]{1,0:T(8,128)(2,1)S(1)}, bf16[192,320]{1,0:T(8,128)(2,1)}, u32[]{:S(2)}, u32[]{:S(2)}) collective-permute-start(bf16[192,320]{1,0:T(8,128)(2,1)S(1)} %add_convert_fusion.7), channel_id=1, source_target_pairs={{2,0},{3,1},{8,6},{9,7},{14,12},{15,13},{20,18},{21,19},{26,24},{2... | collective-permute-start | bytes 368648 | tf_op jit(solution)/shard_map/ppermute | solution.py:148
  106.3 23.7 %copy-start.6 = (f32[192,320]{1,0:T(8,128)S(1)}, f32[192,320]{1,0:T(8,128)}, u32[]{:S(2)}) copy-start(f32[192,320]{1,0:T(8,128)} %copy-done.5) | copy-start | bytes 737284
  132.4 1.1 copy-start.17
  132.5 1.4 copy-start.34
  133.8 2.8 %copy-start.29 = (bf16[192,320]{1,0:T(8,128)(2,1)}, bf16[192,320]{1,0:T(8,128)(2,1)S(1)}, u32[]{:S(2)}) copy-start(bf16[192,320]{1,0:T(8,128)(2,1)S(1)} %add_convert_fusion.4) | copy-start | bytes 368644
  133.8 1.1 copy-start.10
  133.8 1.3 copy-start.15
  135.2 1.5 copy-start.1
  135.2 3.5 %copy-start.8 = (bf16[192,320]{1,0:T(8,128)(2,1)S(1)}, bf16[192,320]{1,0:T(8,128)(2,1)}, u32[]{:S(2)}) copy-start(bf16[192,320]{1,0:T(8,128)(2,1)} %copy-done.7) | copy-start | bytes 368644
  136.7 3.9 %copy-start.13 = (bf16[192,640]{1,0:T(8,128)(2,1)S(1)}, bf16[192,640]{1,0:T(8,128)(2,1)}, u32[]{:S(2)}) copy-start(bf16[192,640]{1,0:T(8,128)(2,1)} %copy-done.12) | copy-start | bytes 737284
  136.7 12.3 %collective-permute-start.13 = (bf16[640,320]{0,1:T(8,128)(2,1)}, bf16[640,320]{0,1:T(8,128)(2,1)}, u32[]{:S(2)}, u32[]{:S(2)}) collective-permute-start(bf16[640,320]{0,1:T(8,128)(2,1)} %get-tuple-element.86), channel_id=1, source_target_pairs={{0,1},{1,0},{2,3},{3,2},{4,5},{5,4},{6,7},{7,6},{8,9},{9,8},{10,11... | collective-permute-start | bytes 1228808 | tf_op jit(solution)/shard_map/ppermute | solution.py:144
  140.5 3.8 %copy-start = (f32[640,320]{0,1:T(8,128)S(1)}, f32[640,320]{0,1:T(8,128)}, u32[]{:S(2)}) copy-start(f32[640,320]{0,1:T(8,128)} %get-tuple-element.75) | copy-start | bytes 2457604
  141.9 10.8 %collective-permute-start.12 = (bf16[320,640]{1,0:T(8,128)(2,1)}, bf16[320,640]{1,0:T(8,128)(2,1)}, u32[]{:S(2)}, u32[]{:S(2)}) collective-permute-start(bf16[320,640]{1,0:T(8,128)(2,1)} %get-tuple-element.88), channel_id=1, source_target_pairs={{0,1},{1,0},{2,3},{3,2},{4,5},{5,4},{6,7},{7,6},{8,9},{9,8},{10,11... | collective-permute-start | bytes 1228808 | tf_op jit(solution)/shard_map/ppermute | solution.py:144
  144.3 4.6 %copy-start.2 = (f32[640,320]{0,1:T(8,128)S(1)}, f32[640,320]{0,1:T(8,128)}, u32[]{:S(2)}) copy-start(f32[640,320]{0,1:T(8,128)} %copy-done.1) | copy-start | bytes 2457604
  144.3 4.6 %copy-start.3 = (f32[640,320]{0,1:T(8,128)S(1)}, f32[640,320]{0,1:T(8,128)}, u32[]{:S(2)}) copy-start(f32[640,320]{0,1:T(8,128)} %get-tuple-element.87) | copy-start | bytes 2457604
  148.9 3.8 %copy-start.4 = (f32[320,640]{1,0:T(8,128)S(1)}, f32[320,640]{1,0:T(8,128)}, u32[]{:S(2)}) copy-start(f32[320,640]{1,0:T(8,128)} %get-tuple-element.89) | copy-start | bytes 2457604
  152.8 1.5 copy-start.11
  152.8 1.5 copy-start.14
  (5 other events, 3.9 us)

commit v7 on v6

--- a/solution.py
+++ b/solution.py
@@ -94,12 +94,13 @@
     return (d_joined[:, :width].astype(jnp.bfloat16), d_joined[:, width:], grad_mix, grad_up)
 
 
-def reduce_replicas(parts):
-    total = sum(part.size for part in parts)
+def reduce_replicas(parts, tail, tail_shapes):
+    shapes = [part.shape for part in parts] + list(tail_shapes)
+    total = sum(math.prod(shape) for shape in shapes)
     groups = math.prod(lax.axis_size(name) for name in DP)
     lanes = 128
     length = -(-total // (lanes * groups * 8)) * groups * 8
-    flat = jnp.concatenate([part.reshape(-1) for part in parts])
+    flat = jnp.concatenate([part.reshape(-1) for part in parts] + [tail])
     flat = jnp.pad(flat, (0, length * lanes - total)).reshape(length, lanes)
     for name in SCATTER:
         flat = scatter_sum(flat, name)
@@ -109,9 +110,9 @@
     flat = flat.astype(jnp.float32) * (1.0 / groups)
     flat = flat.reshape(-1)
     out, start = [], 0
-    for part in parts:
-        out.append(flat[start : start + part.size].reshape(part.shape))
-        start += part.size
+    for shape in shapes:
+        out.append(flat[start : start + math.prod(shape)].reshape(shape))
+        start += math.prod(shape)
     return tuple(out)
 
 
@@ -166,7 +167,6 @@
         return (jnp.where(first, own, other), jnp.where(first, other, own))
 
     in_pair, out_pair = pair(w_in), pair(w_out)
-    mix_pair, up_pair = pair(w_mix), pair(w_up)
 
     offset = core * rows
     match = clip_of_row[0][:, None] == jnp.arange(timestep.shape[1], dtype=jnp.int32)[None, :]
@@ -188,6 +188,9 @@
         hidden = down_forward(upper, embedding, in_pair[1], out_pair[1])
         down_in = [keep(valid, lower, down_in[0]), keep(valid, upper, down_in[1])]
         skip = [keep(valid, upper, skip[0]), keep(valid, hidden, skip[1])]
+        if tick == 0:
+            w_mix, w_up, hidden = lax.optimization_barrier((w_mix, w_up, hidden))
+            mix_pair, up_pair = pair(w_mix), pair(w_up)
 
     up_in = [None, None]
     below = skip[1]
@@ -220,6 +223,9 @@
         return mine + swap_core(theirs.astype(jnp.bfloat16)).astype(jnp.float32)
 
 
+    up_flat = jnp.concatenate(
+        [combine(grad_mix).reshape(-1), combine(grad_up).reshape(-1)]
+    )
     grad_in = [None, None]
     grad_out = [None, None]
     carry = cotan
@@ -227,6 +233,8 @@
         owner = stages - 1 - tick
         if tick > 0:
             carry = hop(carry, owner + 1, owner)
+        if tick == 1:
+            carry, up_flat = lax.optimization_barrier((carry, up_flat))
         valid = stage == owner
         upper_c = (d_skip[1] + carry.astype(jnp.float32)).astype(jnp.bfloat16)
         upper_d, in1, out1 = down_backward(down_in[1], embedding, in_pair[1], out_pair[1], upper_c)
@@ -236,7 +244,7 @@
         grad_out = [keep(valid, out0, grad_out[0]), keep(valid, out1, grad_out[1])]
 
     total_in, total_out, total_mix, total_up = reduce_replicas(
-        (combine(grad_in), combine(grad_out), combine(grad_mix), combine(grad_up))
+        (combine(grad_in), combine(grad_out)), up_flat, (grad_mix[0].shape, grad_up[0].shape)
     )
     return (total_in[None], total_out[None], total_mix[None], total_up[None])
 

time: 258 us -> 253 us (0.981)
  waiting for transfers between devices: 53.8 us -> 45 us
    ppermute x8, waiting for transfers between devices: 53.7 us -> 43.7 us  [hop(): return lax.ppermute(value, 'zh', [(source, target)])]
    another operation x4 -> x2, other arithmetic: 5.14 us -> 1.27 us
    add x0 -> x2, other arithmetic: none -> 2.64 us  [combine(): return mine + swap_core(theirs.astype(jnp.bfloat16)).astype(jnp.float32)]
    unnamed x79 -> x83, local copies, waits for them, and re-layouts: 6.97 us -> 7.33 us
  transfers between devices with their start and end apart: 16 -> 16, of which waited for: 4 -> 4; matrix products, arithmetic and copies ran while one was open for 16% -> 13% of each run, Pallas kernels for 0% -> 0%
where the time goes in v7:
time: 253 us; the launch traced here: 251 us
  blocking collectives  98.1 us (39%)
  waiting for transfers between devices  45 us (18%)
  starting transfers between devices  36.4 us (14%)
  matrix products  35.7 us (14%)
  other arithmetic  17.4 us (7%)
  local copies, waits for them, and re-layouts  17.1 us (7%)
    all_to_all x2, blocking collectives, scatter_sum(): got = lax.all_to_all(blocks, name, 0, 0, tiled=False)  57.6 us
    ppermute x8, waiting for transfers between devices, hop(): return lax.ppermute(value, 'zh', [(source, target)])  43.7 us
    all_to_all x2, blocking collectives, gather_all(): lax.all_to_all(blocks, name, 0, 0, tiled=False).reshape(-1, flat.shape[1])  40.5 us
    ppermute x8, starting transfers between devices, hop(): return lax.ppermute(value, 'zh', [(source, target)])  18.8 us
    ppermute x8, starting transfers between devices, swap_core(): return lax.ppermute(value, 'core', [(0, 1), (1, 0)])  17.6 us
    dot_general x24, matrix products, rows_product(): lax.dot_general(left, right, (((0,), (0,)), ((), ())), preferred_element_...  14.3 us
    dot_general x22, matrix products, times_transposed(): lax.dot_general(left, right, (((1,), (1,)), ((), ())), preferred_element_...  7.58 us
    dot_general x6, matrix products, down_forward(): jnp.dot(gated, out_matrix, preferred_element_type=jnp.float32)  7.42 us
  transfers between devices with their start and end apart: 16, of which 4 were waited for; matrix products, arithmetic and copies ran while one was open for 13% of the time, Pallas kernels for 0%

profile of v7, /device:TPU:2, one launch (start us, length us, event | category | flops | bytes accessed | tf_op | source)
XLA Modules:
  0.0 251.4 jit_solution(10410435750944865765)
XLA Ops:
  0.6 2.1 collective-permute-start
  2.7 2.4 collective-permute-start.1
  5.1 1.2 constant_dynamic-slice_fusion
  9.2 1.1 broadcast_select_fusion.3
  11.6 1.2 fusion.13
  12.9 10.9 %collective-permute-start.2 = (bf16[192,320]{1,0:T(8,128)(2,1)}, bf16[192,320]{1,0:T(8,128)(2,1)S(1)}, u32[]{:S(2)}, u32[]{:S(2)}) collective-permute-start(bf16[192,320]{1,0:T(8,128)(2,1)} %fusion.13), channel_id=1, source_target_pairs={{0,2},{1,3},{6,8},{7,9},{12,14},{13,15},{18,20},{19,21},{24,26},{2... | collective-permute-start | bytes 368648 | tf_op jit(solution)/shard_map/ppermute | solution.py:149
  24.0 1.9 collective-permute-start.5
  25.9 2.4 collective-permute-start.4
  29.8 1.6 fusion.15
  32.1 0.8 broadcast_select_fusion.6
  33.1 1.7 multiply_reduce_fusion.5
  35.0 1.1 fusion.108
  36.0 1.6 fusion.24
  37.7 1.1 broadcast_select_fusion.1
  43.0 1.3 collective-permute-start.7
  44.6 26.3 %collective-permute-done.7 = bf16[192,320]{1,0:T(8,128)(2,1)S(1)} collective-permute-done((bf16[192,320]{1,0:T(8,128)(2,1)S(1)}, bf16[192,320]{1,0:T(8,128)(2,1)S(1)}, u32[]{:S(2)}, u32[]{:S(2)}) %collective-permute-start.7) | collective-permute-done | bytes 122912 | tf_op jit(solution)/shard_map/ppermute | solution.py:149
  75.4 1.6 collective-permute-start.8
  77.4 2.1 collective-permute-done.8
  85.7 1.2 select_convert_fusion.2
  86.9 1.9 collective-permute-start.11
  89.5 2.4 collective-permute-start.12
  93.0 1.1 add_convert_fusion.10
  95.7 1.3 collective-permute-start.10
  97.8 1.9 reshape.216
  99.7 1.9 convert_add_fusion
  101.6 1.3 copy.22
  102.9 1.3 reshape.215
  104.2 1.9 pad_maximum_fusion
  106.1 0.9 add_convert_fusion.8
  112.2 1.6 collective-permute-start.13
  113.9 1.3 convolution_select_fusion
  115.2 1.3 convolution_select_fusion.2
  116.5 1.2 convolution_select_fusion.6
  117.7 15.3 %collective-permute-done.13 = bf16[192,320]{1,0:T(8,128)(2,1)S(1)} collective-permute-done((bf16[192,320]{1,0:T(8,128)(2,1)S(1)}, bf16[192,320]{1,0:T(8,128)(2,1)S(1)}, u32[]{:S(2)}, u32[]{:S(2)}) %collective-permute-start.13) | collective-permute-done | bytes 122912 | tf_op jit(solution)/shard_map/ppermute | solution.py:149
  134.4 1.6 convolution_select_fusion.7
  136.3 2.1 collective-permute-start.14
  138.8 1.2 select_convert_fusion
  140.0 2.4 collective-permute-start.15
  142.8 1.3 collective-permute-done.15
  144.1 1.2 add_convert_fusion
  146.3 24.4 %all_to_all.20 = bf16[4,1536,128]{2,1,0:T(8,128)(2,1)S(1)} all-to-all(bf16[4,1536,128]{2,1,0:T(8,128)(2,1)S(1)} %bitcast.119), channel_id=1, replica_groups=mesh['y'=8,'x'=4,'zl'=4,'zh'=3,'core'=2] {'x'}, dimensions={0} | all-to-all | bytes 3145728 | tf_op jit(solution)/shard_map/all_to_all | solution.py:126
  171.1 33.2 %all_to_all.21 = bf16[32,48,128]{2,1,0:T(8,128)(2,1)S(1)} all-to-all(bf16[32,48,128]{2,1,0:T(8,128)(2,1)S(1)} %bitcast.120), channel_id=1, replica_groups=mesh['y'=8,'x'=4,'zl'=4,'zh'=3,'core'=2] {'y','zl'}, dimensions={0} | all-to-all | bytes 786432 | tf_op jit(solution)/shard_map/all_to_all | solution.py:126
  204.5 19.0 %all_to_all.22 = bf16[32,48,128]{2,1,0:T(8,128)(2,1)S(1)} all-to-all(bf16[32,48,128]{2,1,0:T(8,128)(2,1)S(1)} %broadcast_in_dim.23), channel_id=1, replica_groups=mesh['y'=8,'x'=4,'zl'=4,'zh'=3,'core'=2] {'y','zl'}, dimensions={0} | all-to-all | bytes 786432 | tf_op jit(solution)/shard_map/all_to_all | solution.py:133
  223.6 21.5 %all_to_all.23 = bf16[4,1536,128]{2,1,0:T(8,128)(2,1)S(1)} all-to-all(bf16[4,1536,128]{2,1,0:T(8,128)(2,1)S(1)} %broadcast_in_dim.25), channel_id=1, replica_groups=mesh['y'=8,'x'=4,'zl'=4,'zh'=3,'core'=2] {'x'}, dimensions={0} | all-to-all | bytes 3145728 | tf_op jit(solution)/shard_map/all_to_all | solution.py:133
  246.6 1.2 copy.24
  248.2 1.2 copy.25
  249.4 1.1 broadcast_in_dim_reshape.13
  250.5 1.0 broadcast_in_dim_reshape.16
  (218 shorter events, 37.1 us)
Async XLA Ops:
  0.6 8.4 %copy-start.22 = (bf16[1,320,640]{2,1,0:T(8,128)(2,1)S(1)}, bf16[1,320,640]{2,1,0:T(8,128)(2,1)}, u32[]{:S(2)}) copy-start(bf16[1,320,640]{2,1,0:T(8,128)(2,1)} %param.11) | copy-start | bytes 1228804
  0.6 8.4 %collective-permute-start = (bf16[320,640]{1,0:T(8,128)(2,1)}, bf16[320,640]{1,0:T(8,128)(2,1)S(1)}, u32[]{:S(2)}, u32[]{:S(2)}) collective-permute-start(bf16[320,640]{1,0:T(8,128)(2,1)} %bitcast.122), channel_id=1, source_target_pairs={{0,1},{1,0},{2,3},{3,2},{4,5},{5,4},{6,7},{7,6},{8,9},{9,8},{10,11... | collective-permute-start | bytes 1228808 | tf_op jit(solution)/shard_map/ppermute | solution.py:145
  2.7 6.5 %collective-permute-start.1 = (bf16[640,320]{0,1:T(8,128)(2,1)}, bf16[640,320]{0,1:T(8,128)(2,1)}, u32[]{:S(2)}, u32[]{:S(2)}) collective-permute-start(bf16[640,320]{0,1:T(8,128)(2,1)} %bitcast.123), channel_id=1, source_target_pairs={{0,1},{1,0},{2,3},{3,2},{4,5},{5,4},{6,7},{7,6},{8,9},{9,8},{10,11... | collective-permute-start | bytes 1228808 | tf_op jit(solution)/shard_map/ppermute | solution.py:145
  6.4 2.8 %copy-start.23 = (bf16[1,640,320]{1,2,0:T(8,128)(2,1)S(1)}, bf16[1,640,320]{1,2,0:T(8,128)(2,1)}, u32[]{:S(2)}) copy-start(bf16[1,640,320]{1,2,0:T(8,128)(2,1)} %param.12) | copy-start | bytes 1228804
  10.3 22.8 %copy-start.25 = (bf16[640,320]{0,1:T(8,128)(2,1)}, bf16[640,320]{0,1:T(8,128)(2,1)S(1)}, u32[]{:S(2)}) copy-start(bf16[640,320]{0,1:T(8,128)(2,1)S(1)} %get-tuple-element.42) | copy-start | bytes 1228804
  11.6 12.3 %copy-start.31 = (bf16[1,320,320]{2,1,0:T(8,128)(2,1)S(1)}, bf16[1,320,320]{2,1,0:T(8,128)(2,1)}, u32[]{:S(2)}) copy-start(bf16[1,320,320]{2,1,0:T(8,128)(2,1)} %param.14) | copy-start | bytes 614404
  11.6 14.2 %copy-start.24 = (bf16[1,640,320]{1,2,0:T(8,128)(2,1)S(1)}, bf16[1,640,320]{1,2,0:T(8,128)(2,1)}, u32[]{:S(2)}) copy-start(bf16[1,640,320]{1,2,0:T(8,128)(2,1)} %param.13) | copy-start | bytes 1228804
  12.9 15.4 %collective-permute-start.2 = (bf16[192,320]{1,0:T(8,128)(2,1)}, bf16[192,320]{1,0:T(8,128)(2,1)S(1)}, u32[]{:S(2)}, u32[]{:S(2)}) collective-permute-start(bf16[192,320]{1,0:T(8,128)(2,1)} %fusion.13), channel_id=1, source_target_pairs={{0,2},{1,3},{6,8},{7,9},{12,14},{13,15},{18,20},{19,21},{24,26},{2... | collective-permute-start | bytes 368648 | tf_op jit(solution)/shard_map/ppermute | solution.py:149
  24.0 8.1 %collective-permute-start.5 = (bf16[320,320]{1,0:T(8,128)(2,1)S(1)}, bf16[320,320]{1,0:T(8,128)(2,1)S(1)}, u32[]{:S(2)}, u32[]{:S(2)}) collective-permute-start(bf16[320,320]{1,0:T(8,128)(2,1)S(1)} %bitcast.125), channel_id=1, source_target_pairs={{0,1},{1,0},{2,3},{3,2},{4,5},{5,4},{6,7},{7,6},{8,9},{9,8},{10,11... | collective-permute-start | bytes 614408 | tf_op jit(solution)/shard_map/ppermute | solution.py:145
  25.9 11.8 %collective-permute-start.4 = (bf16[640,320]{0,1:T(8,128)(2,1)S(1)}, bf16[640,320]{0,1:T(8,128)(2,1)}, u32[]{:S(2)}, u32[]{:S(2)}) collective-permute-start(bf16[640,320]{0,1:T(8,128)(2,1)S(1)} %bitcast.124), channel_id=1, source_target_pairs={{0,1},{1,0},{2,3},{3,2},{4,5},{5,4},{6,7},{7,6},{8,9},{9,8},{10,11... | collective-permute-start | bytes 1228808 | tf_op jit(solution)/shard_map/ppermute | solution.py:145
  31.4 1.7 copy-start.34
  31.4 1.5 collective-permute-start.3
  34.8 1.2 copy-start.35
  37.6 1.7 copy-start.32
  39.3 1.0 copy-start.33
  40.6 0.8 collective-permute-start.6
  41.3 3.0 %copy-start.2 = (bf16[192,320]{1,0:T(8,128)(2,1)}, bf16[192,320]{1,0:T(8,128)(2,1)S(1)}, u32[]{:S(2)}) copy-start(bf16[192,320]{1,0:T(8,128)(2,1)S(1)} %multiply_convert_fusion.32) | copy-start | bytes 368644
  43.0 27.9 %collective-permute-start.7 = (bf16[192,320]{1,0:T(8,128)(2,1)S(1)}, bf16[192,320]{1,0:T(8,128)(2,1)S(1)}, u32[]{:S(2)}, u32[]{:S(2)}) collective-permute-start(bf16[192,320]{1,0:T(8,128)(2,1)S(1)} %fusion.21), channel_id=1, source_target_pairs={{2,0},{3,1},{8,6},{9,7},{14,12},{15,13},{20,18},{21,19},{26,24},{2... | collective-permute-start | bytes 368648 | tf_op jit(solution)/shard_map/ppermute | solution.py:149
  44.6 49.5 %copy-start.19 = (f32[192,640]{1,0:T(8,128)}, f32[192,640]{1,0:T(8,128)S(1)}, u32[]{:S(2)}) copy-start(f32[192,640]{1,0:T(8,128)S(1)} %fusion.109) | copy-start | bytes 1474564
  75.4 4.1 %collective-permute-start.8 = (bf16[192,320]{1,0:T(8,128)(2,1)S(1)}, bf16[192,320]{1,0:T(8,128)(2,1)S(1)}, u32[]{:S(2)}, u32[]{:S(2)}) collective-permute-start(bf16[192,320]{1,0:T(8,128)(2,1)S(1)} %slice.121), channel_id=1, source_target_pairs={{0,2},{1,3},{6,8},{7,9},{12,14},{13,15},{18,20},{19,21},{24,26},{2... | collective-permute-start | bytes 368648 | tf_op jit(solution)/shard_map/ppermute | solution.py:149
  82.0 1.4 collective-permute-start.9
  86.9 12.9 %collective-permute-start.11 = (bf16[640,320]{0,1:T(8,128)(2,1)}, bf16[640,320]{0,1:T(8,128)(2,1)}, u32[]{:S(2)}, u32[]{:S(2)}) collective-permute-start(bf16[640,320]{0,1:T(8,128)(2,1)} %get-tuple-element.87), channel_id=1, source_target_pairs={{0,1},{1,0},{2,3},{3,2},{4,5},{5,4},{6,7},{7,6},{8,9},{9,8},{10,11... | collective-permute-start | bytes 1228808 | tf_op jit(solution)/shard_map/ppermute | solution.py:145
  89.2 3.0 %copy-start.4 = (f32[192,640]{1,0:T(8,128)S(1)}, f32[192,640]{1,0:T(8,128)}, u32[]{:S(2)}) copy-start(f32[192,640]{1,0:T(8,128)} %fusion.108) | copy-start | bytes 1474564
  89.2 3.0 %copy-start.29 = (bf16[640,320]{0,1:T(8,128)(2,1)S(1)}, bf16[640,320]{0,1:T(8,128)(2,1)}, u32[]{:S(2)}) copy-start(bf16[640,320]{0,1:T(8,128)(2,1)} %copy-done.28) | copy-start | bytes 1228804
  89.5 7.5 %collective-permute-start.12 = (bf16[320,320]{1,0:T(8,128)(2,1)S(1)}, bf16[320,320]{1,0:T(8,128)(2,1)S(1)}, u32[]{:S(2)}, u32[]{:S(2)}) collective-permute-start(bf16[320,320]{1,0:T(8,128)(2,1)S(1)} %get-tuple-element.85), channel_id=1, source_target_pairs={{0,1},{1,0},{2,3},{3,2},{4,5},{5,4},{6,7},{7,6},{8,9},{9,8},{10,11... | collective-permute-start | bytes 614408 | tf_op jit(solution)/shard_map/ppermute | solution.py:145
  92.6 1.5 copy-start.11
  92.6 1.5 copy-start.26
  94.4 1.3 copy-start.9
  95.7 10.5 %collective-permute-start.10 = (bf16[192,320]{1,0:T(8,128)(2,1)}, bf16[192,320]{1,0:T(8,128)(2,1)}, u32[]{:S(2)}, u32[]{:S(2)}) collective-permute-start(bf16[192,320]{1,0:T(8,128)(2,1)} %add_convert_fusion.9), channel_id=1, source_target_pairs={{4,2},{5,3},{10,8},{11,9},{16,14},{17,15},{22,20},{23,21},{28,26},... | collective-permute-start | bytes 368648 | tf_op jit(solution)/shard_map/ppermute | solution.py:149
  101.6 2.7 %copy-start.13 = (bf16[102400]{0:T(1024)(128)(2,1)S(1)}, bf16[102400]{0:T(1024)(128)(2,1)}, u32[]{:S(2)}) copy-start(bf16[102400]{0:T(1024)(128)(2,1)} %reshape.216) | copy-start | bytes 614404
  102.9 4.2 %copy-start.5 = (f32[192,640]{1,0:T(8,128)S(1)}, f32[192,640]{1,0:T(8,128)}, u32[]{:S(2)}) copy-start(f32[192,640]{1,0:T(8,128)} %fusion.108) | copy-start | bytes 1474564
  104.2 2.9 %copy-start.30 = (bf16[640,320]{0,1:T(8,128)(2,1)S(1)}, bf16[640,320]{0,1:T(8,128)(2,1)}, u32[]{:S(2)}) copy-start(bf16[640,320]{0,1:T(8,128)(2,1)} %copy-done.28) | copy-start | bytes 1228804
  107.4 1.0 copy-start
  107.4 1.1 copy-start.20
  107.4 1.2 copy-start.27
  111.7 2.2 copy-start.6
  111.7 2.2 copy-start.16
  112.2 3.0 %copy-start.18 = (bf16[192,320]{1,0:T(8,128)(2,1)S(1)}, bf16[192,320]{1,0:T(8,128)(2,1)}, u32[]{:S(2)}) copy-start(bf16[192,320]{1,0:T(8,128)(2,1)} %copy-done.17) | copy-start | bytes 368644
  112.2 20.8 %collective-permute-start.13 = (bf16[192,320]{1,0:T(8,128)(2,1)S(1)}, bf16[192,320]{1,0:T(8,128)(2,1)S(1)}, u32[]{:S(2)}, u32[]{:S(2)}) collective-permute-start(bf16[192,320]{1,0:T(8,128)(2,1)S(1)} %add_convert_fusion.5), channel_id=1, source_target_pairs={{2,0},{3,1},{8,6},{9,7},{14,12},{15,13},{20,18},{21,19},{26,24},{2... | collective-permute-start | bytes 368648 | tf_op jit(solution)/shard_map/ppermute | solution.py:149
  115.2 1.3 copy-start.10
  133.4 1.0 copy-start.21
  136.0 2.4 copy-start.36
  136.3 2.5 copy-start.7
  136.3 2.5 copy-start.14
  136.3 6.1 %collective-permute-start.14 = (bf16[320,640]{1,0:T(8,128)(2,1)S(1)}, bf16[320,640]{1,0:T(8,128)(2,1)S(1)}, u32[]{:S(2)}, u32[]{:S(2)}) collective-permute-start(bf16[320,640]{1,0:T(8,128)(2,1)S(1)} %get-tuple-element.97), channel_id=1, source_target_pairs={{0,1},{1,0},{2,3},{3,2},{4,5},{5,4},{6,7},{7,6},{8,9},{9,8},{10,11... | collective-permute-start | bytes 1228808 | tf_op jit(solution)/shard_map/ppermute | solution.py:145
  140.0 4.1 %collective-permute-start.15 = (bf16[640,320]{0,1:T(8,128)(2,1)}, bf16[640,320]{0,1:T(8,128)(2,1)}, u32[]{:S(2)}, u32[]{:S(2)}) collective-permute-start(bf16[640,320]{0,1:T(8,128)(2,1)} %get-tuple-element.95), channel_id=1, source_target_pairs={{0,1},{1,0},{2,3},{3,2},{4,5},{5,4},{6,7},{7,6},{8,9},{9,8},{10,11... | collective-permute-start | bytes 1228808 | tf_op jit(solution)/shard_map/ppermute | solution.py:145
  144.1 2.0 copy-start.1
  248.2 2.3 copy-start.8
  (7 other events, 5.5 us)

commit v8 on v7

--- a/solution.py
+++ b/solution.py
@@ -92,6 +92,39 @@
     grad_mix = rows_product(joined, d_mixed)
     d_joined = times_transposed(d_mixed, mix_matrix)
     return (d_joined[:, :width].astype(jnp.bfloat16), d_joined[:, width:], grad_mix, grad_up)
+
+
+def up_forward_saving(below, side, mix_matrix, up_matrix):
+    joined = jnp.concatenate([below, side], axis=-1)
+    mixed = jnp.dot(joined, mix_matrix, preferred_element_type=jnp.float32)
+    scale = rms_scale(mixed)
+    normed = mixed * scale
+    active = jax.nn.silu(normed).astype(jnp.bfloat16)
+    result = (mixed + jnp.dot(active, up_matrix, preferred_element_type=jnp.float32)).astype(
+        jnp.bfloat16
+    )
+    return result, (joined, scale, normed, active)
+
+
+def up_backward_saved(saved, mix_matrix, up_matrix, cotan):
+    joined, scale, normed, active = saved
+    width = joined.shape[-1] // 2
+    grad_up = rows_product(active, cotan)
+    d_active = times_transposed(cotan, up_matrix)
+    d_normed = d_active * silu_slope(normed)
+    d_mixed = (
+        cotan.astype(jnp.float32)
+        + scale * (d_normed - normed * jnp.mean(d_normed * normed, axis=-1, keepdims=True))
+    ).astype(jnp.bfloat16)
+    grad_mix = rows_product(joined, d_mixed)
+    d_joined = times_transposed(d_mixed, mix_matrix)
+    return (d_joined[:, :width].astype(jnp.bfloat16), d_joined[:, width:], grad_mix, grad_up)
+
+
+def keep_all(valid, new, old):
+    if old is None:
+        return new
+    return tuple(jnp.where(valid, a, b) for a, b in zip(new, old))
 
 
 def reduce_replicas(parts, tail, tail_shapes):
@@ -192,16 +225,16 @@
             w_mix, w_up, hidden = lax.optimization_barrier((w_mix, w_up, hidden))
             mix_pair, up_pair = pair(w_mix), pair(w_up)
 
-    up_in = [None, None]
+    up_saved = [None, None]
     below = skip[1]
     for tick in range(stages):
         owner = stages - 1 - tick
         if tick > 0:
             below = hop(below, owner + 1, owner)
         valid = stage == owner
-        middle = up_forward(below, skip[1], mix_pair[1], up_pair[1])
-        up_in = [keep(valid, middle, up_in[0]), keep(valid, below, up_in[1])]
-        below = up_forward(middle, skip[0], mix_pair[0], up_pair[0])
+        middle, saved1 = up_forward_saving(below, skip[1], mix_pair[1], up_pair[1])
+        below, saved0 = up_forward_saving(middle, skip[0], mix_pair[0], up_pair[0])
+        up_saved = [keep_all(valid, saved0, up_saved[0]), keep_all(valid, saved1, up_saved[1])]
 
     d_skip = [None, None]
     grad_mix = [None, None]
@@ -211,8 +244,8 @@
         if tick > 0:
             cotan = hop(cotan, tick - 1, tick)
         valid = stage == tick
-        middle, side0, mix0, up0 = up_backward(up_in[0], skip[0], mix_pair[0], up_pair[0], cotan)
-        cotan, side1, mix1, up1 = up_backward(up_in[1], skip[1], mix_pair[1], up_pair[1], middle)
+        middle, side0, mix0, up0 = up_backward_saved(up_saved[0], mix_pair[0], up_pair[0], cotan)
+        cotan, side1, mix1, up1 = up_backward_saved(up_saved[1], mix_pair[1], up_pair[1], middle)
         d_skip = [keep(valid, side0, d_skip[0]), keep(valid, side1, d_skip[1])]
         grad_mix = [keep(valid, mix0, grad_mix[0]), keep(valid, mix1, grad_mix[1])]
         grad_up = [keep(valid, up0, grad_up[0]), keep(valid, up1, grad_up[1])]

time: 253 us -> 252 us (level)
    unnamed x83 -> x87, local copies, waits for them, and re-layouts: 7.33 us -> 7.79 us
  transfers between devices with their start and end apart: 16 -> 16, of which waited for: 4 -> 4; matrix products, arithmetic and copies ran while one was open for 13% -> 14% of each run, Pallas kernels for 0% -> 0%
where the time goes in v8:
time: 252 us; the launch traced here: 250 us
  blocking collectives  98 us (39%)
  waiting for transfers between devices  43.3 us (17%)
  starting transfers between devices  36.4 us (14%)
  matrix products  34.4 us (14%)
  other arithmetic  19.4 us (8%)
  local copies, waits for them, and re-layouts  16.8 us (7%)
    all_to_all x2, blocking collectives, scatter_sum(): got = lax.all_to_all(blocks, name, 0, 0, tiled=False)  57.6 us
    ppermute x8, waiting for transfers between devices, hop(): return lax.ppermute(value, 'zh', [(source, target)])  42.1 us
    all_to_all x2, blocking collectives, gather_all(): lax.all_to_all(blocks, name, 0, 0, tiled=False).reshape(-1, flat.shape[1])  40.5 us
    ppermute x8, starting transfers between devices, hop(): return lax.ppermute(value, 'zh', [(source, target)])  18.7 us
    ppermute x8, starting transfers between devices, swap_core(): return lax.ppermute(value, 'core', [(0, 1), (1, 0)])  17.7 us
    dot_general x24, matrix products, rows_product(): lax.dot_general(left, right, (((0,), (0,)), ((), ())), preferred_element_...  13.7 us
    dot_general x6, matrix products, down_forward(): jnp.dot(gated, out_matrix, preferred_element_type=jnp.float32)  8.02 us
    unnamed x87, local copies, waits for them, and re-layouts  7.79 us
  transfers between devices with their start and end apart: 16, of which 4 were waited for; matrix products, arithmetic and copies ran while one was open for 14% of the time, Pallas kernels for 0%

profile of v8, /device:TPU:2, one launch (start us, length us, event | category | flops | bytes accessed | tf_op | source)
XLA Modules:
  0.0 250.3 jit_solution(18367196300883988607)
XLA Ops:
  0.6 2.1 collective-permute-start.1
  2.7 2.4 collective-permute-start
  6.7 1.2 constant_dynamic-slice_fusion
  9.1 0.8 broadcast_select_fusion.3
  9.9 1.2 broadcast_select_fusion.5
  12.7 10.9 %collective-permute-start.2 = (bf16[192,320]{1,0:T(8,128)(2,1)S(1)}, bf16[192,320]{1,0:T(8,128)(2,1)S(1)}, u32[]{:S(2)}, u32[]{:S(2)}) collective-permute-start(bf16[192,320]{1,0:T(8,128)(2,1)S(1)} %fusion.13), channel_id=1, source_target_pairs={{0,2},{1,3},{6,8},{7,9},{12,14},{13,15},{18,20},{19,21},{24,26},{2... | collective-permute-start | bytes 368648 | tf_op jit(solution)/shard_map/ppermute | solution.py:182
  24.5 1.9 collective-permute-start.5
  26.4 2.4 collective-permute-start.4
  29.0 1.2 multiply_reduce_fusion.21
  30.2 1.7 fusion.15
  32.6 0.8 broadcast_select_fusion.6
  33.7 2.2 multiply_reduce_fusion.5
  36.8 1.7 fusion.23
  38.5 1.3 broadcast_select_fusion.1
  44.0 1.3 collective-permute-start.7
  45.7 25.3 %collective-permute-done.7 = bf16[192,320]{1,0:T(8,128)(2,1)S(1)} collective-permute-done((bf16[192,320]{1,0:T(8,128)(2,1)S(1)}, bf16[192,320]{1,0:T(8,128)(2,1)S(1)}, u32[]{:S(2)}, u32[]{:S(2)}) %collective-permute-start.7) | collective-permute-done | bytes 122912 | tf_op jit(solution)/shard_map/ppermute | solution.py:182
  75.5 1.6 collective-permute-start.8
  78.2 1.4 collective-permute-done.8
  87.1 2.1 collective-permute-start.12
  89.2 1.1 add_convert_fusion.10
  91.6 1.2 select_convert_fusion.2
  92.7 2.4 collective-permute-start.11
  96.0 1.3 collective-permute-start.10
  98.1 1.9 reshape.228
  100.0 1.9 convert_add_fusion
  101.9 1.3 copy.22
  103.2 1.3 reshape.227
  104.5 1.9 pad_maximum_fusion
  106.4 0.9 add_convert_fusion.8
  111.7 1.5 collective-permute-start.13
  113.2 1.2 convolution_select_fusion.6
  114.5 1.3 convolution_select_fusion.2
  115.8 1.3 convolution_select_fusion
  117.4 15.3 %collective-permute-done.13 = bf16[192,320]{1,0:T(8,128)(2,1)S(1)} collective-permute-done((bf16[192,320]{1,0:T(8,128)(2,1)S(1)}, bf16[192,320]{1,0:T(8,128)(2,1)S(1)}, u32[]{:S(2)}, u32[]{:S(2)}) %collective-permute-start.13) | collective-permute-done | bytes 122912 | tf_op jit(solution)/shard_map/ppermute | solution.py:182
  134.1 1.6 convolution_select_fusion.7
  136.0 2.1 collective-permute-start.14
  138.5 1.2 select_convert_fusion
  139.7 2.4 collective-permute-start.15
  142.5 1.3 collective-permute-done.15
  143.8 1.2 add_convert_fusion
  145.9 24.4 %all_to_all.20 = bf16[4,1536,128]{2,1,0:T(8,128)(2,1)S(1)} all-to-all(bf16[4,1536,128]{2,1,0:T(8,128)(2,1)S(1)} %bitcast.124), channel_id=1, replica_groups=mesh['y'=8,'x'=4,'zl'=4,'zh'=3,'core'=2] {'x'}, dimensions={0} | all-to-all | bytes 3145728 | tf_op jit(solution)/shard_map/all_to_all | solution.py:159
  170.8 33.2 %all_to_all.21 = bf16[32,48,128]{2,1,0:T(8,128)(2,1)S(1)} all-to-all(bf16[32,48,128]{2,1,0:T(8,128)(2,1)S(1)} %bitcast.125), channel_id=1, replica_groups=mesh['y'=8,'x'=4,'zl'=4,'zh'=3,'core'=2] {'y','zl'}, dimensions={0} | all-to-all | bytes 786432 | tf_op jit(solution)/shard_map/all_to_all | solution.py:159
  204.1 19.0 %all_to_all.22 = bf16[32,48,128]{2,1,0:T(8,128)(2,1)S(1)} all-to-all(bf16[32,48,128]{2,1,0:T(8,128)(2,1)S(1)} %broadcast_in_dim.23), channel_id=1, replica_groups=mesh['y'=8,'x'=4,'zl'=4,'zh'=3,'core'=2] {'y','zl'}, dimensions={0} | all-to-all | bytes 786432 | tf_op jit(solution)/shard_map/all_to_all | solution.py:166
  223.2 21.5 %all_to_all.23 = bf16[4,1536,128]{2,1,0:T(8,128)(2,1)S(1)} all-to-all(bf16[4,1536,128]{2,1,0:T(8,128)(2,1)S(1)} %broadcast_in_dim.25), channel_id=1, replica_groups=mesh['y'=8,'x'=4,'zl'=4,'zh'=3,'core'=2] {'x'}, dimensions={0} | all-to-all | bytes 3145728 | tf_op jit(solution)/shard_map/all_to_all | solution.py:166
  245.2 1.0 broadcast_in_dim_reshape.16
  246.5 1.2 copy.25
  247.7 1.1 broadcast_in_dim_reshape.13
  249.1 1.2 copy.24
  (224 shorter events, 36.8 us)
Async XLA Ops:
  0.6 8.4 %copy-start.24 = (bf16[1,640,320]{1,2,0:T(8,128)(2,1)S(1)}, bf16[1,640,320]{1,2,0:T(8,128)(2,1)}, u32[]{:S(2)}) copy-start(bf16[1,640,320]{1,2,0:T(8,128)(2,1)} %param.12) | copy-start | bytes 1228804
  0.6 8.4 %collective-permute-start.1 = (bf16[640,320]{0,1:T(8,128)(2,1)}, bf16[640,320]{0,1:T(8,128)(2,1)S(1)}, u32[]{:S(2)}, u32[]{:S(2)}) collective-permute-start(bf16[640,320]{0,1:T(8,128)(2,1)} %bitcast.127), channel_id=1, source_target_pairs={{0,1},{1,0},{2,3},{3,2},{4,5},{5,4},{6,7},{7,6},{8,9},{9,8},{10,11... | collective-permute-start | bytes 1228808 | tf_op jit(solution)/shard_map/ppermute | solution.py:178
  2.7 7.2 %collective-permute-start = (bf16[320,640]{1,0:T(8,128)(2,1)}, bf16[320,640]{1,0:T(8,128)(2,1)}, u32[]{:S(2)}, u32[]{:S(2)}) collective-permute-start(bf16[320,640]{1,0:T(8,128)(2,1)} %bitcast.128), channel_id=1, source_target_pairs={{0,1},{1,0},{2,3},{3,2},{4,5},{5,4},{6,7},{7,6},{8,9},{9,8},{10,11... | collective-permute-start | bytes 1228808 | tf_op jit(solution)/shard_map/ppermute | solution.py:178
  7.9 2.0 copy-start.25
  9.9 23.7 %copy-start.27 = (bf16[640,320]{0,1:T(8,128)(2,1)}, bf16[640,320]{0,1:T(8,128)(2,1)S(1)}, u32[]{:S(2)}) copy-start(bf16[640,320]{0,1:T(8,128)(2,1)S(1)} %get-tuple-element.42) | copy-start | bytes 1228804
  11.1 1.0 copy-start.30
  12.2 12.3 %copy-start.33 = (bf16[1,320,320]{2,1,0:T(8,128)(2,1)S(1)}, bf16[1,320,320]{2,1,0:T(8,128)(2,1)}, u32[]{:S(2)}) copy-start(bf16[1,320,320]{2,1,0:T(8,128)(2,1)} %param.14) | copy-start | bytes 614404
  12.2 14.2 %copy-start.26 = (bf16[1,640,320]{1,2,0:T(8,128)(2,1)S(1)}, bf16[1,640,320]{1,2,0:T(8,128)(2,1)}, u32[]{:S(2)}) copy-start(bf16[1,640,320]{1,2,0:T(8,128)(2,1)} %param.13) | copy-start | bytes 1228804
  12.7 17.5 %copy-start.36 = (bf16[192,320]{1,0:T(8,128)(2,1)}, bf16[192,320]{1,0:T(8,128)(2,1)S(1)}, u32[]{:S(2)}) copy-start(bf16[192,320]{1,0:T(8,128)(2,1)S(1)} %fusion.13) | copy-start | bytes 368644
  12.7 16.1 %collective-permute-start.2 = (bf16[192,320]{1,0:T(8,128)(2,1)S(1)}, bf16[192,320]{1,0:T(8,128)(2,1)S(1)}, u32[]{:S(2)}, u32[]{:S(2)}) collective-permute-start(bf16[192,320]{1,0:T(8,128)(2,1)S(1)} %fusion.13), channel_id=1, source_target_pairs={{0,2},{1,3},{6,8},{7,9},{12,14},{13,15},{18,20},{19,21},{24,26},{2... | collective-permute-start | bytes 368648 | tf_op jit(solution)/shard_map/ppermute | solution.py:182
  24.5 8.1 %collective-permute-start.5 = (bf16[320,320]{1,0:T(8,128)(2,1)S(1)}, bf16[320,320]{1,0:T(8,128)(2,1)S(1)}, u32[]{:S(2)}, u32[]{:S(2)}) collective-permute-start(bf16[320,320]{1,0:T(8,128)(2,1)S(1)} %bitcast.130), channel_id=1, source_target_pairs={{0,1},{1,0},{2,3},{3,2},{4,5},{5,4},{6,7},{7,6},{8,9},{9,8},{10,11... | collective-permute-start | bytes 614408 | tf_op jit(solution)/shard_map/ppermute | solution.py:178
  26.4 12.1 %collective-permute-start.4 = (bf16[640,320]{0,1:T(8,128)(2,1)S(1)}, bf16[640,320]{0,1:T(8,128)(2,1)}, u32[]{:S(2)}, u32[]{:S(2)}) collective-permute-start(bf16[640,320]{0,1:T(8,128)(2,1)S(1)} %bitcast.129), channel_id=1, source_target_pairs={{0,1},{1,0},{2,3},{3,2},{4,5},{5,4},{6,7},{7,6},{8,9},{9,8},{10,11... | collective-permute-start | bytes 1228808 | tf_op jit(solution)/shard_map/ppermute | solution.py:178
  31.9 4.0 %copy-start.38 = (bf16[192,320]{1,0:T(8,128)(2,1)}, bf16[192,320]{1,0:T(8,128)(2,1)S(1)}, u32[]{:S(2)}) copy-start(bf16[192,320]{1,0:T(8,128)(2,1)S(1)} %fusion.15) | copy-start | bytes 368644
  31.9 1.5 collective-permute-start.3
  36.3 49.3 %copy-start.4 = (f32[192,640]{1,0:T(8,128)}, f32[192,640]{1,0:T(8,128)S(1)}, u32[]{:S(2)}) copy-start(f32[192,640]{1,0:T(8,128)S(1)} %fusion.86) | copy-start | bytes 1474564
  38.5 44.1 %copy-start.14 = (bf16[192,320]{1,0:T(8,128)(2,1)}, bf16[192,320]{1,0:T(8,128)(2,1)S(1)}, u32[]{:S(2)}) copy-start(bf16[192,320]{1,0:T(8,128)(2,1)S(1)} %fusion.23) | copy-start | bytes 368644
  38.5 1.8 copy-start.34
  41.6 0.8 collective-permute-start.6
  42.3 3.0 %copy-start.2 = (bf16[192,320]{1,0:T(8,128)(2,1)}, bf16[192,320]{1,0:T(8,128)(2,1)S(1)}, u32[]{:S(2)}) copy-start(bf16[192,320]{1,0:T(8,128)(2,1)S(1)} %multiply_convert_fusion.26) | copy-start | bytes 368644
  44.0 27.0 %collective-permute-start.7 = (bf16[192,320]{1,0:T(8,128)(2,1)S(1)}, bf16[192,320]{1,0:T(8,128)(2,1)S(1)}, u32[]{:S(2)}, u32[]{:S(2)}) collective-permute-start(bf16[192,320]{1,0:T(8,128)(2,1)S(1)} %fusion.21), channel_id=1, source_target_pairs={{2,0},{3,1},{8,6},{9,7},{14,12},{15,13},{20,18},{21,19},{26,24},{2... | collective-permute-start | bytes 368648 | tf_op jit(solution)/shard_map/ppermute | solution.py:182
  45.6 44.6 %copy-start.21 = (f32[192,640]{1,0:T(8,128)}, f32[192,640]{1,0:T(8,128)S(1)}, u32[]{:S(2)}) copy-start(f32[192,640]{1,0:T(8,128)S(1)} %fusion.87) | copy-start | bytes 1474564
  75.5 4.1 %collective-permute-start.8 = (bf16[192,320]{1,0:T(8,128)(2,1)S(1)}, bf16[192,320]{1,0:T(8,128)(2,1)S(1)}, u32[]{:S(2)}, u32[]{:S(2)}) collective-permute-start(bf16[192,320]{1,0:T(8,128)(2,1)S(1)} %slice.121), channel_id=1, source_target_pairs={{0,2},{1,3},{6,8},{7,9},{12,14},{13,15},{18,20},{19,21},{24,26},{2... | collective-permute-start | bytes 368648 | tf_op jit(solution)/shard_map/ppermute | solution.py:182
  81.3 2.0 collective-permute-start.9
  85.5 3.6 %copy-start.16 = (bf16[192,320]{1,0:T(8,128)(2,1)}, bf16[192,320]{1,0:T(8,128)(2,1)S(1)}, u32[]{:S(2)}) copy-start(bf16[192,320]{1,0:T(8,128)(2,1)S(1)} %get-tuple-element.30) | copy-start | bytes 368644
  86.1 1.0 copy-start.10
  87.1 3.2 %copy-start.28 = (bf16[640,320]{0,1:T(8,128)(2,1)S(1)}, bf16[640,320]{0,1:T(8,128)(2,1)}, u32[]{:S(2)}) copy-start(bf16[640,320]{0,1:T(8,128)(2,1)} %copy-done.27) | copy-start | bytes 1228804
  87.1 10.2 %collective-permute-start.12 = (bf16[320,320]{1,0:T(8,128)(2,1)S(1)}, bf16[320,320]{1,0:T(8,128)(2,1)S(1)}, u32[]{:S(2)}, u32[]{:S(2)}) collective-permute-start(bf16[320,320]{1,0:T(8,128)(2,1)S(1)} %get-tuple-element.86), channel_id=1, source_target_pairs={{0,1},{1,0},{2,3},{3,2},{4,5},{5,4},{6,7},{7,6},{8,9},{9,8},{10,11... | collective-permute-start | bytes 614408 | tf_op jit(solution)/shard_map/ppermute | solution.py:178
  90.3 4.9 %copy-start.18 = (bf16[192,320]{1,0:T(8,128)(2,1)}, bf16[192,320]{1,0:T(8,128)(2,1)S(1)}, u32[]{:S(2)}) copy-start(bf16[192,320]{1,0:T(8,128)(2,1)S(1)} %get-tuple-element.26) | copy-start | bytes 368644
  92.7 7.2 %collective-permute-start.11 = (bf16[640,320]{0,1:T(8,128)(2,1)}, bf16[640,320]{0,1:T(8,128)(2,1)}, u32[]{:S(2)}, u32[]{:S(2)}) collective-permute-start(bf16[640,320]{0,1:T(8,128)(2,1)} %get-tuple-element.88), channel_id=1, source_target_pairs={{0,1},{1,0},{2,3},{3,2},{4,5},{5,4},{6,7},{7,6},{8,9},{9,8},{10,11... | collective-permute-start | bytes 1228808 | tf_op jit(solution)/shard_map/ppermute | solution.py:178
  96.0 10.5 %collective-permute-start.10 = (bf16[192,320]{1,0:T(8,128)(2,1)}, bf16[192,320]{1,0:T(8,128)(2,1)}, u32[]{:S(2)}, u32[]{:S(2)}) collective-permute-start(bf16[192,320]{1,0:T(8,128)(2,1)} %add_convert_fusion.9), channel_id=1, source_target_pairs={{4,2},{5,3},{10,8},{11,9},{16,14},{17,15},{22,20},{23,21},{28,26},... | collective-permute-start | bytes 368648 | tf_op jit(solution)/shard_map/ppermute | solution.py:182
  101.8 2.7 %copy-start.12 = (bf16[102400]{0:T(1024)(128)(2,1)S(1)}, bf16[102400]{0:T(1024)(128)(2,1)}, u32[]{:S(2)}) copy-start(bf16[102400]{0:T(1024)(128)(2,1)} %reshape.228) | copy-start | bytes 614404
  103.2 4.2 %copy-start.5 = (f32[192,640]{1,0:T(8,128)S(1)}, f32[192,640]{1,0:T(8,128)}, u32[]{:S(2)}) copy-start(f32[192,640]{1,0:T(8,128)} %copy-done.4) | copy-start | bytes 1474564
  104.5 2.9 %copy-start.32 = (bf16[640,320]{0,1:T(8,128)(2,1)S(1)}, bf16[640,320]{0,1:T(8,128)(2,1)}, u32[]{:S(2)}) copy-start(bf16[640,320]{0,1:T(8,128)(2,1)} %get-tuple-element.43) | copy-start | bytes 1228804
  107.7 1.1 copy-start.22
  107.7 1.2 copy-start.29
  110.1 1.0 copy-start.6
  111.1 2.1 copy-start.9
  111.5 2.9 %copy-start.19 = (bf16[192,320]{1,0:T(8,128)(2,1)S(1)}, bf16[192,320]{1,0:T(8,128)(2,1)}, u32[]{:S(2)}) copy-start(bf16[192,320]{1,0:T(8,128)(2,1)} %copy-done.18) | copy-start | bytes 368644
  111.7 21.0 %collective-permute-start.13 = (bf16[192,320]{1,0:T(8,128)(2,1)S(1)}, bf16[192,320]{1,0:T(8,128)(2,1)S(1)}, u32[]{:S(2)}, u32[]{:S(2)}) collective-permute-start(bf16[192,320]{1,0:T(8,128)(2,1)S(1)} %add_convert_fusion.5), channel_id=1, source_target_pairs={{2,0},{3,1},{8,6},{9,7},{14,12},{15,13},{20,18},{21,19},{26,24},{2... | collective-permute-start | bytes 368648 | tf_op jit(solution)/shard_map/ppermute | solution.py:182
  114.5 1.3 copy-start.17
  115.8 1.3 copy-start.11
  133.0 1.0 copy-start.23
  135.6 2.4 copy-start.39
  136.0 2.5 copy-start.7
  136.0 2.5 copy-start.13
  136.0 6.1 %collective-permute-start.14 = (bf16[320,640]{1,0:T(8,128)(2,1)S(1)}, bf16[320,640]{1,0:T(8,128)(2,1)S(1)}, u32[]{:S(2)}, u32[]{:S(2)}) collective-permute-start(bf16[320,640]{1,0:T(8,128)(2,1)S(1)} %get-tuple-element.98), channel_id=1, source_target_pairs={{0,1},{1,0},{2,3},{3,2},{4,5},{5,4},{6,7},{7,6},{8,9},{9,8},{10,11... | collective-permute-start | bytes 1228808 | tf_op jit(solution)/shard_map/ppermute | solution.py:178
  139.7 4.1 %collective-permute-start.15 = (bf16[640,320]{0,1:T(8,128)(2,1)}, bf16[640,320]{0,1:T(8,128)(2,1)}, u32[]{:S(2)}, u32[]{:S(2)}) collective-permute-start(bf16[640,320]{0,1:T(8,128)(2,1)} %get-tuple-element.96), channel_id=1, source_target_pairs={{0,1},{1,0},{2,3},{3,2},{4,5},{5,4},{6,7},{7,6},{8,9},{9,8},{10,11... | collective-permute-start | bytes 1228808 | tf_op jit(solution)/shard_map/ppermute | solution.py:178
  143.8 2.0 copy-start.1
  (9 other events, 8.4 us)

commit v9 on v8

--- a/solution.py
+++ b/solution.py
@@ -92,6 +92,34 @@
     grad_mix = rows_product(joined, d_mixed)
     d_joined = times_transposed(d_mixed, mix_matrix)
     return (d_joined[:, :width].astype(jnp.bfloat16), d_joined[:, width:], grad_mix, grad_up)
+
+
+def down_forward_saving(hidden, embedding, in_matrix, out_matrix):
+    lifted = hidden.astype(jnp.float32) + embedding
+    scale = rms_scale(lifted)
+    normed = lifted * scale
+    inner = jnp.dot(normed.astype(jnp.bfloat16), in_matrix, preferred_element_type=jnp.float32)
+    gated = jax.nn.silu(inner).astype(jnp.bfloat16)
+    result = (lifted + jnp.dot(gated, out_matrix, preferred_element_type=jnp.float32)).astype(
+        jnp.bfloat16
+    )
+    return result, (scale, normed)
+
+
+def down_backward_saved(saved, in_matrix, out_matrix, cotan):
+    scale, normed = saved
+    normed_b = normed.astype(jnp.bfloat16)
+    inner = jnp.dot(normed_b, in_matrix, preferred_element_type=jnp.float32)
+    gated = jax.nn.silu(inner).astype(jnp.bfloat16)
+    grad_out = rows_product(gated, cotan)
+    d_gated = times_transposed(cotan, out_matrix)
+    d_inner = (d_gated * silu_slope(inner)).astype(jnp.bfloat16)
+    grad_in = rows_product(normed_b, d_inner)
+    d_normed = times_transposed(d_inner, in_matrix)
+    d_lifted = cotan.astype(jnp.float32) + scale * (
+        d_normed - normed * jnp.mean(d_normed * normed, axis=-1, keepdims=True)
+    )
+    return (d_lifted.astype(jnp.bfloat16), grad_in, grad_out)
 
 
 def up_forward_saving(below, side, mix_matrix, up_matrix):
@@ -209,17 +237,16 @@
     source = lax.dynamic_slice_in_dim(latents, offset, rows)
     seed = lax.dynamic_slice_in_dim(out_grad, offset, rows)
 
-    down_in = [None, None]
+    down_saved = [None, None]
     skip = [None, None]
     hidden = source
     for tick in range(stages):
         if tick > 0:
             hidden = hop(hidden, tick - 1, tick)
         valid = stage == tick
-        lower = hidden
-        upper = down_forward(lower, embedding, in_pair[0], out_pair[0])
-        hidden = down_forward(upper, embedding, in_pair[1], out_pair[1])
-        down_in = [keep(valid, lower, down_in[0]), keep(valid, upper, down_in[1])]
+        upper, saved0 = down_forward_saving(hidden, embedding, in_pair[0], out_pair[0])
+        hidden, saved1 = down_forward_saving(upper, embedding, in_pair[1], out_pair[1])
+        down_saved = [keep_all(valid, saved0, down_saved[0]), keep_all(valid, saved1, down_saved[1])]
         skip = [keep(valid, upper, skip[0]), keep(valid, hidden, skip[1])]
         if tick == 0:
             w_mix, w_up, hidden = lax.optimization_barrier((w_mix, w_up, hidden))
@@ -270,9 +297,9 @@
             carry, up_flat = lax.optimization_barrier((carry, up_flat))
         valid = stage == owner
         upper_c = (d_skip[1] + carry.astype(jnp.float32)).astype(jnp.bfloat16)
-        upper_d, in1, out1 = down_backward(down_in[1], embedding, in_pair[1], out_pair[1], upper_c)
+        upper_d, in1, out1 = down_backward_saved(down_saved[1], in_pair[1], out_pair[1], upper_c)
         lower_c = (d_skip[0] + upper_d.astype(jnp.float32)).astype(jnp.bfloat16)
-        carry, in0, out0 = down_backward(down_in[0], embedding, in_pair[0], out_pair[0], lower_c)
+        carry, in0, out0 = down_backward_saved(down_saved[0], in_pair[0], out_pair[0], lower_c)
         grad_in = [keep(valid, in0, grad_in[0]), keep(valid, in1, grad_in[1])]
         grad_out = [keep(valid, out0, grad_out[0]), keep(valid, out1, grad_out[1])]
 

time: 252 us -> 253 us (level)
    ppermute x8, waiting for transfers between devices: 42.1 us -> 44.9 us  [hop(): return lax.ppermute(value, 'zh', [(source, target)])]
    unnamed x87 -> x119, local copies, waits for them, and re-layouts: 7.79 us -> 5.94 us
  transfers between devices with their start and end apart: 16 -> 16, of which waited for: 4 -> 4; matrix products, arithmetic and copies ran while one was open for 14% -> 13% of each run, Pallas kernels for 0% -> 0%
where the time goes in v9:
time: 253 us; the launch traced here: 252 us
  blocking collectives  98 us (39%)
  waiting for transfers between devices  45.5 us (18%)
  starting transfers between devices  36.4 us (14%)
  matrix products  33.1 us (13%)
  other arithmetic  20.9 us (8%)
  local copies, waits for them, and re-layouts  15.9 us (6%)
    all_to_all x2, blocking collectives, scatter_sum(): got = lax.all_to_all(blocks, name, 0, 0, tiled=False)  57.6 us
    ppermute x8, waiting for transfers between devices, hop(): return lax.ppermute(value, 'zh', [(source, target)])  44.9 us
    all_to_all x2, blocking collectives, gather_all(): lax.all_to_all(blocks, name, 0, 0, tiled=False).reshape(-1, flat.shape[1])  40.5 us
    ppermute x8, starting transfers between devices, hop(): return lax.ppermute(value, 'zh', [(source, target)])  18.7 us
    ppermute x8, starting transfers between devices, swap_core(): return lax.ppermute(value, 'core', [(0, 1), (1, 0)])  17.7 us
    dot_general x24, matrix products, rows_product(): lax.dot_general(left, right, (((0,), (0,)), ((), ())), preferred_element_...  13 us
    dot_general x22, matrix products, times_transposed(): lax.dot_general(left, right, (((1,), (1,)), ((), ())), preferred_element_...  7.54 us
    dot_general x6, matrix products, down_forward_saving(): jnp.dot(gated, out_matrix, preferred_element_type=jnp.float32)  7.44 us
  transfers between devices with their start and end apart: 16, of which 4 were waited for; matrix products, arithmetic and copies ran while one was open for 13% of the time, Pallas kernels for 0%

profile of v9, /device:TPU:2, one launch (start us, length us, event | category | flops | bytes accessed | tf_op | source)
XLA Modules:
  0.0 251.9 jit_solution(12219332613658929318)
XLA Ops:
  0.7 2.1 collective-permute-start.1
  2.7 2.4 collective-permute-start
  8.0 0.8 broadcast_select_fusion.3
  9.7 1.7 fusion.13
  11.4 10.9 %collective-permute-start.2 = (bf16[192,320]{1,0:T(8,128)(2,1)S(1)}, bf16[192,320]{1,0:T(8,128)(2,1)S(1)}, u32[]{:S(2)}, u32[]{:S(2)}) collective-permute-start(bf16[192,320]{1,0:T(8,128)(2,1)S(1)} %fusion.13), channel_id=1, source_target_pairs={{0,2},{1,3},{6,8},{7,9},{12,14},{13,15},{18,20},{19,21},{24,26},{2... | collective-permute-start | bytes 368648 | tf_op jit(solution)/shard_map/ppermute | solution.py:210
  22.6 1.9 collective-permute-start.5
  24.6 2.4 collective-permute-start.4
  28.5 1.6 fusion.15
  30.8 1.7 broadcast_select_fusion.6
  33.3 1.3 select_select_fusion.7
  35.8 1.6 fusion.23
  37.4 1.4 fusion.74
  38.8 1.1 broadcast_select_fusion.1
  44.5 1.3 collective-permute-start.7
  46.1 25.5 %collective-permute-done.7 = bf16[192,320]{1,0:T(8,128)(2,1)S(1)} collective-permute-done((bf16[192,320]{1,0:T(8,128)(2,1)S(1)}, bf16[192,320]{1,0:T(8,128)(2,1)S(1)}, u32[]{:S(2)}, u32[]{:S(2)}) %collective-permute-start.7) | collective-permute-done | bytes 122912 | tf_op jit(solution)/shard_map/ppermute | solution.py:210
  75.6 1.6 collective-permute-start.8
  78.3 1.4 collective-permute-done.8
  87.2 2.1 collective-permute-start.12
  89.3 1.1 add_convert_fusion.10
  91.7 1.2 select_convert_fusion.2
  92.8 2.4 collective-permute-start.11
  95.3 0.8 add_convert_fusion.9
  96.1 1.3 collective-permute-start.10
  98.1 1.9 reshape.232
  100.1 1.9 convert_add_fusion
  101.9 1.3 copy.22
  103.9 0.9 pad_maximum_fusion
  104.7 0.9 add_convert_fusion.8
  110.0 1.5 collective-permute-start.13
  111.9 1.3 convolution_select_fusion.2
  113.2 1.3 convolution_select_fusion
  114.8 18.0 %collective-permute-done.13 = bf16[192,320]{1,0:T(8,128)(2,1)S(1)} collective-permute-done((bf16[192,320]{1,0:T(8,128)(2,1)S(1)}, bf16[192,320]{1,0:T(8,128)(2,1)S(1)}, u32[]{:S(2)}, u32[]{:S(2)}) %collective-permute-start.13) | collective-permute-done | bytes 122912 | tf_op jit(solution)/shard_map/ppermute | solution.py:210
  133.6 0.8 add_convert_fusion.2
  134.4 1.8 convolution_select_fusion.7
  136.6 2.1 collective-permute-start.14
  139.1 1.2 select_convert_fusion
  140.3 2.4 collective-permute-start.15
  142.8 1.1 reshape.233
  144.4 1.2 add_convert_fusion
  146.7 24.4 %all_to_all.20 = bf16[4,1536,128]{2,1,0:T(8,128)(2,1)S(1)} all-to-all(bf16[4,1536,128]{2,1,0:T(8,128)(2,1)S(1)} %bitcast.124), channel_id=1, replica_groups=mesh['y'=8,'x'=4,'zl'=4,'zh'=3,'core'=2] {'x'}, dimensions={0} | all-to-all | bytes 3145728 | tf_op jit(solution)/shard_map/all_to_all | solution.py:187
  171.5 33.1 %all_to_all.21 = bf16[32,48,128]{2,1,0:T(8,128)(2,1)S(1)} all-to-all(bf16[32,48,128]{2,1,0:T(8,128)(2,1)S(1)} %bitcast.125), channel_id=1, replica_groups=mesh['y'=8,'x'=4,'zl'=4,'zh'=3,'core'=2] {'y','zl'}, dimensions={0} | all-to-all | bytes 786432 | tf_op jit(solution)/shard_map/all_to_all | solution.py:187
  204.8 19.0 %all_to_all.22 = bf16[32,48,128]{2,1,0:T(8,128)(2,1)S(1)} all-to-all(bf16[32,48,128]{2,1,0:T(8,128)(2,1)S(1)} %broadcast_in_dim.23), channel_id=1, replica_groups=mesh['y'=8,'x'=4,'zl'=4,'zh'=3,'core'=2] {'y','zl'}, dimensions={0} | all-to-all | bytes 786432 | tf_op jit(solution)/shard_map/all_to_all | solution.py:194
  224.0 21.5 %all_to_all.23 = bf16[4,1536,128]{2,1,0:T(8,128)(2,1)S(1)} all-to-all(bf16[4,1536,128]{2,1,0:T(8,128)(2,1)S(1)} %broadcast_in_dim.25), channel_id=1, replica_groups=mesh['y'=8,'x'=4,'zl'=4,'zh'=3,'core'=2] {'x'}, dimensions={0} | all-to-all | bytes 3145728 | tf_op jit(solution)/shard_map/all_to_all | solution.py:194
  245.7 1.1 fusion.78
  246.8 1.0 broadcast_in_dim_reshape.16
  248.1 1.2 copy.25
  249.3 1.1 broadcast_in_dim_reshape.13
  250.7 1.2 copy.24
  (253 shorter events, 37.4 us)
Async XLA Ops:
  0.6 6.1 %copy-start = (bf16[384,320]{0,1:T(8,128)(2,1)S(1)}, bf16[384,320]{0,1:T(8,128)(2,1)}, u32[]{:S(2)}) copy-start(bf16[384,320]{0,1:T(8,128)(2,1)} %param.8) | copy-start | bytes 737284
  0.6 7.3 %copy-start.28 = (bf16[1,640,320]{1,2,0:T(8,128)(2,1)S(1)}, bf16[1,640,320]{1,2,0:T(8,128)(2,1)}, u32[]{:S(2)}) copy-start(bf16[1,640,320]{1,2,0:T(8,128)(2,1)} %param.12) | copy-start | bytes 1228804
  0.7 7.3 %collective-permute-start.1 = (bf16[640,320]{0,1:T(8,128)(2,1)}, bf16[640,320]{0,1:T(8,128)(2,1)S(1)}, u32[]{:S(2)}, u32[]{:S(2)}) collective-permute-start(bf16[640,320]{0,1:T(8,128)(2,1)} %bitcast.127), channel_id=1, source_target_pairs={{0,1},{1,0},{2,3},{3,2},{4,5},{5,4},{6,7},{7,6},{8,9},{9,8},{10,11... | collective-permute-start | bytes 1228808 | tf_op jit(solution)/shard_map/ppermute | solution.py:206
  2.7 6.1 %collective-permute-start = (bf16[320,640]{1,0:T(8,128)(2,1)}, bf16[320,640]{1,0:T(8,128)(2,1)S(1)}, u32[]{:S(2)}, u32[]{:S(2)}) collective-permute-start(bf16[320,640]{1,0:T(8,128)(2,1)} %bitcast.128), channel_id=1, source_target_pairs={{0,1},{1,0},{2,3},{3,2},{4,5},{5,4},{6,7},{7,6},{8,9},{9,8},{10,11... | collective-permute-start | bytes 1228808 | tf_op jit(solution)/shard_map/ppermute | solution.py:206
  6.8 2.0 copy-start.29
  9.6 12.7 %copy-start.44 = (bf16[384,320]{0,1:T(8,128)(2,1)S(1)}, bf16[384,320]{0,1:T(8,128)(2,1)}, u32[]{:S(2)}) copy-start(bf16[384,320]{0,1:T(8,128)(2,1)} %param.15) | copy-start | bytes 737284
  9.7 13.0 %copy-start.37 = (bf16[1,320,320]{2,1,0:T(8,128)(2,1)S(1)}, bf16[1,320,320]{2,1,0:T(8,128)(2,1)}, u32[]{:S(2)}) copy-start(bf16[1,320,320]{2,1,0:T(8,128)(2,1)} %param.14) | copy-start | bytes 614404
  9.7 14.9 %copy-start.30 = (bf16[1,640,320]{1,2,0:T(8,128)(2,1)S(1)}, bf16[1,640,320]{1,2,0:T(8,128)(2,1)}, u32[]{:S(2)}) copy-start(bf16[1,640,320]{1,2,0:T(8,128)(2,1)} %param.13) | copy-start | bytes 1228804
  9.7 17.5 %copy-start.32 = (bf16[640,320]{0,1:T(8,128)(2,1)S(1)}, bf16[640,320]{0,1:T(8,128)(2,1)}, u32[]{:S(2)}) copy-start(bf16[640,320]{0,1:T(8,128)(2,1)} %copy-done.31) | copy-start | bytes 1228804
  11.4 16.4 %copy-start.53 = (bf16[192,320]{1,0:T(8,128)(2,1)}, bf16[192,320]{1,0:T(8,128)(2,1)S(1)}, u32[]{:S(2)}) copy-start(bf16[192,320]{1,0:T(8,128)(2,1)S(1)} %fusion.13) | copy-start | bytes 368644
  11.4 15.6 %collective-permute-start.2 = (bf16[192,320]{1,0:T(8,128)(2,1)S(1)}, bf16[192,320]{1,0:T(8,128)(2,1)S(1)}, u32[]{:S(2)}, u32[]{:S(2)}) collective-permute-start(bf16[192,320]{1,0:T(8,128)(2,1)S(1)} %fusion.13), channel_id=1, source_target_pairs={{0,2},{1,3},{6,8},{7,9},{12,14},{13,15},{18,20},{19,21},{24,26},{2... | collective-permute-start | bytes 368648 | tf_op jit(solution)/shard_map/ppermute | solution.py:210
  22.6 8.2 %collective-permute-start.5 = (bf16[320,320]{1,0:T(8,128)(2,1)S(1)}, bf16[320,320]{1,0:T(8,128)(2,1)}, u32[]{:S(2)}, u32[]{:S(2)}) collective-permute-start(bf16[320,320]{1,0:T(8,128)(2,1)S(1)} %bitcast.130), channel_id=1, source_target_pairs={{0,1},{1,0},{2,3},{3,2},{4,5},{5,4},{6,7},{7,6},{8,9},{9,8},{10,11... | collective-permute-start | bytes 614408 | tf_op jit(solution)/shard_map/ppermute | solution.py:206
  24.6 14.3 %collective-permute-start.4 = (bf16[640,320]{0,1:T(8,128)(2,1)S(1)}, bf16[640,320]{0,1:T(8,128)(2,1)}, u32[]{:S(2)}, u32[]{:S(2)}) collective-permute-start(bf16[640,320]{0,1:T(8,128)(2,1)S(1)} %bitcast.129), channel_id=1, source_target_pairs={{0,1},{1,0},{2,3},{3,2},{4,5},{5,4},{6,7},{7,6},{8,9},{9,8},{10,11... | collective-permute-start | bytes 1228808 | tf_op jit(solution)/shard_map/ppermute | solution.py:206
  27.9 2.2 copy-start.50
  28.5 4.8 %copy-start.40 = (bf16[192,320]{1,0:T(8,128)(2,1)S(1)}, bf16[192,320]{1,0:T(8,128)(2,1)}, u32[]{:S(2)}) copy-start(bf16[192,320]{1,0:T(8,128)(2,1)} %copy-done.39) | copy-start | bytes 368644
  30.1 3.1 %copy-start.55 = (bf16[192,320]{1,0:T(8,128)(2,1)}, bf16[192,320]{1,0:T(8,128)(2,1)S(1)}, u32[]{:S(2)}) copy-start(bf16[192,320]{1,0:T(8,128)(2,1)S(1)} %fusion.15) | copy-start | bytes 368644
  30.1 2.4 collective-permute-start.3
  33.3 2.6 %copy-start.54 = (bf16[192,320]{1,0:T(8,128)(2,1)S(1)}, bf16[192,320]{1,0:T(8,128)(2,1)}, u32[]{:S(2)}) copy-start(bf16[192,320]{1,0:T(8,128)(2,1)} %copy-done.53) | copy-start | bytes 368644
  37.4 45.3 %copy-start.19 = (bf16[192,320]{1,0:T(8,128)(2,1)}, bf16[192,320]{1,0:T(8,128)(2,1)S(1)}, u32[]{:S(2)}) copy-start(bf16[192,320]{1,0:T(8,128)(2,1)S(1)} %fusion.23) | copy-start | bytes 368644
  38.8 3.6 %copy-start.5 = (bf16[192,320]{1,0:T(8,128)(2,1)}, bf16[192,320]{1,0:T(8,128)(2,1)S(1)}, u32[]{:S(2)}) copy-start(bf16[192,320]{1,0:T(8,128)(2,1)S(1)} %get-tuple-element.22) | copy-start | bytes 368644
  41.8 1.0 collective-permute-start.6
  42.8 47.6 %copy-start.25 = (f32[192,640]{1,0:T(8,128)}, f32[192,640]{1,0:T(8,128)S(1)}, u32[]{:S(2)}) copy-start(f32[192,640]{1,0:T(8,128)S(1)} %fusion.86) | copy-start | bytes 1474564
  44.5 27.1 %collective-permute-start.7 = (bf16[192,320]{1,0:T(8,128)(2,1)S(1)}, bf16[192,320]{1,0:T(8,128)(2,1)S(1)}, u32[]{:S(2)}, u32[]{:S(2)}) collective-permute-start(bf16[192,320]{1,0:T(8,128)(2,1)S(1)} %fusion.21), channel_id=1, source_target_pairs={{2,0},{3,1},{8,6},{9,7},{14,12},{15,13},{20,18},{21,19},{26,24},{2... | collective-permute-start | bytes 368648 | tf_op jit(solution)/shard_map/ppermute | solution.py:210
  46.1 39.6 %copy-start.8 = (f32[192,640]{1,0:T(8,128)}, f32[192,640]{1,0:T(8,128)S(1)}, u32[]{:S(2)}) copy-start(f32[192,640]{1,0:T(8,128)S(1)} %fusion.85) | copy-start | bytes 1474564
  75.6 4.1 %collective-permute-start.8 = (bf16[192,320]{1,0:T(8,128)(2,1)S(1)}, bf16[192,320]{1,0:T(8,128)(2,1)S(1)}, u32[]{:S(2)}, u32[]{:S(2)}) collective-permute-start(bf16[192,320]{1,0:T(8,128)(2,1)S(1)} %slice.121), channel_id=1, source_target_pairs={{0,2},{1,3},{6,8},{7,9},{12,14},{13,15},{18,20},{19,21},{24,26},{2... | collective-permute-start | bytes 368648 | tf_op jit(solution)/shard_map/ppermute | solution.py:210
  81.4 2.0 collective-permute-start.9
  85.6 3.7 %copy-start.21 = (bf16[192,320]{1,0:T(8,128)(2,1)}, bf16[192,320]{1,0:T(8,128)(2,1)S(1)}, u32[]{:S(2)}) copy-start(bf16[192,320]{1,0:T(8,128)(2,1)S(1)} %get-tuple-element.28) | copy-start | bytes 368644
  86.9 2.4 copy-start.45
  87.2 3.2 %copy-start.33 = (bf16[640,320]{0,1:T(8,128)(2,1)S(1)}, bf16[640,320]{0,1:T(8,128)(2,1)}, u32[]{:S(2)}) copy-start(bf16[640,320]{0,1:T(8,128)(2,1)} %copy-done.31) | copy-start | bytes 1228804
  87.2 10.2 %collective-permute-start.12 = (bf16[320,320]{1,0:T(8,128)(2,1)S(1)}, bf16[320,320]{1,0:T(8,128)(2,1)S(1)}, u32[]{:S(2)}, u32[]{:S(2)}) collective-permute-start(bf16[320,320]{1,0:T(8,128)(2,1)S(1)} %get-tuple-element.89), channel_id=1, source_target_pairs={{0,1},{1,0},{2,3},{3,2},{4,5},{5,4},{6,7},{7,6},{8,9},{9,8},{10,11... | collective-permute-start | bytes 614408 | tf_op jit(solution)/shard_map/ppermute | solution.py:206
  90.3 4.9 %copy-start.23 = (bf16[192,320]{1,0:T(8,128)(2,1)}, bf16[192,320]{1,0:T(8,128)(2,1)S(1)}, u32[]{:S(2)}) copy-start(bf16[192,320]{1,0:T(8,128)(2,1)S(1)} %get-tuple-element.24) | copy-start | bytes 368644
  91.7 3.6 %copy-start.46 = (f32[192]{0:T(256)S(1)}, f32[192]{0:T(256)}, u32[]{:S(2)}) copy-start(f32[192]{0:T(256)} %get-tuple-element.47) | copy-start | bytes 2308
  92.8 7.2 %collective-permute-start.11 = (bf16[640,320]{0,1:T(8,128)(2,1)}, bf16[640,320]{0,1:T(8,128)(2,1)}, u32[]{:S(2)}, u32[]{:S(2)}) collective-permute-start(bf16[640,320]{0,1:T(8,128)(2,1)} %get-tuple-element.91), channel_id=1, source_target_pairs={{0,1},{1,0},{2,3},{3,2},{4,5},{5,4},{6,7},{7,6},{8,9},{9,8},{10,11... | collective-permute-start | bytes 1228808 | tf_op jit(solution)/shard_map/ppermute | solution.py:206
  96.1 8.7 %collective-permute-start.10 = (bf16[192,320]{1,0:T(8,128)(2,1)}, bf16[192,320]{1,0:T(8,128)(2,1)}, u32[]{:S(2)}, u32[]{:S(2)}) collective-permute-start(bf16[192,320]{1,0:T(8,128)(2,1)} %add_convert_fusion.9), channel_id=1, source_target_pairs={{4,2},{5,3},{10,8},{11,9},{16,14},{17,15},{22,20},{23,21},{28,26},... | collective-permute-start | bytes 368648 | tf_op jit(solution)/shard_map/ppermute | solution.py:210
  101.9 1.9 copy-start.17
  103.2 2.4 copy-start.9
  103.8 1.8 copy-start.36
  109.4 2.1 copy-start.16
  109.8 2.0 copy-start.24
  110.0 22.8 %collective-permute-start.13 = (bf16[192,320]{1,0:T(8,128)(2,1)S(1)}, bf16[192,320]{1,0:T(8,128)(2,1)S(1)}, u32[]{:S(2)}, u32[]{:S(2)}) collective-permute-start(bf16[192,320]{1,0:T(8,128)(2,1)S(1)} %add_convert_fusion.5), channel_id=1, source_target_pairs={{2,0},{3,1},{8,6},{9,7},{14,12},{15,13},{20,18},{21,19},{26,24},{2... | collective-permute-start | bytes 368648 | tf_op jit(solution)/shard_map/ppermute | solution.py:210
  136.2 2.5 copy-start.27
  136.2 2.5 copy-start.42
  136.2 2.5 copy-start.56
  136.6 2.5 %copy-start.11 = (f32[192,640]{1,0:T(8,128)S(1)}, f32[192,640]{1,0:T(8,128)}, u32[]{:S(2)}) copy-start(f32[192,640]{1,0:T(8,128)} %copy-done.8) | copy-start | bytes 1474564
  136.6 2.5 copy-start.18
  136.6 6.1 %collective-permute-start.14 = (bf16[320,640]{1,0:T(8,128)(2,1)S(1)}, bf16[320,640]{1,0:T(8,128)(2,1)S(1)}, u32[]{:S(2)}, u32[]{:S(2)}) collective-permute-start(bf16[320,640]{1,0:T(8,128)(2,1)S(1)} %get-tuple-element.101), channel_id=1, source_target_pairs={{0,1},{1,0},{2,3},{3,2},{4,5},{5,4},{6,7},{7,6},{8,9},{9,8},{10,11... | collective-permute-start | bytes 1228808 | tf_op jit(solution)/shard_map/ppermute | solution.py:206
  140.3 4.1 %collective-permute-start.15 = (bf16[640,320]{0,1:T(8,128)(2,1)}, bf16[640,320]{0,1:T(8,128)(2,1)}, u32[]{:S(2)}, u32[]{:S(2)}) collective-permute-start(bf16[640,320]{0,1:T(8,128)(2,1)} %get-tuple-element.99), channel_id=1, source_target_pairs={{0,1},{1,0},{2,3},{3,2},{4,5},{5,4},{6,7},{7,6},{8,9},{9,8},{10,11... | collective-permute-start | bytes 1228808 | tf_op jit(solution)/shard_map/ppermute | solution.py:206
  144.4 2.1 copy-start.4
  (25 other events, 27.0 us)

commit v10 on v8

--- a/solution.py
+++ b/solution.py
@@ -132,7 +132,7 @@
     total = sum(math.prod(shape) for shape in shapes)
     groups = math.prod(lax.axis_size(name) for name in DP)
     lanes = 128
-    length = -(-total // (lanes * groups * 8)) * groups * 8
+    length = -(-total // (lanes * groups)) * groups
     flat = jnp.concatenate([part.reshape(-1) for part in parts] + [tail])
     flat = jnp.pad(flat, (0, length * lanes - total)).reshape(length, lanes)
     for name in SCATTER:

time: 252 us -> 250 us (level)
  blocking collectives: 98 us -> 95.2 us
where the time goes in v10:
time: 250 us; the launch traced here: 248 us
  blocking collectives  95.2 us (38%)
  waiting for transfers between devices  43.3 us (17%)
  starting transfers between devices  36.4 us (15%)
  matrix products  34.4 us (14%)
  other arithmetic  19.3 us (8%)
  local copies, waits for them, and re-layouts  17.5 us (7%)
    all_to_all x2, blocking collectives, scatter_sum(): got = lax.all_to_all(blocks, name, 0, 0, tiled=False)  56.2 us
    ppermute x8, waiting for transfers between devices, hop(): return lax.ppermute(value, 'zh', [(source, target)])  42 us
    all_to_all x2, blocking collectives, gather_all(): lax.all_to_all(blocks, name, 0, 0, tiled=False).reshape(-1, flat.shape[1])  39 us
    ppermute x8, starting transfers between devices, hop(): return lax.ppermute(value, 'zh', [(source, target)])  18.7 us
    ppermute x8, starting transfers between devices, swap_core(): return lax.ppermute(value, 'core', [(0, 1), (1, 0)])  17.7 us
    dot_general x24, matrix products, rows_product(): lax.dot_general(left, right, (((0,), (0,)), ((), ())), preferred_element_...  13.7 us
    unnamed x87, local copies, waits for them, and re-layouts  8.45 us
    dot_general x6, matrix products, down_forward(): jnp.dot(gated, out_matrix, preferred_element_type=jnp.float32)  8.02 us
  transfers between devices with their start and end apart: 16, of which 4 were waited for; matrix products, arithmetic and copies ran while one was open for 14% of the time, Pallas kernels for 0%

profile of v10, /device:TPU:2, one launch (start us, length us, event | category | flops | bytes accessed | tf_op | source)
XLA Modules:
  0.0 248.2 jit_solution(14209578751217483638)
XLA Ops:
  0.6 2.1 collective-permute-start.1
  2.7 2.4 collective-permute-start
  6.7 1.2 constant_dynamic-slice_fusion
  9.1 0.8 broadcast_select_fusion.3
  9.9 1.2 broadcast_select_fusion.5
  12.7 10.9 %collective-permute-start.2 = (bf16[192,320]{1,0:T(8,128)(2,1)S(1)}, bf16[192,320]{1,0:T(8,128)(2,1)S(1)}, u32[]{:S(2)}, u32[]{:S(2)}) collective-permute-start(bf16[192,320]{1,0:T(8,128)(2,1)S(1)} %fusion.13), channel_id=1, source_target_pairs={{0,2},{1,3},{6,8},{7,9},{12,14},{13,15},{18,20},{19,21},{24,26},{2... | collective-permute-start | bytes 368648 | tf_op jit(solution)/shard_map/ppermute | solution.py:182
  24.5 1.9 collective-permute-start.5
  26.4 2.4 collective-permute-start.4
  29.0 1.2 multiply_reduce_fusion.21
  30.2 1.7 fusion.15
  32.6 0.8 broadcast_select_fusion.6
  33.6 2.2 multiply_reduce_fusion.5
  36.8 1.7 fusion.23
  38.5 1.3 broadcast_select_fusion.1
  44.0 1.3 collective-permute-start.7
  45.7 25.3 %collective-permute-done.7 = bf16[192,320]{1,0:T(8,128)(2,1)S(1)} collective-permute-done((bf16[192,320]{1,0:T(8,128)(2,1)S(1)}, bf16[192,320]{1,0:T(8,128)(2,1)S(1)}, u32[]{:S(2)}, u32[]{:S(2)}) %collective-permute-start.7) | collective-permute-done | bytes 122912 | tf_op jit(solution)/shard_map/ppermute | solution.py:182
  75.5 1.6 collective-permute-start.8
  78.2 1.4 collective-permute-done.8
  87.3 2.1 collective-permute-start.12
  89.3 1.1 add_convert_fusion.10
  91.7 1.2 select_convert_fusion.2
  92.9 2.4 collective-permute-start.11
  96.1 1.3 collective-permute-start.10
  98.2 1.9 reshape.228
  100.1 1.9 convert_add_fusion
  102.0 1.3 copy.22
  103.3 1.3 reshape.227
  104.6 1.9 pad_maximum_fusion
  106.6 0.9 add_convert_fusion.8
  112.2 1.5 collective-permute-start.13
  113.7 1.2 convolution_select_fusion.6
  115.0 1.3 convolution_select_fusion.2
  116.3 1.3 convolution_select_fusion
  117.9 15.3 %collective-permute-done.13 = bf16[192,320]{1,0:T(8,128)(2,1)S(1)} collective-permute-done((bf16[192,320]{1,0:T(8,128)(2,1)S(1)}, bf16[192,320]{1,0:T(8,128)(2,1)S(1)}, u32[]{:S(2)}, u32[]{:S(2)}) %collective-permute-start.13) | collective-permute-done | bytes 122912 | tf_op jit(solution)/shard_map/ppermute | solution.py:182
  134.5 1.6 convolution_select_fusion.7
  136.5 2.1 collective-permute-start.14
  139.0 1.2 select_convert_fusion
  140.1 2.4 collective-permute-start.15
  143.0 1.3 collective-permute-done.15
  144.2 1.1 add_convert_fusion
  146.5 23.0 %all_to_all.20 = bf16[4,1408,128]{2,1,0:T(8,128)(2,1)S(1)} all-to-all(bf16[4,1408,128]{2,1,0:T(8,128)(2,1)S(1)} %bitcast.122), channel_id=1, replica_groups=mesh['y'=8,'x'=4,'zl'=4,'zh'=3,'core'=2] {'x'}, dimensions={0} | all-to-all | bytes 2883584 | tf_op jit(solution)/shard_map/all_to_all | solution.py:159
  170.0 33.1 %all_to_all.21 = bf16[32,44,128]{2,1,0:T(8,128)(2,1)S(1)} all-to-all(bf16[32,44,128]{2,1,0:T(8,128)(2,1)S(1)} %reshape.231), channel_id=1, replica_groups=mesh['y'=8,'x'=4,'zl'=4,'zh'=3,'core'=2] {'y','zl'}, dimensions={0} | all-to-all | bytes 720896 | tf_op jit(solution)/shard_map/all_to_all | solution.py:159
  203.3 19.0 %all_to_all.22 = bf16[32,44,128]{2,1,0:T(8,128)(2,1)S(1)} all-to-all(bf16[32,44,128]{2,1,0:T(8,128)(2,1)S(1)} %broadcast_in_dim.23), channel_id=1, replica_groups=mesh['y'=8,'x'=4,'zl'=4,'zh'=3,'core'=2] {'y','zl'}, dimensions={0} | all-to-all | bytes 720896 | tf_op jit(solution)/shard_map/all_to_all | solution.py:166
  222.5 20.1 %all_to_all.23 = bf16[4,1408,128]{2,1,0:T(8,128)(2,1)S(1)} all-to-all(bf16[4,1408,128]{2,1,0:T(8,128)(2,1)S(1)} %broadcast_in_dim.25), channel_id=1, replica_groups=mesh['y'=8,'x'=4,'zl'=4,'zh'=3,'core'=2] {'x'}, dimensions={0} | all-to-all | bytes 2883584 | tf_op jit(solution)/shard_map/all_to_all | solution.py:166
  243.0 1.0 broadcast_in_dim_reshape.16
  244.3 1.2 copy.25
  245.5 1.1 broadcast_in_dim_reshape.13
  246.9 1.2 copy.24
  (226 shorter events, 37.6 us)
Async XLA Ops:
  0.6 8.4 %copy-start.24 = (bf16[1,640,320]{1,2,0:T(8,128)(2,1)S(1)}, bf16[1,640,320]{1,2,0:T(8,128)(2,1)}, u32[]{:S(2)}) copy-start(bf16[1,640,320]{1,2,0:T(8,128)(2,1)} %param.12) | copy-start | bytes 1228804
  0.6 8.4 %collective-permute-start.1 = (bf16[640,320]{0,1:T(8,128)(2,1)}, bf16[640,320]{0,1:T(8,128)(2,1)S(1)}, u32[]{:S(2)}, u32[]{:S(2)}) collective-permute-start(bf16[640,320]{0,1:T(8,128)(2,1)} %bitcast.123), channel_id=1, source_target_pairs={{0,1},{1,0},{2,3},{3,2},{4,5},{5,4},{6,7},{7,6},{8,9},{9,8},{10,11... | collective-permute-start | bytes 1228808 | tf_op jit(solution)/shard_map/ppermute | solution.py:178
  2.7 7.2 %collective-permute-start = (bf16[320,640]{1,0:T(8,128)(2,1)}, bf16[320,640]{1,0:T(8,128)(2,1)}, u32[]{:S(2)}, u32[]{:S(2)}) collective-permute-start(bf16[320,640]{1,0:T(8,128)(2,1)} %bitcast.124), channel_id=1, source_target_pairs={{0,1},{1,0},{2,3},{3,2},{4,5},{5,4},{6,7},{7,6},{8,9},{9,8},{10,11... | collective-permute-start | bytes 1228808 | tf_op jit(solution)/shard_map/ppermute | solution.py:178
  8.0 1.9 copy-start.25
  9.9 23.7 %copy-start.27 = (bf16[640,320]{0,1:T(8,128)(2,1)}, bf16[640,320]{0,1:T(8,128)(2,1)S(1)}, u32[]{:S(2)}) copy-start(bf16[640,320]{0,1:T(8,128)(2,1)S(1)} %get-tuple-element.42) | copy-start | bytes 1228804
  11.1 1.0 copy-start.30
  12.1 12.3 %copy-start.33 = (bf16[1,320,320]{2,1,0:T(8,128)(2,1)S(1)}, bf16[1,320,320]{2,1,0:T(8,128)(2,1)}, u32[]{:S(2)}) copy-start(bf16[1,320,320]{2,1,0:T(8,128)(2,1)} %param.14) | copy-start | bytes 614404
  12.1 14.2 %copy-start.26 = (bf16[1,640,320]{1,2,0:T(8,128)(2,1)S(1)}, bf16[1,640,320]{1,2,0:T(8,128)(2,1)}, u32[]{:S(2)}) copy-start(bf16[1,640,320]{1,2,0:T(8,128)(2,1)} %param.13) | copy-start | bytes 1228804
  12.7 17.5 %copy-start.36 = (bf16[192,320]{1,0:T(8,128)(2,1)}, bf16[192,320]{1,0:T(8,128)(2,1)S(1)}, u32[]{:S(2)}) copy-start(bf16[192,320]{1,0:T(8,128)(2,1)S(1)} %fusion.13) | copy-start | bytes 368644
  12.7 16.1 %collective-permute-start.2 = (bf16[192,320]{1,0:T(8,128)(2,1)S(1)}, bf16[192,320]{1,0:T(8,128)(2,1)S(1)}, u32[]{:S(2)}, u32[]{:S(2)}) collective-permute-start(bf16[192,320]{1,0:T(8,128)(2,1)S(1)} %fusion.13), channel_id=1, source_target_pairs={{0,2},{1,3},{6,8},{7,9},{12,14},{13,15},{18,20},{19,21},{24,26},{2... | collective-permute-start | bytes 368648 | tf_op jit(solution)/shard_map/ppermute | solution.py:182
  24.5 8.1 %collective-permute-start.5 = (bf16[320,320]{1,0:T(8,128)(2,1)S(1)}, bf16[320,320]{1,0:T(8,128)(2,1)S(1)}, u32[]{:S(2)}, u32[]{:S(2)}) collective-permute-start(bf16[320,320]{1,0:T(8,128)(2,1)S(1)} %bitcast.126), channel_id=1, source_target_pairs={{0,1},{1,0},{2,3},{3,2},{4,5},{5,4},{6,7},{7,6},{8,9},{9,8},{10,11... | collective-permute-start | bytes 614408 | tf_op jit(solution)/shard_map/ppermute | solution.py:178
  26.4 12.1 %collective-permute-start.4 = (bf16[640,320]{0,1:T(8,128)(2,1)S(1)}, bf16[640,320]{0,1:T(8,128)(2,1)}, u32[]{:S(2)}, u32[]{:S(2)}) collective-permute-start(bf16[640,320]{0,1:T(8,128)(2,1)S(1)} %bitcast.125), channel_id=1, source_target_pairs={{0,1},{1,0},{2,3},{3,2},{4,5},{5,4},{6,7},{7,6},{8,9},{9,8},{10,11... | collective-permute-start | bytes 1228808 | tf_op jit(solution)/shard_map/ppermute | solution.py:178
  31.9 4.0 %copy-start.38 = (bf16[192,320]{1,0:T(8,128)(2,1)}, bf16[192,320]{1,0:T(8,128)(2,1)S(1)}, u32[]{:S(2)}) copy-start(bf16[192,320]{1,0:T(8,128)(2,1)S(1)} %fusion.15) | copy-start | bytes 368644
  31.9 1.5 collective-permute-start.3
  36.3 49.3 %copy-start.4 = (f32[192,640]{1,0:T(8,128)}, f32[192,640]{1,0:T(8,128)S(1)}, u32[]{:S(2)}) copy-start(f32[192,640]{1,0:T(8,128)S(1)} %fusion.86) | copy-start | bytes 1474564
  38.4 44.1 %copy-start.14 = (bf16[192,320]{1,0:T(8,128)(2,1)}, bf16[192,320]{1,0:T(8,128)(2,1)S(1)}, u32[]{:S(2)}) copy-start(bf16[192,320]{1,0:T(8,128)(2,1)S(1)} %fusion.23) | copy-start | bytes 368644
  38.5 1.8 copy-start.34
  41.6 0.8 collective-permute-start.6
  42.3 3.0 %copy-start.2 = (bf16[192,320]{1,0:T(8,128)(2,1)}, bf16[192,320]{1,0:T(8,128)(2,1)S(1)}, u32[]{:S(2)}) copy-start(bf16[192,320]{1,0:T(8,128)(2,1)S(1)} %multiply_convert_fusion.26) | copy-start | bytes 368644
  44.0 27.0 %collective-permute-start.7 = (bf16[192,320]{1,0:T(8,128)(2,1)S(1)}, bf16[192,320]{1,0:T(8,128)(2,1)S(1)}, u32[]{:S(2)}, u32[]{:S(2)}) collective-permute-start(bf16[192,320]{1,0:T(8,128)(2,1)S(1)} %fusion.21), channel_id=1, source_target_pairs={{2,0},{3,1},{8,6},{9,7},{14,12},{15,13},{20,18},{21,19},{26,24},{2... | collective-permute-start | bytes 368648 | tf_op jit(solution)/shard_map/ppermute | solution.py:182
  45.6 44.8 %copy-start.21 = (f32[192,640]{1,0:T(8,128)}, f32[192,640]{1,0:T(8,128)S(1)}, u32[]{:S(2)}) copy-start(f32[192,640]{1,0:T(8,128)S(1)} %fusion.87) | copy-start | bytes 1474564
  75.5 4.1 %collective-permute-start.8 = (bf16[192,320]{1,0:T(8,128)(2,1)S(1)}, bf16[192,320]{1,0:T(8,128)(2,1)S(1)}, u32[]{:S(2)}, u32[]{:S(2)}) collective-permute-start(bf16[192,320]{1,0:T(8,128)(2,1)S(1)} %slice.121), channel_id=1, source_target_pairs={{0,2},{1,3},{6,8},{7,9},{12,14},{13,15},{18,20},{19,21},{24,26},{2... | collective-permute-start | bytes 368648 | tf_op jit(solution)/shard_map/ppermute | solution.py:182
  81.3 2.0 collective-permute-start.9
  85.5 3.8 %copy-start.16 = (bf16[192,320]{1,0:T(8,128)(2,1)}, bf16[192,320]{1,0:T(8,128)(2,1)S(1)}, u32[]{:S(2)}) copy-start(bf16[192,320]{1,0:T(8,128)(2,1)S(1)} %get-tuple-element.30) | copy-start | bytes 368644
  86.2 1.0 copy-start.10
  87.3 3.2 %copy-start.28 = (bf16[640,320]{0,1:T(8,128)(2,1)S(1)}, bf16[640,320]{0,1:T(8,128)(2,1)}, u32[]{:S(2)}) copy-start(bf16[640,320]{0,1:T(8,128)(2,1)} %copy-done.27) | copy-start | bytes 1228804
  87.3 10.2 %collective-permute-start.12 = (bf16[320,320]{1,0:T(8,128)(2,1)S(1)}, bf16[320,320]{1,0:T(8,128)(2,1)S(1)}, u32[]{:S(2)}, u32[]{:S(2)}) collective-permute-start(bf16[320,320]{1,0:T(8,128)(2,1)S(1)} %get-tuple-element.86), channel_id=1, source_target_pairs={{0,1},{1,0},{2,3},{3,2},{4,5},{5,4},{6,7},{7,6},{8,9},{9,8},{10,11... | collective-permute-start | bytes 614408 | tf_op jit(solution)/shard_map/ppermute | solution.py:178
  90.4 4.9 %copy-start.18 = (bf16[192,320]{1,0:T(8,128)(2,1)}, bf16[192,320]{1,0:T(8,128)(2,1)S(1)}, u32[]{:S(2)}) copy-start(bf16[192,320]{1,0:T(8,128)(2,1)S(1)} %get-tuple-element.26) | copy-start | bytes 368644
  92.9 7.2 %collective-permute-start.11 = (bf16[640,320]{0,1:T(8,128)(2,1)}, bf16[640,320]{0,1:T(8,128)(2,1)}, u32[]{:S(2)}, u32[]{:S(2)}) collective-permute-start(bf16[640,320]{0,1:T(8,128)(2,1)} %get-tuple-element.88), channel_id=1, source_target_pairs={{0,1},{1,0},{2,3},{3,2},{4,5},{5,4},{6,7},{7,6},{8,9},{9,8},{10,11... | collective-permute-start | bytes 1228808 | tf_op jit(solution)/shard_map/ppermute | solution.py:178
  96.1 10.5 %collective-permute-start.10 = (bf16[192,320]{1,0:T(8,128)(2,1)}, bf16[192,320]{1,0:T(8,128)(2,1)}, u32[]{:S(2)}, u32[]{:S(2)}) collective-permute-start(bf16[192,320]{1,0:T(8,128)(2,1)} %add_convert_fusion.9), channel_id=1, source_target_pairs={{4,2},{5,3},{10,8},{11,9},{16,14},{17,15},{22,20},{23,21},{28,26},... | collective-permute-start | bytes 368648 | tf_op jit(solution)/shard_map/ppermute | solution.py:182
  102.0 2.7 %copy-start.12 = (bf16[102400]{0:T(1024)(128)(2,1)S(1)}, bf16[102400]{0:T(1024)(128)(2,1)}, u32[]{:S(2)}) copy-start(bf16[102400]{0:T(1024)(128)(2,1)} %reshape.228) | copy-start | bytes 614404
  103.3 4.2 %copy-start.5 = (f32[192,640]{1,0:T(8,128)S(1)}, f32[192,640]{1,0:T(8,128)}, u32[]{:S(2)}) copy-start(f32[192,640]{1,0:T(8,128)} %copy-done.4) | copy-start | bytes 1474564
  104.6 2.9 %copy-start.32 = (bf16[640,320]{0,1:T(8,128)(2,1)S(1)}, bf16[640,320]{0,1:T(8,128)(2,1)}, u32[]{:S(2)}) copy-start(bf16[640,320]{0,1:T(8,128)(2,1)} %get-tuple-element.43) | copy-start | bytes 1228804
  107.8 1.1 copy-start.22
  107.8 1.2 copy-start.29
  110.6 1.0 copy-start.6
  111.6 2.1 copy-start.9
  112.0 2.9 %copy-start.19 = (bf16[192,320]{1,0:T(8,128)(2,1)S(1)}, bf16[192,320]{1,0:T(8,128)(2,1)}, u32[]{:S(2)}) copy-start(bf16[192,320]{1,0:T(8,128)(2,1)} %copy-done.18) | copy-start | bytes 368644
  112.2 21.0 %collective-permute-start.13 = (bf16[192,320]{1,0:T(8,128)(2,1)S(1)}, bf16[192,320]{1,0:T(8,128)(2,1)S(1)}, u32[]{:S(2)}, u32[]{:S(2)}) collective-permute-start(bf16[192,320]{1,0:T(8,128)(2,1)S(1)} %add_convert_fusion.5), channel_id=1, source_target_pairs={{2,0},{3,1},{8,6},{9,7},{14,12},{15,13},{20,18},{21,19},{26,24},{2... | collective-permute-start | bytes 368648 | tf_op jit(solution)/shard_map/ppermute | solution.py:182
  115.0 1.3 copy-start.17
  116.3 1.3 copy-start.11
  133.5 1.0 copy-start.23
  136.1 2.4 copy-start.39
  136.4 2.5 %copy-start.7 = (f32[192,640]{1,0:T(8,128)S(1)}, f32[192,640]{1,0:T(8,128)}, u32[]{:S(2)}) copy-start(f32[192,640]{1,0:T(8,128)} %copy-done.4) | copy-start | bytes 1474564
  136.5 2.5 %copy-start.13 = (f32[640,320]{0,1:T(8,128)S(1)}, f32[640,320]{0,1:T(8,128)}, u32[]{:S(2)}) copy-start(f32[640,320]{0,1:T(8,128)} %convolution_select_fusion) | copy-start | bytes 2457604
  136.5 6.1 %collective-permute-start.14 = (bf16[320,640]{1,0:T(8,128)(2,1)S(1)}, bf16[320,640]{1,0:T(8,128)(2,1)S(1)}, u32[]{:S(2)}, u32[]{:S(2)}) collective-permute-start(bf16[320,640]{1,0:T(8,128)(2,1)S(1)} %get-tuple-element.98), channel_id=1, source_target_pairs={{0,1},{1,0},{2,3},{3,2},{4,5},{5,4},{6,7},{7,6},{8,9},{9,8},{10,11... | collective-permute-start | bytes 1228808 | tf_op jit(solution)/shard_map/ppermute | solution.py:178
  140.1 4.1 %collective-permute-start.15 = (bf16[640,320]{0,1:T(8,128)(2,1)}, bf16[640,320]{0,1:T(8,128)(2,1)}, u32[]{:S(2)}, u32[]{:S(2)}) collective-permute-start(bf16[640,320]{0,1:T(8,128)(2,1)} %get-tuple-element.96), channel_id=1, source_target_pairs={{0,1},{1,0},{2,3},{3,2},{4,5},{5,4},{6,7},{7,6},{8,9},{9,8},{10,11... | collective-permute-start | bytes 1228808 | tf_op jit(solution)/shard_map/ppermute | solution.py:178
  145.3 1.1 copy-start.1
  (9 other events, 8.4 us)
